TPU v7x, 256 devices: a whole 4x4x8 slice. The times are simulated.
256 devices in a mesh: dp: 16 (over z, core), row: 4 (over x), col: 4 (over y).
Axes of the slice: x: 4, y: 4, z: 8, core: 2. Of those that a mesh axis runs over, the one named last changes fastest.
Arguments:
- latent: bfloat16 [16, 32, 64, 768], P('dp', 'row', 'col'), may hold values from -6 to 6
- norm_shift: float32 [16, 768], P('dp'), may hold values from -3 to 3
- norm_scale: float32 [16, 768], P('dp'), may hold values from -3 to 3
- branch_gate: float32 [16, 768], P('dp'), may hold values from -4 to 4
- query_key_value: bfloat16 [768, 2304], replicated, may hold values from -0.21875 to 0.21875
- output_weight: bfloat16 [768, 768], replicated, may hold values from -0.21875 to 0.21875
- tile_valid: int32 [16, 4, 8], P('dp'), may hold values from 0 to 1, as said below
- cotangent: bfloat16 [16, 32, 64, 768], P('dp', 'row', 'col'), may hold values from -6 to 6
Outputs:
- block_output: bfloat16 [16, 32, 64, 768], P('dp', 'row', 'col')
- latent_gradient: bfloat16 [16, 32, 64, 768], P('dp', 'row', 'col')
- projection_gradient: float32 [768, 2304], P('dp', ('row', 'col'))
- output_weight_gradient: float32 [768, 768], P('dp', ('row', 'col'))
- shift_gradient: float32 [16, 768], P('dp')
- scale_gradient: float32 [16, 768], P('dp')
- gate_gradient: float32 [16, 768], P('dp')
Inputs may be any that keep to these rules, and one draw needn't show every extreme that they name: `tile_valid`: the valid tiles of each sample form a rectangle that starts at tile (0, 0), at least 2 tiles tall and 3 tiles wide; sample 0 is exactly 2 tiles tall.
All inputs are finite; a program needn't handle non-finite values.
Results may differ from a plain program's by a relative error of at most 0.02.
Values may be sent and summed in bfloat16 or wider, within the bound.
No kernel may reach another device: no remote copies, remote signals or barrier semaphores. Data moves between devices by JAX's collectives and lax.ppermute only.
A program may use at most 128 MiB of HBM per device.

v0:
```python
import math

import jax
import jax.numpy as jnp
from jax import lax
from jax.sharding import PartitionSpec as P

HEAD_DIM = 64
TILE = 8


EPSILON = 1e-06


def shifted_2(value, axis, steps):
    count = lax.axis_size(axis)
    first, last = (max(0, -steps), min(count, count - steps))
    return lax.ppermute(value, axis, [(source, source + steps) for source in range(first, last)])


def extended(shard, sides, width):
    for axis, dim in sides:
        devices, length = (lax.axis_size(axis), shard.shape[dim])
        up = [(i, (i + 1) % devices) for i in range(devices - 1)]
        down = [(j, i) for i, j in up]
        last = lax.slice_in_dim(shard, length - width, length, axis=dim)
        first = lax.slice_in_dim(shard, 0, width, axis=dim)
        before = lax.ppermute(last, axis, up)
        after = lax.ppermute(first, axis, down)
        shard = jnp.concatenate([before, shard, after], axis=dim)
    return shard


def product(form, left, right):
    return jnp.einsum(form, left, right, preferred_element_type=jnp.float32)


def to_tiles(latent_image):
    samples, height, across, features = latent_image.shape
    blocks = latent_image.reshape(samples, height // TILE, TILE, across // TILE, TILE, features)
    blocks = blocks.transpose(0, 1, 3, 2, 4, 5)
    return blocks.reshape(samples, height // TILE, across // TILE, TILE * TILE, features)


def from_tiles(tiled):
    samples, tile_rows, tile_cols, tile_cells, features = tiled.shape
    blocks = tiled.reshape(samples, tile_rows, tile_cols, TILE, TILE, features)
    blocks = blocks.transpose(0, 1, 3, 2, 4, 5)
    return blocks.reshape(samples, tile_rows * TILE, tile_cols * TILE, features)


def neighbours(padded):
    tile_rows = padded.shape[1] - 2
    tile_cols = padded.shape[2] - 2
    shifted = [
        padded[:, offset_row : offset_row + tile_rows, offset_col : offset_col + tile_cols]
        for offset_row in range(3)
        for offset_col in range(3)
    ]
    return jnp.concatenate(shifted, axis=3)


def spread_back(gathered):
    samples, tile_rows, tile_cols, key_count, features = gathered.shape
    tile_cells = key_count // 9
    accumulated = jnp.zeros(
        (samples, tile_rows + 2, tile_cols + 2, tile_cells, features), jnp.float32
    )
    for position in range(9):
        offset_row = position // 3
        offset_col = position % 3
        section = gathered[:, :, :, position * tile_cells : (position + 1) * tile_cells]
        accumulated = accumulated + jnp.pad(
            section,
            ((0, 0), (offset_row, 2 - offset_row), (offset_col, 2 - offset_col), (0, 0), (0, 0)),
        )
    return accumulated


def front(latent, norm_shift, norm_scale, weight):
    values = latent.astype(jnp.float32)
    center = values - jnp.mean(values, axis=-1, keepdims=True)
    inverse = lax.rsqrt(jnp.mean(center * center, axis=-1, keepdims=True) + EPSILON)
    normed = center * inverse
    modulated = (
        normed * (1.0 + norm_scale[:, None, None, :]) + norm_shift[:, None, None, :]
    ).astype(jnp.bfloat16)
    samples, height, across, model_width = latent.shape
    mixing = jnp.dot(modulated.reshape(-1, model_width), weight, preferred_element_type=jnp.float32)
    projections = mixing.astype(jnp.bfloat16).reshape(samples, height, across, 3 * model_width)
    return (normed, inverse, modulated, projections)


def attend(queries, keys_nine, values_nine, key_valid, query_valid):
    scores = product("srcqhe,srckhe->srchqk", queries, keys_nine) * (1.0 / math.sqrt(HEAD_DIM))
    unnormed = jnp.exp(scores) * key_valid[:, :, :, None, None, :]
    denominator = (
        jnp.sum(unnormed, axis=-1, keepdims=True) + (1.0 - query_valid)[:, :, :, None, None, None]
    )
    attention = (unnormed / denominator).astype(jnp.bfloat16)
    attended = (
        product("srchqk,srckhe->srcqhe", attention, values_nine)
        * query_valid[:, :, :, None, None, None]
    )
    return (attention, attended.astype(jnp.bfloat16))


def attend_back(queries, keys_nine, values_nine, attention, grad_attended):
    grad_weights = product("srcqhe,srckhe->srchqk", grad_attended, values_nine)
    attention_wide = attention.astype(jnp.float32)
    row_inner = jnp.sum(attention_wide * grad_weights, axis=-1, keepdims=True)
    grad_scores = (
        attention_wide * (grad_weights - row_inner) * (1.0 / math.sqrt(HEAD_DIM))
    ).astype(jnp.bfloat16)
    grad_queries = product("srchqk,srckhe->srcqhe", grad_scores, keys_nine).astype(jnp.bfloat16)
    grad_keys = product("srchqk,srcqhe->srckhe", grad_scores, queries)
    grad_values = product("srchqk,srcqhe->srckhe", attention, grad_attended)
    return (grad_queries, grad_keys, grad_values)


def branch_core(projections, kv_padded, mask_pad, branch_gate, cotangent, output_weight):
    samples, height, across, triple = projections.shape
    model_width = triple // 3
    head_count = model_width // HEAD_DIM
    tile_rows = height // TILE
    tile_cols = across // TILE
    tile_cells = TILE * TILE
    queries = to_tiles(projections[..., :model_width]).reshape(
        samples, tile_rows, tile_cols, tile_cells, head_count, HEAD_DIM
    )
    gathered = neighbours(to_tiles(kv_padded))
    keys_nine = gathered[..., :model_width].reshape(
        samples, tile_rows, tile_cols, 9 * tile_cells, head_count, HEAD_DIM
    )
    values_nine = gathered[..., model_width:].reshape(
        samples, tile_rows, tile_cols, 9 * tile_cells, head_count, HEAD_DIM
    )
    cell_mask = jnp.broadcast_to(mask_pad[:, :, :, None, None], mask_pad.shape + (tile_cells, 1))
    key_valid = neighbours(cell_mask)[..., 0]
    query_valid = mask_pad[:, 1:-1, 1:-1]
    attention, attended = attend(queries, keys_nine, values_nine, key_valid, query_valid)
    attended_image = from_tiles(
        attended.reshape(samples, tile_rows, tile_cols, tile_cells, model_width)
    )
    flat_attended = attended_image.reshape(-1, model_width)
    projected = jnp.dot(flat_attended, output_weight, preferred_element_type=jnp.float32).reshape(
        samples, height, across, model_width
    )
    incoming = cotangent.astype(jnp.float32)
    gate_term = jnp.sum(incoming * projected, axis=(1, 2))
    grad_projected = (incoming * branch_gate[:, None, None, :]).astype(jnp.bfloat16)
    flat_grad = grad_projected.reshape(-1, model_width)
    output_term = product("nd,nf->df", flat_attended, flat_grad)
    grad_image = product("nf,df->nd", flat_grad, output_weight).reshape(
        samples, height, across, model_width
    )
    grad_attended = (to_tiles(grad_image) * query_valid[:, :, :, None, None]).astype(jnp.bfloat16)
    grad_attended = grad_attended.reshape(
        samples, tile_rows, tile_cols, tile_cells, head_count, HEAD_DIM
    )
    grad_queries, grad_keys, grad_values = attend_back(
        queries, keys_nine, values_nine, attention, grad_attended
    )
    query_image = from_tiles(
        grad_queries.reshape(samples, tile_rows, tile_cols, tile_cells, model_width)
    )
    key_spread = spread_back(
        grad_keys.reshape(samples, tile_rows, tile_cols, 9 * tile_cells, model_width)
    )
    value_spread = spread_back(
        grad_values.reshape(samples, tile_rows, tile_cols, 9 * tile_cells, model_width)
    )
    pair_grads = from_tiles(jnp.concatenate([key_spread, value_spread], axis=-1))
    return (projected, gate_term, output_term, query_image, pair_grads)


def branch_back(query_image, pair_grads, modulated, normed, inverse, norm_scale, weight):
    samples, height, across, model_width = normed.shape
    grad_all = jnp.concatenate([query_image, pair_grads.astype(jnp.bfloat16)], axis=-1)
    flat_grad = grad_all.reshape(-1, 3 * model_width)
    input_term = product("nd,nf->df", modulated.reshape(-1, model_width), flat_grad)
    grad_modulated = product("nf,df->nd", flat_grad, weight).reshape(
        samples, height, across, model_width
    )
    shift_term = jnp.sum(grad_modulated, axis=(1, 2))
    scale_term = jnp.sum(grad_modulated * normed, axis=(1, 2))
    grad_normed = grad_modulated * (1.0 + norm_scale[:, None, None, :])
    latent_term = inverse * (
        grad_normed
        - jnp.mean(grad_normed, axis=-1, keepdims=True)
        - normed * jnp.mean(grad_normed * normed, axis=-1, keepdims=True)
    )
    return (input_term, shift_term, scale_term, latent_term)


def guarded(active, function, *operands):
    return function(*operands)


def return_rims(pair_grads):
    samples, padded_rows, padded_cols, features = pair_grads.shape
    across = padded_cols - 2 * TILE
    left_strip = pair_grads[:, :, :TILE]
    right_strip = pair_grads[:, :, -TILE:]
    from_right = shifted_2(left_strip.astype(jnp.bfloat16), "col", -1).astype(left_strip.dtype)
    from_left = shifted_2(right_strip.astype(jnp.bfloat16), "col", 1).astype(right_strip.dtype)
    middle = pair_grads[:, :, TILE:-TILE]
    middle = middle + jnp.pad(from_left, ((0, 0), (0, 0), (0, across - TILE), (0, 0)))
    middle = middle + jnp.pad(from_right, ((0, 0), (0, 0), (across - TILE, 0), (0, 0)))
    top_strip = middle[:, :TILE]
    bottom_strip = middle[:, -TILE:]
    from_below = shifted_2(top_strip.astype(jnp.bfloat16), "row", -1).astype(top_strip.dtype)
    from_above = shifted_2(bottom_strip.astype(jnp.bfloat16), "row", 1).astype(bottom_strip.dtype)
    interior = middle[:, TILE:-TILE]
    interior = interior + from_above
    interior = interior + from_below
    return interior


def local(
    latent,
    norm_shift,
    norm_scale,
    branch_gate,
    query_key_value,
    output_weight,
    tile_valid,
    cotangent,
):
    samples, height, across, model_width = latent.shape
    tile_rows = height // TILE
    tile_cols = across // TILE
    mask_whole = jnp.pad(tile_valid.astype(jnp.float32), ((0, 0), (1, 1), (1, 1)))
    row_start = lax.axis_index("row") * tile_rows
    col_start = lax.axis_index("col") * tile_cols
    mask_pad = lax.dynamic_slice(
        mask_whole, (jnp.int32(0), row_start, col_start), (samples, tile_rows + 2, tile_cols + 2)
    )
    active = jnp.sum(mask_pad[:, 1:-1, 1:-1]) > 0.0
    normed, inverse, modulated, projections = guarded(
        active, front, latent, norm_shift, norm_scale, query_key_value
    )
    key_value = projections[..., model_width:]
    kv_padded = extended(key_value, (("row", 1), ("col", 2)), TILE)
    projected, gate_term, output_term, query_image, pair_grads = guarded(
        active, branch_core, projections, kv_padded, mask_pad, branch_gate, cotangent, output_weight
    )
    pair_grads = return_rims(pair_grads)
    input_term, shift_term, scale_term, latent_term = guarded(
        active,
        branch_back,
        query_image,
        pair_grads,
        modulated,
        normed,
        inverse,
        norm_scale,
        query_key_value,
    )
    shift_total, scale_total, gate_total = lax.psum(
        (shift_term, scale_term, gate_term), ("row", "col")
    )
    mixed = (latent.astype(jnp.float32) + branch_gate[:, None, None, :] * projected).astype(
        jnp.bfloat16
    )
    latent_grad = (cotangent.astype(jnp.float32) + latent_term).astype(jnp.bfloat16)
    input_part, output_part = (
        lax.psum_scatter(
            input_term.astype(jnp.bfloat16), "dp", scatter_dimension=0, tiled=True
        ).astype(jnp.float32),
        lax.psum_scatter(
            output_term.astype(jnp.bfloat16), "dp", scatter_dimension=0, tiled=True
        ).astype(jnp.float32),
    )
    input_grad, output_grad = (
        lax.psum_scatter(
            input_part.astype(jnp.bfloat16), ("row", "col"), scatter_dimension=1, tiled=True
        ).astype(jnp.float32),
        lax.psum_scatter(
            output_part.astype(jnp.bfloat16), ("row", "col"), scatter_dimension=1, tiled=True
        ).astype(jnp.float32),
    )
    return (mixed, latent_grad, input_grad, output_grad, shift_total, scale_total, gate_total)


def solution(mesh):
    placed = (
        P("dp", "row", "col", None),
        P("dp", None),
        P("dp", None),
        P("dp", None),
        P(),
        P(),
        P("dp", None, None),
        P("dp", "row", "col", None),
    )
    return jax.shard_map(
        local,
        mesh=mesh,
        in_specs=placed,
        out_specs=(
            P("dp", "row", "col", None),
            P("dp", "row", "col", None),
            P("dp", ("row", "col")),
            P("dp", ("row", "col")),
            P("dp", None),
            P("dp", None),
            P("dp", None),
        ),
        check_vma=False,
    )
```

profile of v0, /device:TPU:4, one launch (start us, length us, event | category | flops | bytes accessed | tf_op | source)
XLA Modules:
  0.0 392.6 jit_solution(3625084825912492426)
XLA Ops:
  14.5 2.4 collective-permute-start.1
  17.0 4.2 %collective-permute-start = (bf16[1,8,16,1536]{3,2,1,0:T(8,128)(2,1)}, bf16[1,8,16,1536]{3,2,1,0:T(8,128)(2,1)}, u32[]{:S(2)}, u32[]{:S(2)}) collective-permute-start(bf16[1,8,16,1536]{3,2,1,0:T(8,128)(2,1)} %slice.236), channel_id=1, source_target_pairs={{0,4},{4,8},{8,12},{1,5},{5,9},{9,13},{2,6},{6,10},{10,14},{3,7},{... | collective-permute-start | bytes 1179656 | tf_op jit(solution)/shard_map/ppermute | solution.py:28
  27.6 2.2 collective-permute-done
  32.3 4.3 %collective-permute-start.2 = (bf16[1,24,8,1536]{3,2,1,0:T(8,128)(2,1)}, bf16[1,24,8,1536]{3,2,1,0:T(8,128)(2,1)}, u32[]{:S(2)}, u32[]{:S(2)}) collective-permute-start(bf16[1,24,8,1536]{3,2,1,0:T(8,128)(2,1)} %get-tuple-element.42), channel_id=1, source_target_pairs={{0,1},{1,2},{2,3},{4,5},{5,6},{6,7},{8,9},{9,10},{10,11},{12,13},{... | collective-permute-start | bytes 1769480 | tf_op jit(solution)/shard_map/ppermute | solution.py:28
  43.6 2.2 reshape.275
  58.4 3.9 copy.120
  62.3 3.9 copy.118
  66.2 2.7 fusion.3
  71.0 2.6 fusion.52
  73.7 2.7 fusion.50
  76.4 7.5 %fusion.6 = f32[2,12,64,576]{3,2,1,0:T(8,128)} fusion(bf16[2,64,12,64]{1,3,2,0:T(8,128)(2,1)} %copy.128, bf16[2,12,64,576]{3,2,1,0:T(8,128)(2,1)} %copy-done.2, f32[2,12,64,576]{3,2,1,0:T(8,128)} %fusion.52), kind=kOutput, calls=%fused_computation.18 | convolution fusion | flops 119441472 | bytes 9043968 | tf_op jit(solution)/shard_map/srchqk,srcqhe->srckhe/dot_general | solution.py:35
  83.9 7.0 %fusion.58 = (f32[1,1,2,64,768]{3,4,2,1,0:T(8,128)}, f32[1,1,2,64,768]{3,4,2,1,0:T(8,128)}, f32[1,1,2,64,768]{3,4,2,1,0:T(8,128)}, f32[1,1,2,64,768]{3,4,2,1,0:T...) fusion(f32[1,1,2,576,768]{3,4,2,1,0:T(8,128)} %bitcast.129), kind=kLoop, calls=%fused_computation.112 | loop fusion | bytes 7077888 | tf_op jit(solution)/shard_map/slice | solution.py:72
  90.9 2.2 copy.165
  93.1 2.1 copy.172
  95.2 2.1 copy.171
  97.4 2.1 copy.170
  99.5 2.1 copy.169
  101.6 2.1 copy.168
  103.8 2.1 copy.167
  105.9 2.1 copy.166
  108.0 2.1 copy.173
  110.2 7.1 %fusion.57 = (f32[1,1,2,64,768]{3,4,2,1,0:T(8,128)}, f32[1,1,2,64,768]{3,4,2,1,0:T(8,128)}, f32[1,1,2,64,768]{3,4,2,1,0:T(8,128)}, f32[1,1,2,64,768]{3,4,2,1,0:T...) fusion(f32[1,1,2,576,768]{3,4,2,1,0:T(8,128)} %bitcast.128), kind=kLoop, calls=%fused_computation.111 | loop fusion | bytes 7077888 | tf_op jit(solution)/shard_map/slice | solution.py:72
  117.2 2.1 copy.156
  119.4 2.1 copy.163
  121.5 2.1 copy.162
  123.7 2.1 copy.161
  125.8 2.1 copy.160
  127.9 2.2 copy.159
  130.1 2.1 copy.158
  132.2 2.1 copy.157
  134.4 2.1 copy.164
  136.5 3.7 pad_add_fusion
  144.6 5.4 %collective-permute-start.4 = (bf16[1,24,8,1536]{3,2,1,0:T(8,128)(2,1)}, bf16[1,24,8,1536]{3,2,1,0:T(8,128)(2,1)}, u32[]{:S(2)}, u32[]{:S(2)}) collective-permute-start(bf16[1,24,8,1536]{3,2,1,0:T(8,128)(2,1)} %get-tuple-element.38), channel_id=1, source_target_pairs={{0,1},{1,2},{2,3},{4,5},{5,6},{6,7},{8,9},{9,10},{10,11},{12,13},{... | collective-permute-start | bytes 1769480 | tf_op jit(solution)/shard_map/ppermute | solution.py:18
  152.8 2.2 copy.122
  158.7 2.4 convolution_convert_fusion.1
  161.2 4.0 %collective-permute-done.5 = bf16[1,24,8,1536]{3,2,1,0:T(8,128)(2,1)} collective-permute-done((bf16[1,24,8,1536]{3,2,1,0:T(8,128)(2,1)}, bf16[1,24,8,1536]{3,2,1,0:T(8,128)(2,1)}, u32[]{:S(2)}, u32[]{:S(2)}) %collective-permute-start.5) | collective-permute-done | bytes 589856 | tf_op jit(solution)/shard_map/ppermute | solution.py:18
  165.2 4.0 %fusion.55 = (bf16[1,24,16,1536]{3,2,1,0:T(8,128)(2,1)S(1)}, f32[1,24,16,1536]{3,2,1,0:T(8,128)}) fusion(bf16[1,24,8,1536]{3,2,1,0:T(8,128)(2,1)} %collective-permute-done.5, bf16[1,24,8,1536]{3,2,1,0:T(8,128)(2,1)} %collective-permute-done.4, f32[1,24,32,1536]{3,2,1,0:T(8,128)} %bitcast.131), kind=kLoop, calls=%fused_computation.110 | loop fusion | flops 2949120 | bytes 7077888 | tf_op jit(solution)/shard_map/convert.5
  170.2 4.1 %collective-permute-start.6 = (bf16[1,8,16,1536]{3,2,1,0:T(8,128)(2,1)}, bf16[1,8,16,1536]{3,2,1,0:T(8,128)(2,1)}, u32[]{:S(2)}, u32[]{:S(2)}) collective-permute-start(bf16[1,8,16,1536]{3,2,1,0:T(8,128)(2,1)} %get-tuple-element.40), channel_id=1, source_target_pairs={{0,4},{4,8},{8,12},{1,5},{5,9},{9,13},{2,6},{6,10},{10,14},{3,7},{... | collective-permute-start | bytes 1179656 | tf_op jit(solution)/shard_map/ppermute | solution.py:18
  176.3 7.1 %fusion.13 = bf16[1,1,2,64,12,64]{3,5,4,2,1,0:T(8,128)(2,1)} fusion(bf16[2,576,12,64]{1,3,2,0:T(8,128)(2,1)} %bitcast.145, bf16[2,12,64,576]{3,2,1,0:T(8,128)(2,1)} %copy-done.2, f32[2,12,64,576]{3,2,1,0:T(8,128)} %fusion.52), kind=kOutput, calls=%fused_computation.27 | convolution fusion | flops 119539776 | bytes 7274496 | tf_op jit(solution)/shard_map/srchqk,srckhe->srcqhe/dot_general | solution.py:35
  183.4 2.2 copy.126
  191.6 2.9 bitcast_convert_fusion
  197.0 2.5 fusion.63
  199.4 3.1 fusion.54
  204.7 19.7 %reduce-scatter.7.cloned.1.call-done = bf16[48,768]{1,0:T(8,128)(2,1)} async-done(((bf16[768,768]{1,0:T(8,128)(2,1)}), bf16[48,768]{1,0:T(8,128)(2,1)}) %reduce-scatter.7.cloned.1.call-update) | async-done | bytes 73744 | tf_op jit(solution)/shard_map/reduce_scatter | solution.py:271
  224.4 63.4 %reduce-scatter.5.cloned.1.call-done = bf16[48,2304]{1,0:T(8,128)(2,1)} async-done(((bf16[768,2304]{1,0:T(8,128)(2,1)}), bf16[48,2304]{1,0:T(8,128)(2,1)}) %reduce-scatter.5.cloned.1.call-update) | async-done | bytes 221200 | tf_op jit(solution)/shard_map/reduce_scatter | solution.py:268
  292.9 2.2 fusion.41
  295.1 35.1 %all-reduce.23 = (f32[1,768]{1,0:T(1,128)}, f32[1,768]{1,0:T(1,128)}, f32[1,768]{1,0:T(1,128)}) all-reduce(f32[1,768]{1,0:T(1,128)} %reduce_sum.94, f32[1,768]{1,0:T(1,128)} %reduce_sum.96, f32[1,768]{1,0:T(1,128)S(1)} %reduce_sum.98), channel_id=1, replica_groups=mesh['dp'=16,'row'=4,'col'=4] {'row','col'}, use_global_device_ids=true, to_apply=%region_11.12 | all-reduce | flops 2304 | bytes 18432 | tf_op jit(solution)/shard_map/psum | solution.py:260
  330.2 53.0 %all-reduce.27.cloned.1.call-done = (bf16[48,2304]{1,0:T(8,128)(2,1)}, bf16[48,768]{1,0:T(8,128)(2,1)}) async-done(((bf16[48,2304]{1,0:T(8,128)(2,1)}, bf16[48,768]{1,0:T(8,128)(2,1)}), (bf16[48,2304]{1,0:T(8,128)(2,1)}, bf16[48,768]{1,0:T(8,128)(2,1)})) %all-reduce.27.cloned.1.call-update) | async-done | bytes 294928
  (132 shorter events, 68.9 us)
Async XLA Ops:
  7.2 5.1 %copy-start = (bf16[768,2304]{1,0:T(8,128)(2,1)S(1)}, bf16[768,2304]{1,0:T(8,128)(2,1)}, u32[]{:S(2)}) copy-start(bf16[768,2304]{1,0:T(8,128)(2,1)} %param.12) | copy-start | bytes 10616836
  7.2 217.2 %reduce-scatter.7.cloned.1.call-start = ((), (), s32[]{:S(2)}) async-start(), calls=%async_computation.3 | async-start | bytes 1253376 | tf_op jit(solution)/shard_map/reduce_scatter | solution.py:271
  10.4 2.5 copy-start.15
  12.3 2.3 copy-start.13
  12.9 0.8 copy-start.9
  14.5 13.1 %collective-permute-start.1 = (bf16[1,8,16,1536]{3,2,1,0:T(8,128)(2,1)}, bf16[1,8,16,1536]{3,2,1,0:T(8,128)(2,1)}, u32[]{:S(2)}, u32[]{:S(2)}) collective-permute-start(bf16[1,8,16,1536]{3,2,1,0:T(8,128)(2,1)} %slice.236), channel_id=1, source_target_pairs={{4,0},{8,4},{12,8},{5,1},{9,5},{13,9},{6,2},{10,6},{14,10},{7,3},{... | collective-permute-start | bytes 1179656 | tf_op jit(solution)/shard_map/ppermute | solution.py:29
  17.0 12.8 %collective-permute-start = (bf16[1,8,16,1536]{3,2,1,0:T(8,128)(2,1)}, bf16[1,8,16,1536]{3,2,1,0:T(8,128)(2,1)}, u32[]{:S(2)}, u32[]{:S(2)}) collective-permute-start(bf16[1,8,16,1536]{3,2,1,0:T(8,128)(2,1)} %slice.236), channel_id=1, source_target_pairs={{0,4},{4,8},{8,12},{1,5},{5,9},{9,13},{2,6},{6,10},{10,14},{3,7},{... | collective-permute-start | bytes 1179656 | tf_op jit(solution)/shard_map/ppermute | solution.py:28
  21.8 16.0 %copy-start.19 = (f32[1,4,8]{2,1,0:T(4,128)}, f32[1,4,8]{2,1,0:T(4,128)S(1)}, u32[]{:S(2)}) copy-start(f32[1,4,8]{2,1,0:T(4,128)S(1)} %convert_element_type.128) | copy-start | bytes 388
  22.5 8.6 %copy-start.17 = (f32[768]{0:T(1024)}, f32[768]{0:T(1024)S(1)}, u32[]{:S(2)}) copy-start(f32[768]{0:T(1024)S(1)} %reduce.12) | copy-start | bytes 9220
  23.5 4.1 %copy-start.10 = (bf16[1,8,16,768]{3,2,1,0:T(8,128)(2,1)}, bf16[1,8,16,768]{3,2,1,0:T(8,128)(2,1)S(1)}, u32[]{:S(2)}) copy-start(bf16[1,8,16,768]{3,2,1,0:T(8,128)(2,1)S(1)} %fusion.39) | copy-start | bytes 589828
  32.3 21.5 %collective-permute-start.2 = (bf16[1,24,8,1536]{3,2,1,0:T(8,128)(2,1)}, bf16[1,24,8,1536]{3,2,1,0:T(8,128)(2,1)}, u32[]{:S(2)}, u32[]{:S(2)}) collective-permute-start(bf16[1,24,8,1536]{3,2,1,0:T(8,128)(2,1)} %get-tuple-element.42), channel_id=1, source_target_pairs={{0,1},{1,2},{2,3},{4,5},{5,6},{6,7},{8,9},{9,10},{10,11},{12,13},{... | collective-permute-start | bytes 1769480 | tf_op jit(solution)/shard_map/ppermute | solution.py:28
  36.6 17.2 %collective-permute-start.3 = (bf16[1,24,8,1536]{3,2,1,0:T(8,128)(2,1)}, bf16[1,24,8,1536]{3,2,1,0:T(8,128)(2,1)}, u32[]{:S(2)}, u32[]{:S(2)}) collective-permute-start(bf16[1,24,8,1536]{3,2,1,0:T(8,128)(2,1)} %get-tuple-element.43), channel_id=1, source_target_pairs={{1,0},{2,1},{3,2},{5,4},{6,5},{7,6},{9,8},{10,9},{11,10},{13,12},{... | collective-permute-start | bytes 1769480 | tf_op jit(solution)/shard_map/ppermute | solution.py:29
  66.2 2.7 copy-start.22
  69.0 1.5 copy-start.4
  69.0 2.1 copy-start.6
  69.0 2.1 copy-start.20
  69.8 3.9 copy-start.2
  141.1 2.3 copy-start.1
  141.1 10.1 %copy-start.5 = (bf16[1,1,2,576,768]{3,4,2,1,0:T(8,128)(2,1)S(1)}, bf16[1,1,2,576,768]{3,4,2,1,0:T(8,128)(2,1)}, u32[]{:S(2)}) copy-start(bf16[1,1,2,576,768]{3,4,2,1,0:T(8,128)(2,1)} %copy.118) | copy-start | bytes 5308420
  143.4 7.9 %copy-start.3 = (bf16[2,12,64,576]{3,2,1,0:T(8,128)(2,1)S(1)}, bf16[2,12,64,576]{3,2,1,0:T(8,128)(2,1)}, u32[]{:S(2)}) copy-start(bf16[2,12,64,576]{3,2,1,0:T(8,128)(2,1)} %copy-done.2) | copy-start | bytes 5308420
  143.4 7.9 %copy-start.21 = (f32[2]{0:T(128)S(1)}, f32[2]{0:T(128)}, u32[]{:S(2)}) copy-start(f32[2]{0:T(128)} %get-tuple-element.49) | copy-start | bytes 28
  144.6 16.6 %collective-permute-start.4 = (bf16[1,24,8,1536]{3,2,1,0:T(8,128)(2,1)}, bf16[1,24,8,1536]{3,2,1,0:T(8,128)(2,1)}, u32[]{:S(2)}, u32[]{:S(2)}) collective-permute-start(bf16[1,24,8,1536]{3,2,1,0:T(8,128)(2,1)} %get-tuple-element.38), channel_id=1, source_target_pairs={{0,1},{1,2},{2,3},{4,5},{5,6},{6,7},{8,9},{9,10},{10,11},{12,13},{... | collective-permute-start | bytes 1769480 | tf_op jit(solution)/shard_map/ppermute | solution.py:18
  149.9 15.3 %collective-permute-start.5 = (bf16[1,24,8,1536]{3,2,1,0:T(8,128)(2,1)}, bf16[1,24,8,1536]{3,2,1,0:T(8,128)(2,1)}, u32[]{:S(2)}, u32[]{:S(2)}) collective-permute-start(bf16[1,24,8,1536]{3,2,1,0:T(8,128)(2,1)} %get-tuple-element.39), channel_id=1, source_target_pairs={{1,0},{2,1},{3,2},{5,4},{6,5},{7,6},{9,8},{10,9},{11,10},{13,12},{... | collective-permute-start | bytes 1769480 | tf_op jit(solution)/shard_map/ppermute | solution.py:18
  158.0 0.7 copy-start.11
  161.1 126.7 %reduce-scatter.5.cloned.1.call-start = ((), (), s32[]{:S(2)}) async-start(), calls=%async_computation.2 | async-start | bytes 3760128 | tf_op jit(solution)/shard_map/reduce_scatter | solution.py:268
  170.2 19.1 %collective-permute-start.6 = (bf16[1,8,16,1536]{3,2,1,0:T(8,128)(2,1)}, bf16[1,8,16,1536]{3,2,1,0:T(8,128)(2,1)}, u32[]{:S(2)}, u32[]{:S(2)}) collective-permute-start(bf16[1,8,16,1536]{3,2,1,0:T(8,128)(2,1)} %get-tuple-element.40), channel_id=1, source_target_pairs={{0,4},{4,8},{8,12},{1,5},{5,9},{9,13},{2,6},{6,10},{10,14},{3,7},{... | collective-permute-start | bytes 1179656 | tf_op jit(solution)/shard_map/ppermute | solution.py:18
  174.4 14.9 %collective-permute-start.7 = (bf16[1,8,16,1536]{3,2,1,0:T(8,128)(2,1)}, bf16[1,8,16,1536]{3,2,1,0:T(8,128)(2,1)}, u32[]{:S(2)}, u32[]{:S(2)}) collective-permute-start(bf16[1,8,16,1536]{3,2,1,0:T(8,128)(2,1)} %get-tuple-element.41), channel_id=1, source_target_pairs={{4,0},{8,4},{12,8},{5,1},{9,5},{13,9},{6,2},{10,6},{14,10},{7,3},{... | collective-permute-start | bytes 1179656 | tf_op jit(solution)/shard_map/ppermute | solution.py:18
  187.6 3.9 copy-start.14
  190.8 0.7 copy-start.12
  194.4 0.7 copy-start.23
  194.5 188.8 %all-reduce.27.cloned.1.call-start = ((), (), s32[]{:S(2)}) async-start(), calls=%async_computation.4 | async-start | bytes 589824
  199.4 3.8 copy-start.8
  199.4 3.8 copy-start.16
  199.4 93.4 %copy-start.18 = (f32[768]{0:T(1024)S(1)}, f32[768]{0:T(1024)}, u32[]{:S(2)}) copy-start(f32[768]{0:T(1024)} %copy-done.17) | copy-start | bytes 9220
  202.5 0.7 copy-start.7
Sparse Core Ops, SparseCore 0:
  161.3 63.0 reduce-scatter.6
  226.9 60.8 reduce-scatter.4
  291.2 92.0 all-reduce.26
where the time goes:
time: 396 us; the launch traced here: 393 us
  waiting for transfers between devices  144 us (36%)
  local copies, waits for them, and re-layouts  106 us (27%)
  matrix products  37.6 us (9%)
  blocking collectives  35.1 us (9%)
  other arithmetic  29.9 us (8%)
  starting transfers between devices  25 us (6%)
  between operations  15.5 us (4%)
    reduce_scatter x1, waiting for transfers between devices, local(): lax.psum_scatter(input_term.astype(jnp.bfloat16), 'dp', scatter_dimension...  63.4 us
    unnamed x4, waiting for transfers between devices  53.1 us
    unnamed x75, local copies, waits for them, and re-layouts  46.1 us
    psum x1, blocking collectives, local(): lax.psum((shift_term, scale_term, gate_term), ('row', 'col'))  35.1 us
    dot_general x10, matrix products, product(): return jnp.einsum(form, left, right, preferred_element_type=jnp.float32)  34.5 us
    reduce_scatter x1, waiting for transfers between devices, local(): lax.psum_scatter(output_term.astype(jnp.bfloat16), 'dp', scatter_dimensio...  19.7 us
    slice x2, local copies, waits for them, and re-layouts, spread_back(): gathered[:, :, :, position * tile_cells:(position + 1) * tile_cells]  14 us
    ppermute x4, starting transfers between devices, shifted_2(): lax.ppermute(value, axis, [(source, source + steps) for source in range(f...  12.7 us
  transfers between devices with their start and end apart: 11, of which 6 were waited for; matrix products, arithmetic and copies ran while one was open for 17% of the time, Pallas kernels for 0%

commit v1 on v0

v1 whole, which is shorter than its diff:
```python
import math

import jax
import jax.numpy as jnp
import numpy as np
from jax import lax
from jax.sharding import PartitionSpec as P

HEAD_DIM = 64
TILE = 8
CELLS = TILE * TILE
EPSILON = 1e-06
F32 = jnp.float32
BF16 = jnp.bfloat16


def to_tiles(image):
    rows, cols, features = image.shape
    blocks = image.reshape(rows // TILE, TILE, cols // TILE, TILE, features)
    blocks = blocks.transpose(0, 2, 1, 3, 4)
    return blocks.reshape((rows // TILE) * (cols // TILE) * CELLS, features)


def from_tiles(flat, rows, cols):
    features = flat.shape[-1]
    blocks = flat.reshape(rows // TILE, cols // TILE, TILE, TILE, features)
    blocks = blocks.transpose(0, 2, 1, 3, 4)
    return blocks.reshape(rows, cols, features)


def forward_pairs(count):
    return [(i, i + 1) for i in range(count - 1)]


def backward_pairs(count):
    return [(i + 1, i) for i in range(count - 1)]


def halo(grid):
    rows, cols = lax.axis_size("row"), lax.axis_size("col")
    from_above = lax.ppermute(grid[-1:], "row", forward_pairs(rows))
    from_below = lax.ppermute(grid[:1], "row", backward_pairs(rows))
    grid = jnp.concatenate([from_above, grid, from_below], axis=0)
    from_left = lax.ppermute(grid[:, -1:], "col", forward_pairs(cols))
    from_right = lax.ppermute(grid[:, :1], "col", backward_pairs(cols))
    return jnp.concatenate([from_left, grid, from_right], axis=1)


def return_rims(grid):
    rows, cols = lax.axis_size("row"), lax.axis_size("col")
    tile_rows, tile_cols = grid.shape[0] - 2, grid.shape[1] - 2
    from_right = lax.ppermute(grid[:, :1].astype(BF16), "col", backward_pairs(cols))
    from_left = lax.ppermute(grid[:, -1:].astype(BF16), "col", forward_pairs(cols))
    middle = grid[:, 1:-1]
    pad_c = ((0, 0), (0, tile_cols - 1), (0, 0), (0, 0))
    middle = middle + jnp.pad(from_left.astype(F32), pad_c)
    middle = middle + jnp.pad(from_right.astype(F32), (pad_c[0], pad_c[1][::-1], pad_c[2], pad_c[3]))
    from_below = lax.ppermute(middle[:1].astype(BF16), "row", backward_pairs(rows))
    from_above = lax.ppermute(middle[-1:].astype(BF16), "row", forward_pairs(rows))
    inner = middle[1:-1]
    pad_r = ((0, tile_rows - 1), (0, 0), (0, 0), (0, 0))
    inner = inner + jnp.pad(from_above.astype(F32), pad_r)
    inner = inner + jnp.pad(from_below.astype(F32), (pad_r[0][::-1], pad_r[1], pad_r[2], pad_r[3]))
    return inner


def neighbour_table(tile_rows, tile_cols):
    grid_cols = tile_cols + 2
    table = np.zeros((tile_rows * tile_cols, (tile_rows + 2) * grid_cols), np.float32)
    for a in range(tile_rows):
        for b in range(tile_cols):
            for da in range(3):
                for db in range(3):
                    table[a * tile_cols + b, (a + da) * grid_cols + (b + db)] = 1.0
    return table


def exchange(value, extra, axis, xor, split_axis):
    count = lax.axis_size(axis)
    mine = (lax.axis_index(axis) // xor) % 2
    low = lax.index_in_dim(value, 0, split_axis, keepdims=False)
    high = lax.index_in_dim(value, 1, split_axis, keepdims=False)
    keep = jnp.where(mine == 1, high, low)
    send = jnp.where(mine == 1, low, high)
    pairs = [(i, i ^ xor) for i in range(count)]
    got, got_extra = lax.ppermute((send.astype(BF16), extra), axis, pairs)
    return keep + got.astype(F32), extra + got_extra


def reduce_weights(combined, extra):
    model_width = combined.shape[0]
    part = lax.psum_scatter(combined.astype(BF16), "dp", scatter_dimension=0, tiled=True).astype(F32)
    rows, cols = lax.axis_size("row"), lax.axis_size("col")
    rest = part.shape[0]
    value = part.reshape(rest, rows // 2, 2, cols // 2, 2, -1).transpose(1, 2, 3, 4, 0, 5)
    value, extra = exchange(value, extra, "row", 1, 1)
    value, extra = exchange(value, extra, "row", 2, 0)
    value, extra = exchange(value, extra, "col", 1, 1)
    value, extra = exchange(value, extra, "col", 2, 0)
    return value, extra


def local(latent, norm_shift, norm_scale, branch_gate, query_key_value, output_weight, tile_valid, cotangent):
    _, height, across, model_width = latent.shape
    tile_rows, tile_cols = height // TILE, across // TILE
    tiles = tile_rows * tile_cols
    tokens = tiles * CELLS
    heads = model_width // HEAD_DIM
    grid_tiles = (tile_rows + 2) * (tile_cols + 2)

    mask_whole = jnp.pad(tile_valid[0].astype(F32), ((1, 1), (1, 1)))
    row_start = lax.axis_index("row") * tile_rows
    col_start = lax.axis_index("col") * tile_cols
    mask_pad = lax.dynamic_slice(mask_whole, (row_start, col_start), (tile_rows + 2, tile_cols + 2))
    key_mask = jnp.asarray(neighbour_table(tile_rows, tile_cols)) * mask_pad.reshape(1, grid_tiles)
    token_key_mask = jnp.repeat(jnp.repeat(key_mask, CELLS, axis=0), CELLS, axis=1)
    query_valid = mask_pad[1:-1, 1:-1].reshape(tiles)
    token_valid = jnp.repeat(query_valid, CELLS)[:, None]

    image = to_tiles(latent[0])
    incoming = to_tiles(cotangent[0]).astype(F32)
    values = image.astype(F32)
    center = values - jnp.mean(values, axis=-1, keepdims=True)
    inverse = lax.rsqrt(jnp.mean(center * center, axis=-1, keepdims=True) + EPSILON)
    normed = center * inverse
    scale_one = 1.0 + norm_scale
    modulated = (normed * scale_one + norm_shift).astype(BF16)
    projections = jnp.dot(modulated, query_key_value, preferred_element_type=F32).astype(BF16)

    queries = projections[:, :model_width]
    key_value = projections[:, model_width:].reshape(tile_rows, tile_cols, CELLS, 2 * model_width)
    grid = halo(key_value).reshape(grid_tiles * CELLS, 2 * model_width)

    q_h = queries.reshape(tokens, heads, HEAD_DIM).transpose(1, 0, 2)
    k_h = grid[:, :model_width].reshape(-1, heads, HEAD_DIM).transpose(1, 0, 2)
    v_h = grid[:, model_width:].reshape(-1, heads, HEAD_DIM).transpose(1, 0, 2)

    scale = 1.0 / math.sqrt(HEAD_DIM)
    scores = jnp.einsum("hqe,hke->hqk", q_h, k_h, preferred_element_type=F32) * scale
    unnormed = jnp.where(token_key_mask[None] > 0.0, jnp.exp(scores), 0.0)
    denominator = jnp.sum(unnormed, axis=-1, keepdims=True) + (1.0 - token_valid)[None]
    attention = (unnormed / denominator).astype(BF16)
    attended_h = jnp.einsum("hqk,hke->hqe", attention, v_h, preferred_element_type=F32) * token_valid[None]
    attended = attended_h.astype(BF16).transpose(1, 0, 2).reshape(tokens, model_width)

    projected = jnp.dot(attended, output_weight, preferred_element_type=F32)
    gate_term = jnp.sum(incoming * projected, axis=0)
    grad_projected = (incoming * branch_gate).astype(BF16)
    output_term = jnp.einsum("nd,nf->df", attended, grad_projected, preferred_element_type=F32)
    grad_image = jnp.einsum("nf,df->nd", grad_projected, output_weight, preferred_element_type=F32)
    grad_attended = (grad_image * token_valid).astype(BF16)
    ga_h = grad_attended.reshape(tokens, heads, HEAD_DIM).transpose(1, 0, 2)

    grad_weights = jnp.einsum("hqe,hke->hqk", ga_h, v_h, preferred_element_type=F32)
    attention_wide = attention.astype(F32)
    row_inner = jnp.sum(attention_wide * grad_weights, axis=-1, keepdims=True)
    grad_scores = (attention_wide * (grad_weights - row_inner) * scale).astype(BF16)
    grad_q = jnp.einsum("hqk,hke->hqe", grad_scores, k_h, preferred_element_type=F32).astype(BF16)
    grad_k = jnp.einsum("hqk,hqe->hke", grad_scores, q_h, preferred_element_type=F32)
    grad_v = jnp.einsum("hqk,hqe->hke", attention, ga_h, preferred_element_type=F32)
    grad_k = grad_k.transpose(1, 0, 2).reshape(tile_rows + 2, tile_cols + 2, CELLS, model_width)
    grad_v = grad_v.transpose(1, 0, 2).reshape(tile_rows + 2, tile_cols + 2, CELLS, model_width)
    pair_grid = jnp.concatenate([grad_k, grad_v], axis=-1)
    pair_grads = return_rims(pair_grid).reshape(tokens, 2 * model_width)

    query_flat = grad_q.transpose(1, 0, 2).reshape(tokens, model_width)
    grad_all = jnp.concatenate([query_flat, pair_grads.astype(BF16)], axis=-1)
    input_term = jnp.einsum("nd,nf->df", modulated, grad_all, preferred_element_type=F32)
    grad_modulated = jnp.einsum("nf,df->nd", grad_all, query_key_value, preferred_element_type=F32)
    shift_term = jnp.sum(grad_modulated, axis=0)
    scale_term = jnp.sum(grad_modulated * normed, axis=0)
    grad_normed = grad_modulated * scale_one
    latent_term = inverse * (
        grad_normed
        - jnp.mean(grad_normed, axis=-1, keepdims=True)
        - normed * jnp.mean(grad_normed * normed, axis=-1, keepdims=True)
    )

    mixed = (values + branch_gate * projected).astype(BF16)
    latent_grad = (incoming + latent_term).astype(BF16)

    blocks = lax.axis_size("row") * lax.axis_size("col")
    width_in = input_term.shape[1] // blocks
    width_out = output_term.shape[1] // blocks
    combined = jnp.concatenate(
        [
            input_term.reshape(model_width, blocks, width_in),
            output_term.reshape(model_width, blocks, width_out),
        ],
        axis=-1,
    ).reshape(model_width, blocks * (width_in + width_out))
    reduced, sums = reduce_weights(combined, jnp.stack([shift_term, scale_term, gate_term]))
    input_grad = reduced[:, :width_in]
    output_grad = reduced[:, width_in:]

    return (
        from_tiles(mixed, height, across)[None],
        from_tiles(latent_grad, height, across)[None],
        input_grad,
        output_grad,
        sums[0:1],
        sums[1:2],
        sums[2:3],
    )


def solution(mesh):
    placed = (
        P("dp", "row", "col", None),
        P("dp", None),
        P("dp", None),
        P("dp", None),
        P(),
        P(),
        P("dp", None, None),
        P("dp", "row", "col", None),
    )
    return jax.shard_map(
        local,
        mesh=mesh,
        in_specs=placed,
        out_specs=(
            P("dp", "row", "col", None),
            P("dp", "row", "col", None),
            P("dp", ("row", "col")),
            P("dp", ("row", "col")),
            P("dp", None),
            P("dp", None),
            P("dp", None),
        ),
        check_vma=False,
    )
```

time: 396 us -> 287 us (0.72)
  waiting for transfers between devices: 144 us -> 78.1 us
  blocking collectives: 35.1 us -> 0 us
  local copies, waits for them, and re-layouts: 106 us -> 75.4 us
  starting transfers between devices: 25 us -> 36.9 us
  other arithmetic: 29.9 us -> 41.1 us
    unnamed x4 -> x1, waiting for transfers between devices: 53.1 us -> 0.02 us
    unnamed x75 -> x43, local copies, waits for them, and re-layouts: 46.1 us -> 7.4 us
    psum x1 -> x0, blocking collectives: 35.1 us -> none  [local(): lax.psum((shift_term, scale_term, gate_term), ('row', 'col'))]
    reduce_scatter x2 -> x1, waiting for transfers between devices: 83.2 us -> 55.3 us  [reduce_weights(): lax.psum_scatter(combined.astype(BF16), 'dp', scatter_dimension=0, tiled=...]
    reshape x2 -> x6, local copies, waits for them, and re-layouts: 3.9 us -> 25.8 us  [the longest x2 11.4 us: local(): grad_v.transpose(1, 0, 2)]
    slice x10 -> x9, local copies, waits for them, and re-layouts: 28 us -> 10.2 us  [the longest x2 3.37 us: local(): queries = projections[:, :model_width]]
    ppermute x8 -> x16, waiting for transfers between devices: 7.46 us -> 22.8 us  [the longest x8 15.6 us: exchange(): got, got_extra = lax.ppermute((send.astype(BF16), extra), axis, pairs)]
    ppermute x8 -> x16, starting transfers between devices: 24.9 us -> 36.9 us  [the longest x8 12.8 us: exchange(): got, got_extra = lax.ppermute((send.astype(BF16), extra), axis, pairs)]
  transfers between devices with their start and end apart: 11 -> 17, of which waited for: 6 -> 9; matrix products, arithmetic and copies ran while one was open for 17% -> 22% of each run, Pallas kernels for 0% -> 0%
where the time goes in v1:
time: 287 us; the launch traced here: 285 us
  waiting for transfers between devices  78.1 us (27%)
  local copies, waits for them, and re-layouts  75.4 us (26%)
  other arithmetic  41.1 us (14%)
  matrix products  39 us (14%)
  starting transfers between devices  36.9 us (13%)
  between operations  14.4 us (5%)
    reduce_scatter x1, waiting for transfers between devices, reduce_weights(): lax.psum_scatter(combined.astype(BF16), 'dp', scatter_dimension=0, tiled=...  55.3 us
    ppermute x8, waiting for transfers between devices, exchange(): got, got_extra = lax.ppermute((send.astype(BF16), extra), axis, pairs)  15.6 us
    ppermute x8, starting transfers between devices, exchange(): got, got_extra = lax.ppermute((send.astype(BF16), extra), axis, pairs)  12.8 us
    reshape x2, local copies, waits for them, and re-layouts, local(): grad_v.transpose(1, 0, 2)  11.4 us
    reshape x2, local copies, waits for them, and re-layouts, local(): grad_k.transpose(1, 0, 2)  11.4 us
    dot_general x1, matrix products, local(): jnp.einsum('hqk,hqe->hke', grad_scores, q_h, preferred_element_type=F32)  8.11 us
    dot_general x1, matrix products, local(): jnp.einsum('hqk,hke->hqe', grad_scores, k_h, preferred_element_type=F32)  7.67 us
    unnamed x43, local copies, waits for them, and re-layouts  7.4 us
  transfers between devices with their start and end apart: 17, of which 9 were waited for; matrix products, arithmetic and copies ran while one was open for 22% of the time, Pallas kernels for 0%

profile of v1, /device:TPU:4, one launch (start us, length us, event | category | flops | bytes accessed | tf_op | source)
XLA Modules:
  0.0 284.9 jit_solution(16031567494202882975)
XLA Ops:
  8.4 1.7 multiply_reduce_fusion.2
  15.0 1.8 copy.115
  21.5 3.1 %collective-permute-start = (bf16[1,2,64,1536]{3,2,1,0:T(8,128)(2,1)}, bf16[1,2,64,1536]{3,2,1,0:T(8,128)(2,1)}, u32[]{:S(2)}, u32[]{:S(2)}) collective-permute-start(bf16[1,2,64,1536]{3,2,1,0:T(8,128)(2,1)} %bitcast.8), channel_id=1, source_target_pairs={{0,4},{4,8},{8,12},{1,5},{5,9},{9,13},{2,6},{6,10},{10,14},{3,7},{... | collective-permute-start | bytes 1179656 | tf_op jit(solution)/shard_map/ppermute | solution.py:41
  24.6 2.7 collective-permute-start.1
  35.0 1.7 fusion.20
  39.8 4.3 %collective-permute-start.2 = (bf16[3,1,64,1536]{3,2,1,0:T(8,128)(2,1)}, bf16[3,1,64,1536]{3,2,1,0:T(8,128)(2,1)}, u32[]{:S(2)}, u32[]{:S(2)}) collective-permute-start(bf16[3,1,64,1536]{3,2,1,0:T(8,128)(2,1)} %get-tuple-element.19), channel_id=1, source_target_pairs={{0,1},{1,2},{2,3},{4,5},{5,6},{6,7},{8,9},{9,10},{10,11},{12,13},{... | collective-permute-start | bytes 1769480 | tf_op jit(solution)/shard_map/ppermute | solution.py:44
  53.4 1.8 copy.117
  57.7 2.5 fusion.13
  60.2 1.7 copy.122
  63.1 1.9 pad_maximum_fusion.2
  66.5 2.4 copy.146
  68.9 2.4 copy.147
  71.3 2.7 fusion.4
  75.3 3.0 %fusion.47 = f32[12,128,768]{2,1,0:T(8,128)} fusion(bf16[12,128,64]{1,2,0:T(8,128)(2,1)S(1)} %bitcast.187, bf16[12,768,64]{1,2,0:T(8,128)(2,1)S(1)} %bitcast.182), kind=kOutput, calls=%fused_computation.105 | convolution fusion | flops 150994944 | bytes 6094848 | tf_op jit(solution)/shard_map/hqe,hke->hqk/dot_general | solution.py:154
  78.3 1.9 convolution_bitcast_fusion
  80.2 8.1 %fusion.11 = f32[768,12,64]{0,2,1:T(8,128)} fusion(bf16[12,128,64]{1,2,0:T(8,128)(2,1)} %bitcast.204, bf16[12,128,768]{2,1,0:T(8,128)(2,1)} %copy-done.2, f32[12,128,768]{2,1,0:T(8,128)} %fusion.47), kind=kOutput, calls=%fused_computation.22 | convolution fusion | flops 159254784 | bytes 9633792 | tf_op jit(solution)/shard_map/hqk,hqe->hke/dot_general | solution.py:159
  88.3 5.3 %reshape.218 = f32[3,4,64,768]{2,1,0,3:T(4,128)} reshape(f32[768,12,64]{0,2,1:T(8,128)} %fusion.11) | data formatting | bytes 4718592 | tf_op jit(solution)/shard_map/reshape | solution.py:161
  93.6 6.0 %copy.123 = f32[3,4,64,768]{3,2,1,0:T(8,128)} copy(f32[3,4,64,768]{2,1,0,3:T(4,128)} %reshape.218) | data formatting | bytes 4718592 | tf_op jit(solution)/shard_map/reshape | solution.py:161
  99.7 5.3 %reshape.219 = f32[3,4,64,768]{2,1,0,3:T(4,128)} reshape(f32[768,12,64]{0,2,1:T(8,128)} %convolution_bitcast_fusion) | data formatting | bytes 4718592 | tf_op jit(solution)/shard_map/reshape | solution.py:162
  105.0 6.1 %copy.124 = f32[3,4,64,768]{3,2,1,0:T(8,128)} copy(f32[3,4,64,768]{2,1,0,3:T(4,128)} %reshape.219) | data formatting | bytes 4718592 | tf_op jit(solution)/shard_map/reshape | solution.py:162
  111.1 2.7 fusion.1
  114.9 5.4 %collective-permute-start.4 = (bf16[3,1,64,1536]{3,2,1,0:T(8,128)(2,1)}, bf16[3,1,64,1536]{3,2,1,0:T(8,128)(2,1)}, u32[]{:S(2)}, u32[]{:S(2)}) collective-permute-start(bf16[3,1,64,1536]{3,2,1,0:T(8,128)(2,1)} %get-tuple-element.13), channel_id=1, source_target_pairs={{0,1},{1,2},{2,3},{4,5},{5,6},{6,7},{8,9},{9,10},{10,11},{12,13},{... | collective-permute-start | bytes 1769480 | tf_op jit(solution)/shard_map/ppermute | solution.py:53
  121.7 1.7 copy.128
  123.5 2.0 add_convert_fusion
  125.4 3.6 %fusion.12 = bf16[12,128,64]{1,2,0:T(8,128)(2,1)} fusion(bf16[12,128,768]{2,1,0:T(8,128)(2,1)} %copy-done.2, bf16[12,768,64]{1,2,0:T(8,128)(2,1)} %bitcast.181, f32[128]{0:T(128)} %broadcast_in_dim_reshape.10), kind=kOutput, calls=%fused_computation.28 | convolution fusion | flops 151191552 | bytes 3736064 | tf_op jit(solution)/shard_map/hqk,hke->hqe/dot_general | solution.py:143
  130.6 5.0 %collective-permute-done.5 = bf16[3,1,64,1536]{3,2,1,0:T(8,128)(2,1)} collective-permute-done((bf16[3,1,64,1536]{3,2,1,0:T(8,128)(2,1)}, bf16[3,1,64,1536]{3,2,1,0:T(8,128)(2,1)}, u32[]{:S(2)}, u32[]{:S(2)}) %collective-permute-start.5) | collective-permute-done | bytes 589856 | tf_op jit(solution)/shard_map/ppermute | solution.py:52
  135.6 3.6 %fusion.40 = (bf16[3,2,64,1536]{3,2,1,0:T(8,128)(2,1)S(1)}, f32[3,2,64,1536]{3,2,1,0:T(8,128)}) fusion(bf16[3,1,64,1536]{3,2,1,0:T(8,128)(2,1)} %collective-permute-done.5, bf16[3,1,64,1536]{3,2,1,0:T(8,128)(2,1)} %collective-permute-done.4, f32[3,4,64,768]{3,2,1,0:T(8,128)} %copy.124, f32[3,4,64,768]{3,2,1,0:T(8,128)S(1)} %copy-done.1), kind=kLoop, calls=%fused_computation.99 | loop fusion | flops 3538944 | bytes 9437184 | tf_op jit(solution)/shard_map/convert.17
  140.1 3.8 %collective-permute-start.6 = (bf16[1,2,64,1536]{3,2,1,0:T(8,128)(2,1)}, bf16[1,2,64,1536]{3,2,1,0:T(8,128)(2,1)}, u32[]{:S(2)}, u32[]{:S(2)}) collective-permute-start(bf16[1,2,64,1536]{3,2,1,0:T(8,128)(2,1)} %get-tuple-element.17), channel_id=1, source_target_pairs={{0,4},{4,8},{8,12},{1,5},{5,9},{9,13},{2,6},{6,10},{10,14},{3,7},{... | collective-permute-start | bytes 1179656 | tf_op jit(solution)/shard_map/ppermute | solution.py:59
  143.8 2.1 collective-permute-start.7
  145.9 7.7 %fusion.14 = bf16[12,128,64]{1,2,0:T(8,128)(2,1)} fusion(bf16[12,768,64]{1,2,0:T(8,128)(2,1)} %bitcast.195, bf16[12,128,768]{2,1,0:T(8,128)(2,1)} %copy-done.2, f32[12,128,768]{2,1,0:T(8,128)} %fusion.47), kind=kOutput, calls=%fused_computation.30 | convolution fusion | flops 159353088 | bytes 8454144 | tf_op jit(solution)/shard_map/hqk,hke->hqe/dot_general | solution.py:158
  153.6 1.7 copy.125
  155.3 2.6 convolution_convert_fusion.2
  161.0 2.1 copy.127
  163.1 2.3 convolution_convert_fusion.1
  165.5 2.7 pad_maximum_fusion.1
  168.1 6.6 %copy.130 = bf16[768,3072]{1,0:T(8,128)(2,1)} copy(bf16[768,3072]{0,1:T(8,128)(2,1)} %bitcast.180) | data formatting | bytes 9437184 | tf_op jit(solution)/shard_map/convert_element_type | solution.py:92
  175.5 2.8 multiply_reduce_fusion
  180.2 2.6 collective-permute-start.12
  182.8 2.0 collective-permute-done.12
  186.8 55.3 %reduce-scatter.2.cloned.1.call-done = bf16[48,3072]{1,0:T(8,128)(2,1)} async-done(((bf16[768,3072]{1,0:T(8,128)(2,1)}), bf16[48,3072]{1,0:T(8,128)(2,1)}) %reduce-scatter.2.cloned.1.call-update) | async-done | bytes 294928 | tf_op jit(solution)/shard_map/reduce_scatter | solution.py:92
  242.1 2.6 reshape.224
  244.7 2.0 fusion.30
  250.2 2.3 collective-permute-done.14
  252.5 3.0 %collective-permute-start.15 = (f32[3,768]{1,0:T(4,128)S(1)}, f32[3,768]{1,0:T(4,128)}, u32[]{:S(2)}, u32[]{:S(2)}) collective-permute-start(f32[3,768]{1,0:T(4,128)S(1)} %add.149), channel_id=1, source_target_pairs={{0,2},{1,3},{2,0},{3,1},{4,6},{5,7},{6,4},{7,5},{8,10},{9,11},{10,... | collective-permute-start | bytes 27656 | tf_op jit(solution)/shard_map/ppermute | solution.py:86
  262.5 4.7 %collective-permute-done.9 = bf16[2,2,48,192]{3,1,0,2:T(2,128)(2,1)S(1)} collective-permute-done((bf16[2,2,48,192]{3,1,0,2:T(2,128)(2,1)S(1)}, bf16[2,2,48,192]{3,1,0,2:T(2,128)(2,1)S(1)}, u32[]{:S(2)}, u32[]{:S(2)}) %collective-permute-start.9) | collective-permute-done | bytes 73760 | tf_op jit(solution)/shard_map/ppermute | solution.py:86
  268.4 3.4 %collective-permute-done.10 = bf16[2,48,192]{2,0,1:T(2,128)(2,1)S(1)} collective-permute-done((bf16[2,48,192]{2,0,1:T(2,128)(2,1)S(1)}, bf16[2,48,192]{2,0,1:T(2,128)(2,1)S(1)}, u32[]{:S(2)}, u32[]{:S(2)}) %collective-permute-start.10) | collective-permute-done | bytes 36896 | tf_op jit(solution)/shard_map/ppermute | solution.py:86
  272.0 2.2 collective-permute-start.11
  274.2 3.2 %collective-permute-done.11 = bf16[48,192]{1,0:T(8,128)(2,1)S(1)} collective-permute-done((bf16[48,192]{1,0:T(8,128)(2,1)S(1)}, bf16[48,192]{1,0:T(8,128)(2,1)S(1)}, u32[]{:S(2)}, u32[]{:S(2)}) %collective-permute-start.11) | collective-permute-done | bytes 18464 | tf_op jit(solution)/shard_map/ppermute | solution.py:86
  (121 shorter events, 62.7 us)
Async XLA Ops:
  7.2 12.1 %copy-start = (bf16[768,2304]{1,0:T(8,128)(2,1)S(1)}, bf16[768,2304]{1,0:T(8,128)(2,1)}, u32[]{:S(2)}) copy-start(bf16[768,2304]{1,0:T(8,128)(2,1)} %param.13) | copy-start | bytes 10616836
  7.2 234.9 %reduce-scatter.2.cloned.1.call-start = ((), (), s32[]{:S(2)}) async-start(), calls=%async_computation.1 | async-start | bytes 5013504 | tf_op jit(solution)/shard_map/reduce_scatter | solution.py:92
  19.9 0.8 copy-start.8
  21.5 15.2 %collective-permute-start = (bf16[1,2,64,1536]{3,2,1,0:T(8,128)(2,1)}, bf16[1,2,64,1536]{3,2,1,0:T(8,128)(2,1)}, u32[]{:S(2)}, u32[]{:S(2)}) collective-permute-start(bf16[1,2,64,1536]{3,2,1,0:T(8,128)(2,1)} %bitcast.8), channel_id=1, source_target_pairs={{0,4},{4,8},{8,12},{1,5},{5,9},{9,13},{2,6},{6,10},{10,14},{3,7},{... | collective-permute-start | bytes 1179656 | tf_op jit(solution)/shard_map/ppermute | solution.py:41
  24.6 12.8 %collective-permute-start.1 = (bf16[1,2,64,1536]{3,2,1,0:T(8,128)(2,1)}, bf16[1,2,64,1536]{3,2,1,0:T(8,128)(2,1)}, u32[]{:S(2)}, u32[]{:S(2)}) collective-permute-start(bf16[1,2,64,1536]{3,2,1,0:T(8,128)(2,1)} %bitcast.8), channel_id=1, source_target_pairs={{4,0},{8,4},{12,8},{5,1},{9,5},{13,9},{6,2},{10,6},{14,10},{7,3},{... | collective-permute-start | bytes 1179656 | tf_op jit(solution)/shard_map/ppermute | solution.py:42
  39.8 23.3 %collective-permute-start.2 = (bf16[3,1,64,1536]{3,2,1,0:T(8,128)(2,1)}, bf16[3,1,64,1536]{3,2,1,0:T(8,128)(2,1)}, u32[]{:S(2)}, u32[]{:S(2)}) collective-permute-start(bf16[3,1,64,1536]{3,2,1,0:T(8,128)(2,1)} %get-tuple-element.19), channel_id=1, source_target_pairs={{0,1},{1,2},{2,3},{4,5},{5,6},{6,7},{8,9},{9,10},{10,11},{12,13},{... | collective-permute-start | bytes 1769480 | tf_op jit(solution)/shard_map/ppermute | solution.py:44
  44.1 19.0 %collective-permute-start.3 = (bf16[3,1,64,1536]{3,2,1,0:T(8,128)(2,1)}, bf16[3,1,64,1536]{3,2,1,0:T(8,128)(2,1)}, u32[]{:S(2)}, u32[]{:S(2)}) collective-permute-start(bf16[3,1,64,1536]{3,2,1,0:T(8,128)(2,1)} %get-tuple-element.20), channel_id=1, source_target_pairs={{1,0},{2,1},{3,2},{5,4},{6,5},{7,6},{9,8},{10,9},{11,10},{13,12},{... | collective-permute-start | bytes 1769480 | tf_op jit(solution)/shard_map/ppermute | solution.py:45
  71.3 2.7 copy-start.19
  71.3 2.8 copy-start.13
  74.1 1.3 copy-start.3
  74.1 1.3 copy-start.9
  75.0 3.3 %copy-start.2 = (bf16[12,128,768]{2,1,0:T(8,128)(2,1)}, bf16[12,128,768]{2,1,0:T(8,128)(2,1)S(1)}, u32[]{:S(2)}) copy-start(bf16[12,128,768]{2,1,0:T(8,128)(2,1)S(1)} %divide_convert_fusion) | copy-start | bytes 7077892
  114.9 15.7 %collective-permute-start.4 = (bf16[3,1,64,1536]{3,2,1,0:T(8,128)(2,1)}, bf16[3,1,64,1536]{3,2,1,0:T(8,128)(2,1)}, u32[]{:S(2)}, u32[]{:S(2)}) collective-permute-start(bf16[3,1,64,1536]{3,2,1,0:T(8,128)(2,1)} %get-tuple-element.13), channel_id=1, source_target_pairs={{0,1},{1,2},{2,3},{4,5},{5,6},{6,7},{8,9},{9,10},{10,11},{12,13},{... | collective-permute-start | bytes 1769480 | tf_op jit(solution)/shard_map/ppermute | solution.py:53
  120.3 15.3 %collective-permute-start.5 = (bf16[3,1,64,1536]{3,2,1,0:T(8,128)(2,1)}, bf16[3,1,64,1536]{3,2,1,0:T(8,128)(2,1)}, u32[]{:S(2)}, u32[]{:S(2)}) collective-permute-start(bf16[3,1,64,1536]{3,2,1,0:T(8,128)(2,1)} %get-tuple-element.14), channel_id=1, source_target_pairs={{1,0},{2,1},{3,2},{5,4},{6,5},{7,6},{9,8},{10,9},{11,10},{13,12},{... | collective-permute-start | bytes 1769480 | tf_op jit(solution)/shard_map/ppermute | solution.py:52
  123.5 12.1 %copy-start.1 = (f32[3,4,64,768]{3,2,1,0:T(8,128)S(1)}, f32[3,4,64,768]{3,2,1,0:T(8,128)}, u32[]{:S(2)}) copy-start(f32[3,4,64,768]{3,2,1,0:T(8,128)} %copy.123) | copy-start | bytes 7077892
  140.1 17.8 %collective-permute-start.6 = (bf16[1,2,64,1536]{3,2,1,0:T(8,128)(2,1)}, bf16[1,2,64,1536]{3,2,1,0:T(8,128)(2,1)}, u32[]{:S(2)}, u32[]{:S(2)}) collective-permute-start(bf16[1,2,64,1536]{3,2,1,0:T(8,128)(2,1)} %get-tuple-element.17), channel_id=1, source_target_pairs={{0,4},{4,8},{8,12},{1,5},{5,9},{9,13},{2,6},{6,10},{10,14},{3,7},{... | collective-permute-start | bytes 1179656 | tf_op jit(solution)/shard_map/ppermute | solution.py:59
  143.8 14.1 %collective-permute-start.7 = (bf16[1,2,64,1536]{3,2,1,0:T(8,128)(2,1)}, bf16[1,2,64,1536]{3,2,1,0:T(8,128)(2,1)}, u32[]{:S(2)}, u32[]{:S(2)}) collective-permute-start(bf16[1,2,64,1536]{3,2,1,0:T(8,128)(2,1)} %get-tuple-element.18), channel_id=1, source_target_pairs={{4,0},{8,4},{12,8},{5,1},{9,5},{13,9},{6,2},{10,6},{14,10},{7,3},{... | collective-permute-start | bytes 1179656 | tf_op jit(solution)/shard_map/ppermute | solution.py:58
  155.3 4.8 %copy-start.12 = (bf16[128,768]{1,0:T(8,128)(2,1)S(1)}, bf16[128,768]{1,0:T(8,128)(2,1)}, u32[]{:S(2)}) copy-start(bf16[128,768]{1,0:T(8,128)(2,1)} %copy.125) | copy-start | bytes 589828
  159.4 0.8 copy-start.11
  163.1 2.3 copy-start.4
  174.7 0.7 copy-start.15
  174.8 0.7 copy-start.17
  174.8 0.7 copy-start.18
  175.4 2.8 copy-start.5
  175.4 2.8 copy-start.6
  175.4 2.8 copy-start.7
  175.5 2.8 copy-start.10
  175.5 2.8 copy-start.16
  180.2 4.6 %collective-permute-start.12 = (f32[3,768]{1,0:T(4,128)}, f32[3,768]{1,0:T(4,128)}, u32[]{:S(2)}, u32[]{:S(2)}) collective-permute-start(f32[3,768]{1,0:T(4,128)} %pad_maximum_fusion.6), channel_id=1, source_target_pairs={{0,4},{4,0},{8,12},{12,8},{1,5},{5,1},{9,13},{13,9},{2,6},{6,2},{1... | collective-permute-start | bytes 27656 | tf_op jit(solution)/shard_map/ppermute | solution.py:86
  186.1 61.9 %collective-permute-start.13 = (f32[3,768]{1,0:T(4,128)}, f32[3,768]{1,0:T(4,128)}, u32[]{:S(2)}, u32[]{:S(2)}) collective-permute-start(f32[3,768]{1,0:T(4,128)} %fusion.39), channel_id=1, source_target_pairs={{0,8},{4,12},{8,0},{12,4},{1,9},{5,13},{9,1},{13,5},{2,10},{6,14},... | collective-permute-start | bytes 27656 | tf_op jit(solution)/shard_map/ppermute | solution.py:86
  246.7 12.7 %collective-permute-start.8 = (bf16[2,2,2,48,192]{4,2,1,0,3:T(2,128)(2,1)}, bf16[2,2,2,48,192]{4,2,1,0,3:T(2,128)(2,1)}, u32[]{:S(2)}, u32[]{:S(2)}) collective-permute-start(bf16[2,2,2,48,192]{4,2,1,0,3:T(2,128)(2,1)} %fusion.30), channel_id=1, source_target_pairs={{0,4},{4,0},{8,12},{12,8},{1,5},{5,1},{9,13},{13,9},{2,6},{6,2},{1... | collective-permute-start | bytes 442376 | tf_op jit(solution)/shard_map/ppermute | solution.py:86
  248.7 3.8 %collective-permute-start.14 = (f32[3,768]{1,0:T(4,128)S(1)}, f32[3,768]{1,0:T(4,128)S(1)}, u32[]{:S(2)}, u32[]{:S(2)}) collective-permute-start(f32[3,768]{1,0:T(4,128)S(1)} %fusion.69), channel_id=1, source_target_pairs={{0,1},{1,0},{2,3},{3,2},{4,5},{5,4},{6,7},{7,6},{8,9},{9,8},{10,11... | collective-permute-start | bytes 27656 | tf_op jit(solution)/shard_map/ppermute | solution.py:86
  252.5 6.3 %collective-permute-start.15 = (f32[3,768]{1,0:T(4,128)S(1)}, f32[3,768]{1,0:T(4,128)}, u32[]{:S(2)}, u32[]{:S(2)}) collective-permute-start(f32[3,768]{1,0:T(4,128)S(1)} %add.149), channel_id=1, source_target_pairs={{0,2},{1,3},{2,0},{3,1},{4,6},{5,7},{6,4},{7,5},{8,10},{9,11},{10,... | collective-permute-start | bytes 27656 | tf_op jit(solution)/shard_map/ppermute | solution.py:86
  261.0 6.2 %collective-permute-start.9 = (bf16[2,2,48,192]{3,1,0,2:T(2,128)(2,1)S(1)}, bf16[2,2,48,192]{3,1,0,2:T(2,128)(2,1)S(1)}, u32[]{:S(2)}, u32[]{:S(2)}) collective-permute-start(bf16[2,2,48,192]{3,1,0,2:T(2,128)(2,1)S(1)} %fusion.32), channel_id=1, source_target_pairs={{0,8},{4,12},{8,0},{12,4},{1,9},{5,13},{9,1},{13,5},{2,10},{6,14},... | collective-permute-start | bytes 221192 | tf_op jit(solution)/shard_map/ppermute | solution.py:86
  267.6 4.2 %collective-permute-start.10 = (bf16[2,48,192]{2,0,1:T(2,128)(2,1)S(1)}, bf16[2,48,192]{2,0,1:T(2,128)(2,1)S(1)}, u32[]{:S(2)}, u32[]{:S(2)}) collective-permute-start(bf16[2,48,192]{2,0,1:T(2,128)(2,1)S(1)} %copy.140), channel_id=1, source_target_pairs={{0,1},{1,0},{2,3},{3,2},{4,5},{5,4},{6,7},{7,6},{8,9},{9,8},{10,11... | collective-permute-start | bytes 110600 | tf_op jit(solution)/shard_map/ppermute | solution.py:86
  272.0 5.4 %collective-permute-start.11 = (bf16[48,192]{1,0:T(8,128)(2,1)S(1)}, bf16[48,192]{1,0:T(8,128)(2,1)S(1)}, u32[]{:S(2)}, u32[]{:S(2)}) collective-permute-start(bf16[48,192]{1,0:T(8,128)(2,1)S(1)} %bitcast.208), channel_id=1, source_target_pairs={{0,2},{1,3},{2,0},{3,1},{4,6},{5,7},{6,4},{7,5},{8,10},{9,11},{10,... | collective-permute-start | bytes 55304 | tf_op jit(solution)/shard_map/ppermute | solution.py:86
  277.4 0.7 copy-start.14
Sparse Core Ops, SparseCore 0:
  174.9 67.1 reduce-scatter.1

commit v2 on v1

--- a/solution.py
+++ b/solution.py
@@ -5,6 +5,8 @@
 import numpy as np
 from jax import lax
 from jax.sharding import PartitionSpec as P
+from jax.experimental import pallas as pl
+from jax.experimental.pallas import tpu as pltpu
 
 HEAD_DIM = 64
 TILE = 8
@@ -100,6 +102,65 @@
     return value, extra
 
 
+def attention_kernel(q_ref, kv_ref, ga_ref, mask_ref, valid_ref, att_ref, gq_ref, gkv_ref):
+    model_width = q_ref.shape[1]
+    pair = 2 * HEAD_DIM
+    scale = 1.0 / math.sqrt(HEAD_DIM)
+    keep = mask_ref[...] > 0.0
+    valid = valid_ref[...]
+    empty = 1.0 - valid
+    lane = lax.broadcasted_iota(jnp.int32, (1, pair), 1)
+    first = lane < HEAD_DIM
+    for p in range(model_width // pair):
+        cols = slice(p * pair, (p + 1) * pair)
+        q2 = q_ref[:, cols]
+        k2 = kv_ref[:, cols]
+        v2 = kv_ref[:, model_width + p * pair : model_width + (p + 1) * pair]
+        ga2 = ga_ref[:, cols]
+        outs = []
+        for j in range(2):
+            side = first if j == 0 else jnp.logical_not(first)
+            qj = jnp.where(side, q2, jnp.zeros_like(q2))
+            gaj = jnp.where(side, ga2, jnp.zeros_like(ga2))
+            scores = lax.dot_general(qj, k2, (((1,), (1,)), ((), ())), preferred_element_type=F32) * scale
+            unnormed = jnp.where(keep, jnp.exp(scores), 0.0)
+            denominator = jnp.sum(unnormed, axis=1, keepdims=True) + empty
+            attention = (unnormed / denominator).astype(BF16)
+            attended = jnp.dot(attention, v2, preferred_element_type=F32)
+            weights = lax.dot_general(gaj, v2, (((1,), (1,)), ((), ())), preferred_element_type=F32)
+            wide = attention.astype(F32)
+            inner = jnp.sum(wide * weights, axis=1, keepdims=True)
+            grad_scores = (wide * (weights - inner) * scale).astype(BF16)
+            gq = jnp.dot(grad_scores, k2, preferred_element_type=F32)
+            gk = jnp.dot(grad_scores.T, qj, preferred_element_type=F32)
+            gv = jnp.dot(attention.T, gaj, preferred_element_type=F32)
+            outs.append((attended, gq, gk, gv))
+        (a0, q0, k0, v0), (a1, q1, k1, v1) = outs
+        att_ref[:, cols] = (jnp.where(first, a0, a1) * valid).astype(att_ref.dtype)
+        gq_ref[:, cols] = jnp.where(first, q0, q1).astype(gq_ref.dtype)
+        gkv_ref[:, cols] = jnp.where(first, k0, k1)
+        gkv_ref[:, model_width + p * pair : model_width + (p + 1) * pair] = jnp.where(first, v0, v1)
+
+
+def attention(queries, grid, grad_attended, token_key_mask, token_valid):
+    tokens, model_width = queries.shape
+    keys = grid.shape[0]
+    whole = pl.BlockSpec(memory_space=pltpu.VMEM)
+    flops = 2 * 2 * tokens * keys * 2 * model_width * 5
+    return pl.pallas_call(
+        attention_kernel,
+        out_shape=(
+            jax.ShapeDtypeStruct((tokens, model_width), BF16),
+            jax.ShapeDtypeStruct((tokens, model_width), BF16),
+            jax.ShapeDtypeStruct((keys, 2 * model_width), F32),
+        ),
+        in_specs=[whole] * 5,
+        out_specs=(whole, whole, whole),
+        compiler_params=pltpu.CompilerParams(vmem_limit_bytes=48 * 1024 * 1024),
+        cost_estimate=pl.CostEstimate(flops=flops, transcendentals=2 * tokens * keys * model_width // HEAD_DIM, bytes_accessed=12 * 1024 * 1024),
+    )(queries, grid, grad_attended, token_key_mask, token_valid)
+
+
 def local(latent, norm_shift, norm_scale, branch_gate, query_key_value, output_weight, tile_valid, cotangent):
     _, height, across, model_width = latent.shape
     tile_rows, tile_cols = height // TILE, across // TILE
@@ -131,40 +192,18 @@
     key_value = projections[:, model_width:].reshape(tile_rows, tile_cols, CELLS, 2 * model_width)
     grid = halo(key_value).reshape(grid_tiles * CELLS, 2 * model_width)
 
-    q_h = queries.reshape(tokens, heads, HEAD_DIM).transpose(1, 0, 2)
-    k_h = grid[:, :model_width].reshape(-1, heads, HEAD_DIM).transpose(1, 0, 2)
-    v_h = grid[:, model_width:].reshape(-1, heads, HEAD_DIM).transpose(1, 0, 2)
-
-    scale = 1.0 / math.sqrt(HEAD_DIM)
-    scores = jnp.einsum("hqe,hke->hqk", q_h, k_h, preferred_element_type=F32) * scale
-    unnormed = jnp.where(token_key_mask[None] > 0.0, jnp.exp(scores), 0.0)
-    denominator = jnp.sum(unnormed, axis=-1, keepdims=True) + (1.0 - token_valid)[None]
-    attention = (unnormed / denominator).astype(BF16)
-    attended_h = jnp.einsum("hqk,hke->hqe", attention, v_h, preferred_element_type=F32) * token_valid[None]
-    attended = attended_h.astype(BF16).transpose(1, 0, 2).reshape(tokens, model_width)
+    grad_projected = (incoming * branch_gate).astype(BF16)
+    grad_image = jnp.einsum("nf,df->nd", grad_projected, output_weight, preferred_element_type=F32)
+    grad_attended = (grad_image * token_valid).astype(BF16)
+    attended, grad_q, pair_grid = attention(queries, grid, grad_attended, token_key_mask, token_valid)
 
     projected = jnp.dot(attended, output_weight, preferred_element_type=F32)
     gate_term = jnp.sum(incoming * projected, axis=0)
-    grad_projected = (incoming * branch_gate).astype(BF16)
     output_term = jnp.einsum("nd,nf->df", attended, grad_projected, preferred_element_type=F32)
-    grad_image = jnp.einsum("nf,df->nd", grad_projected, output_weight, preferred_element_type=F32)
-    grad_attended = (grad_image * token_valid).astype(BF16)
-    ga_h = grad_attended.reshape(tokens, heads, HEAD_DIM).transpose(1, 0, 2)
-
-    grad_weights = jnp.einsum("hqe,hke->hqk", ga_h, v_h, preferred_element_type=F32)
-    attention_wide = attention.astype(F32)
-    row_inner = jnp.sum(attention_wide * grad_weights, axis=-1, keepdims=True)
-    grad_scores = (attention_wide * (grad_weights - row_inner) * scale).astype(BF16)
-    grad_q = jnp.einsum("hqk,hke->hqe", grad_scores, k_h, preferred_element_type=F32).astype(BF16)
-    grad_k = jnp.einsum("hqk,hqe->hke", grad_scores, q_h, preferred_element_type=F32)
-    grad_v = jnp.einsum("hqk,hqe->hke", attention, ga_h, preferred_element_type=F32)
-    grad_k = grad_k.transpose(1, 0, 2).reshape(tile_rows + 2, tile_cols + 2, CELLS, model_width)
-    grad_v = grad_v.transpose(1, 0, 2).reshape(tile_rows + 2, tile_cols + 2, CELLS, model_width)
-    pair_grid = jnp.concatenate([grad_k, grad_v], axis=-1)
+    pair_grid = pair_grid.reshape(tile_rows + 2, tile_cols + 2, CELLS, 2 * model_width)
     pair_grads = return_rims(pair_grid).reshape(tokens, 2 * model_width)
 
-    query_flat = grad_q.transpose(1, 0, 2).reshape(tokens, model_width)
-    grad_all = jnp.concatenate([query_flat, pair_grads.astype(BF16)], axis=-1)
+    grad_all = jnp.concatenate([grad_q, pair_grads.astype(BF16)], axis=-1)
     input_term = jnp.einsum("nd,nf->df", modulated, grad_all, preferred_element_type=F32)
     grad_modulated = jnp.einsum("nf,df->nd", grad_all, query_key_value, preferred_element_type=F32)
     shift_term = jnp.sum(grad_modulated, axis=0)

time: 287 us -> 247 us (0.86)
  local copies, waits for them, and re-layouts: 75.4 us -> 44.1 us
  matrix products: 39 us -> 11.1 us
  Pallas kernels: 0 us -> 12 us
  waiting for transfers between devices: 78.1 us -> 86.7 us
    dot_general x6 -> x0, matrix products: 27 us -> none  [the longest x1 8.11 us: local(): jnp.einsum('hqk,hqe->hke', grad_scores, q_h, preferred_element_type=F32)]
    reshape x5 -> x2, local copies, waits for them, and re-layouts: 24.5 us -> 3.29 us  [the longest x1 1.91 us: local(): jnp.repeat(jnp.repeat(key_mask, CELLS, axis=0), CELLS, axis=1)]
    pallas_call x0 -> x1, Pallas kernels: none -> 12 us  [attention(): pl.pallas_call(attention_kernel, out_shape=(jax.ShapeDtypeStruct((tokens,...]
    unnamed x43, local copies, waits for them, and re-layouts: 7.4 us -> 1.56 us
    ppermute x1, waiting for transfers between devices: 1.53 us -> 7.26 us  [return_rims(): lax.ppermute(grid[:, -1:].astype(BF16), 'col', forward_pairs(cols))]
    gt x2 -> x0, local copies, waits for them, and re-layouts: 3.05 us -> none  [local(): unnormed = jnp.where(token_key_mask[None] > 0.0, jnp.exp(scores), 0.0)]
  transfers between devices with their start and end apart: 17 -> 17, of which waited for: 9 -> 11; matrix products, arithmetic and copies ran while one was open for 22% -> 19% of each run, Pallas kernels for 0% -> 0%
where the time goes in v2:
time: 247 us; the launch traced here: 245 us
  waiting for transfers between devices  86.7 us (35%)
  local copies, waits for them, and re-layouts  44.1 us (18%)
  other arithmetic  40.2 us (16%)
  starting transfers between devices  36.5 us (15%)
  between operations  14.5 us (6%)
  Pallas kernels  12 us (5%)
  matrix products  11.1 us (4%)
    reduce_scatter x1, waiting for transfers between devices, reduce_weights(): lax.psum_scatter(combined.astype(BF16), 'dp', scatter_dimension=0, tiled=...  52.7 us
    ppermute x8, waiting for transfers between devices, exchange(): got, got_extra = lax.ppermute((send.astype(BF16), extra), axis, pairs)  17.5 us
    ppermute x8, starting transfers between devices, exchange(): got, got_extra = lax.ppermute((send.astype(BF16), extra), axis, pairs)  12.4 us
    pallas_call x1, Pallas kernels, attention(): pl.pallas_call(attention_kernel, out_shape=(jax.ShapeDtypeStruct((tokens,...  12 us
    ppermute x1, waiting for transfers between devices, return_rims(): lax.ppermute(grid[:, -1:].astype(BF16), 'col', forward_pairs(cols))  7.26 us
    another operation x2, other arithmetic  6.74 us
    convert_element_type x1, local copies, waits for them, and re-layouts, reduce_weights(): combined.astype(BF16)  6.64 us
    ppermute x1, starting transfers between devices, return_rims(): lax.ppermute(grid[:, -1:].astype(BF16), 'col', forward_pairs(cols))  5.42 us
  transfers between devices with their start and end apart: 17, of which 11 were waited for; matrix products, arithmetic and copies ran while one was open for 19% of the time, Pallas kernels for 0%

profile of v2, /device:TPU:4, one launch (start us, length us, event | category | flops | bytes accessed | tf_op | source)
XLA Modules:
  0.0 245.1 jit_solution(3710918932599306319)
XLA Ops:
  8.4 1.7 multiply_reduce_fusion.2
  10.8 1.7 bitcast_convert_fusion.1
  15.1 1.8 copy.50
  21.6 3.1 %collective-permute-start = (bf16[1,2,64,1536]{3,2,1,0:T(8,128)(2,1)}, bf16[1,2,64,1536]{3,2,1,0:T(8,128)(2,1)}, u32[]{:S(2)}, u32[]{:S(2)}) collective-permute-start(bf16[1,2,64,1536]{3,2,1,0:T(8,128)(2,1)} %bitcast.4), channel_id=1, source_target_pairs={{0,4},{4,8},{8,12},{1,5},{5,9},{9,13},{2,6},{6,10},{10,14},{3,7},{... | collective-permute-start | bytes 1179656 | tf_op jit(solution)/shard_map/ppermute | solution.py:43
  24.7 2.7 %collective-permute-start.1 = (bf16[1,2,64,1536]{3,2,1,0:T(8,128)(2,1)}, bf16[1,2,64,1536]{3,2,1,0:T(8,128)(2,1)}, u32[]{:S(2)}, u32[]{:S(2)}) collective-permute-start(bf16[1,2,64,1536]{3,2,1,0:T(8,128)(2,1)} %bitcast.4), channel_id=1, source_target_pairs={{4,0},{8,4},{12,8},{5,1},{9,5},{13,9},{6,2},{10,6},{14,10},{7,3},{... | collective-permute-start | bytes 1179656 | tf_op jit(solution)/shard_map/ppermute | solution.py:44
  32.7 1.7 bitcast_convert_fusion
  34.6 2.8 %collective-permute-done.1 = bf16[1,2,64,1536]{3,2,1,0:T(8,128)(2,1)} collective-permute-done((bf16[1,2,64,1536]{3,2,1,0:T(8,128)(2,1)}, bf16[1,2,64,1536]{3,2,1,0:T(8,128)(2,1)}, u32[]{:S(2)}, u32[]{:S(2)}) %collective-permute-start.1) | collective-permute-done | bytes 393248 | tf_op jit(solution)/shard_map/ppermute | solution.py:44
  39.9 4.3 %collective-permute-start.2 = (bf16[3,1,64,1536]{3,2,1,0:T(8,128)(2,1)}, bf16[3,1,64,1536]{3,2,1,0:T(8,128)(2,1)}, u32[]{:S(2)}, u32[]{:S(2)}) collective-permute-start(bf16[3,1,64,1536]{3,2,1,0:T(8,128)(2,1)} %get-tuple-element.23), channel_id=1, source_target_pairs={{0,1},{1,2},{2,3},{4,5},{5,6},{6,7},{8,9},{9,10},{10,11},{12,13},{... | collective-permute-start | bytes 1769480 | tf_op jit(solution)/shard_map/ppermute | solution.py:46
  48.2 1.5 broadcast_in_dim_reshape.12.valid_ref
  49.6 1.6 slice.100.q_ref
  51.2 1.8 copy.51
  55.7 1.4 reshape.156
  57.0 1.5 broadcast_in_dim.15
  58.5 1.9 copy.52.mask_ref
  61.5 1.9 fusion.1.ga_ref
  63.4 1.9 pad_maximum_fusion.1
  65.4 12.0 %shard_map.144 = (bf16[128,768]{1,0:T(8,128)(2,1)S(1)}, bf16[128,768]{1,0:T(8,128)(2,1)S(1)}, f32[768,1536]{1,0:T(8,128)}) custom-call(bf16[128,768]{1,0:T(8,128)(2,1)S(1)} %copy-done.5, bf16[768,1536]{1,0:T(8,128)(2,1)S(1)} %bitcast.145, bf16[128,768]{1,0:T(8,128)(2,1)S(1)} %fusion.1.ga_ref, f32[128,768]{1,0:T(8,128)S(1)} %copy-done.3, f32[128,1]{1,0:T(8,128)S(1)} %copy-done.6), custom_call_target="tpu_custom_call" | custom-call | flops 3019898880 | bytes 12582912 | tf_op jit(solution)/shard_map/pallas_call | solution.py:150
  77.4 2.8 %convert.28 = bf16[3,4,64,1536]{3,2,1,0:T(8,128)(2,1)S(1)} convert(f32[3,4,64,1536]{3,2,1,0:T(8,128)} %bitcast.147) | non-fusion elementwise | flops 1179648 | bytes 7077888 | tf_op jit(solution)/shard_map/convert.19
  81.4 5.4 %collective-permute-start.4 = (bf16[3,1,64,1536]{3,2,1,0:T(8,128)(2,1)}, bf16[3,1,64,1536]{3,2,1,0:T(8,128)(2,1)}, u32[]{:S(2)}, u32[]{:S(2)}) collective-permute-start(bf16[3,1,64,1536]{3,2,1,0:T(8,128)(2,1)} %get-tuple-element.19), channel_id=1, source_target_pairs={{0,1},{1,2},{2,3},{4,5},{5,6},{6,7},{8,9},{9,10},{10,11},{12,13},{... | collective-permute-start | bytes 1769480 | tf_op jit(solution)/shard_map/ppermute | solution.py:55
  88.1 1.8 copy.58
  89.8 7.3 %collective-permute-done.4 = bf16[3,1,64,1536]{3,2,1,0:T(8,128)(2,1)} collective-permute-done((bf16[3,1,64,1536]{3,2,1,0:T(8,128)(2,1)}, bf16[3,1,64,1536]{3,2,1,0:T(8,128)(2,1)}, u32[]{:S(2)}, u32[]{:S(2)}) %collective-permute-start.4) | collective-permute-done | bytes 589856 | tf_op jit(solution)/shard_map/ppermute | solution.py:55
  97.1 5.0 %collective-permute-done.5 = bf16[3,1,64,1536]{3,2,1,0:T(8,128)(2,1)} collective-permute-done((bf16[3,1,64,1536]{3,2,1,0:T(8,128)(2,1)}, bf16[3,1,64,1536]{3,2,1,0:T(8,128)(2,1)}, u32[]{:S(2)}, u32[]{:S(2)}) %collective-permute-start.5) | collective-permute-done | bytes 589856 | tf_op jit(solution)/shard_map/ppermute | solution.py:54
  102.1 4.0 %fusion.22 = (bf16[3,2,64,1536]{3,2,1,0:T(8,128)(2,1)S(1)}, f32[3,2,64,1536]{3,2,1,0:T(8,128)}) fusion(bf16[3,1,64,1536]{3,2,1,0:T(8,128)(2,1)} %collective-permute-done.5, bf16[3,1,64,1536]{3,2,1,0:T(8,128)(2,1)} %collective-permute-done.4, f32[3,4,64,1536]{3,2,1,0:T(8,128)} %bitcast.148), kind=kLoop, calls=%fused_computation.71 | loop fusion | flops 2949120 | bytes 7077888 | tf_op jit(solution)/shard_map/convert.17
  107.0 1.9 collective-permute-start.6
  109.0 4.1 %collective-permute-start.7 = (bf16[1,2,64,1536]{3,2,1,0:T(8,128)(2,1)}, bf16[1,2,64,1536]{3,2,1,0:T(8,128)(2,1)}, u32[]{:S(2)}, u32[]{:S(2)}) collective-permute-start(bf16[1,2,64,1536]{3,2,1,0:T(8,128)(2,1)} %get-tuple-element.22), channel_id=1, source_target_pairs={{4,0},{8,4},{12,8},{5,1},{9,5},{13,9},{6,2},{10,6},{14,10},{7,3},{... | collective-permute-start | bytes 1179656 | tf_op jit(solution)/shard_map/ppermute | solution.py:60
  114.0 1.7 copy.55
  115.7 2.5 %convolution_convert_fusion.2 = bf16[768,16,48]{0,2,1:T(8,128)(2,1)} fusion(bf16[16,48,128]{2,1,0:T(8,128)(2,1)} %bitcast.158, bf16[128,768]{1,0:T(8,128)(2,1)} %copy-done.1), kind=kOutput, calls=%fused_computation.6 | convolution fusion | flops 151584768 | bytes 1572864 | tf_op jit(solution)/shard_map/nd,nf->df/dot_general | solution.py:202
  119.4 2.3 fusion.3
  121.6 1.9 copy.56
  124.7 2.1 convolution_convert_fusion.1
  126.8 2.7 %pad_maximum_fusion = bf16[768,16,192]{0,2,1:T(8,128)(2,1)} fusion(bf16[768,16,48]{0,2,1:T(8,128)(2,1)S(1)} %copy-done.7, bf16[768,16,144]{0,2,1:T(8,128)(2,1)S(1)} %convolution_convert_fusion.1), kind=kLoop, calls=%fused_computation | loop fusion | flops 9437184 | bytes 9437184 | tf_op jit(solution)/shard_map/concatenate | solution.py:224
  129.5 6.6 %copy.59 = bf16[768,3072]{1,0:T(8,128)(2,1)} copy(bf16[768,3072]{0,1:T(8,128)(2,1)} %bitcast.146) | data formatting | bytes 9437184 | tf_op jit(solution)/shard_map/convert_element_type | solution.py:94
  136.8 2.8 %multiply_reduce_fusion = (f32[768]{0:T(1024)S(1)}, f32[128]{0:T(128)S(1)}, f32[128]{0:T(128)S(1)}, f32[768]{0:T(1024)S(1)}, f32[128,768]{1,0:T(8,128)S(1)}) fusion(f32[1,8,2,8,768]{4,3,1,2,0:T(8,128)} %copy.50, f32[128]{0:T(128)S(1)} %copy-done.20, f32[128]{0:T(128)S(1)} %copy-done.19, f32[768]{0:T(1024)S(1)} %copy-done.16, ...), kind=kOutput, calls=%fused_computation.31 | convolution fusion | flops 455047424 | bytes 4926464 | tf_op jit(solution)/shard_map/nf,df->nd/dot_general | solution.py:208
  141.5 4.0 %collective-permute-done.12 = f32[3,768]{1,0:T(4,128)} collective-permute-done((f32[3,768]{1,0:T(4,128)}, f32[3,768]{1,0:T(4,128)}, u32[]{:S(2)}, u32[]{:S(2)}) %collective-permute-start.12) | collective-permute-done | bytes 9248 | tf_op jit(solution)/shard_map/ppermute | solution.py:88
  146.8 2.7 %collective-permute-start.13 = (f32[3,768]{1,0:T(4,128)}, f32[3,768]{1,0:T(4,128)}, u32[]{:S(2)}, u32[]{:S(2)}) collective-permute-start(f32[3,768]{1,0:T(4,128)} %fusion.20), channel_id=1, source_target_pairs={{0,8},{4,12},{8,0},{12,4},{1,9},{5,13},{9,1},{13,5},{2,10},{6,14},... | collective-permute-start | bytes 27656 | tf_op jit(solution)/shard_map/ppermute | solution.py:88
  149.6 52.7 %reduce-scatter.2.cloned.1.call-done = bf16[48,3072]{1,0:T(8,128)(2,1)} async-done(((bf16[768,3072]{1,0:T(8,128)(2,1)}), bf16[48,3072]{1,0:T(8,128)(2,1)}) %reduce-scatter.2.cloned.1.call-update) | async-done | bytes 294928 | tf_op jit(solution)/shard_map/reduce_scatter | solution.py:94
  202.3 2.6 %reshape.164 = f32[48,2,2,2,2,192]{5,4,3,2,1,0:T(2,128)} reshape(bf16[48,3072]{1,0:T(8,128)(2,1)} %reduce-scatter.2.cloned.1.call-done) | data formatting | bytes 884736 | tf_op jit(solution)/shard_map/transpose | solution.py:97
  204.9 2.0 fusion.16
  208.8 1.6 collective-permute-start.14
  210.4 2.2 collective-permute-done.14
  212.6 3.1 %collective-permute-start.15 = (f32[3,768]{1,0:T(4,128)S(1)}, f32[3,768]{1,0:T(4,128)}, u32[]{:S(2)}, u32[]{:S(2)}) collective-permute-start(f32[3,768]{1,0:T(4,128)S(1)} %add.134), channel_id=1, source_target_pairs={{0,2},{1,3},{2,0},{3,1},{4,6},{5,7},{6,4},{7,5},{8,10},{9,11},{10,... | collective-permute-start | bytes 27656 | tf_op jit(solution)/shard_map/ppermute | solution.py:88
  215.7 1.6 copy.84
  217.3 1.6 copy.85
  219.7 1.5 fusion.6
  222.7 4.7 %collective-permute-done.9 = bf16[2,2,48,192]{3,1,0,2:T(2,128)(2,1)S(1)} collective-permute-done((bf16[2,2,48,192]{3,1,0,2:T(2,128)(2,1)S(1)}, bf16[2,2,48,192]{3,1,0,2:T(2,128)(2,1)S(1)}, u32[]{:S(2)}, u32[]{:S(2)}) %collective-permute-start.9) | collective-permute-done | bytes 73760 | tf_op jit(solution)/shard_map/ppermute | solution.py:88
  228.7 3.3 %collective-permute-done.10 = bf16[2,48,192]{2,0,1:T(2,128)(2,1)S(1)} collective-permute-done((bf16[2,48,192]{2,0,1:T(2,128)(2,1)S(1)}, bf16[2,48,192]{2,0,1:T(2,128)(2,1)S(1)}, u32[]{:S(2)}, u32[]{:S(2)}) %collective-permute-start.10) | collective-permute-done | bytes 36896 | tf_op jit(solution)/shard_map/ppermute | solution.py:88
  232.2 2.2 collective-permute-start.11
  234.4 3.2 %collective-permute-done.11 = bf16[48,192]{1,0:T(8,128)(2,1)S(1)} collective-permute-done((bf16[48,192]{1,0:T(8,128)(2,1)S(1)}, bf16[48,192]{1,0:T(8,128)(2,1)S(1)}, u32[]{:S(2)}, u32[]{:S(2)}) %collective-permute-start.11) | collective-permute-done | bytes 18464 | tf_op jit(solution)/shard_map/ppermute | solution.py:88
  (107 shorter events, 41.4 us)
Async XLA Ops:
  7.2 12.1 %copy-start = (bf16[768,2304]{1,0:T(8,128)(2,1)S(1)}, bf16[768,2304]{1,0:T(8,128)(2,1)}, u32[]{:S(2)}) copy-start(bf16[768,2304]{1,0:T(8,128)(2,1)} %param.13) | copy-start | bytes 10616836
  7.2 195.1 %reduce-scatter.2.cloned.1.call-start = ((), (), s32[]{:S(2)}) async-start(), calls=%async_computation.1 | async-start | bytes 5013504 | tf_op jit(solution)/shard_map/reduce_scatter | solution.py:94
  20.0 0.8 copy-start.12
  21.6 13.1 %collective-permute-start = (bf16[1,2,64,1536]{3,2,1,0:T(8,128)(2,1)}, bf16[1,2,64,1536]{3,2,1,0:T(8,128)(2,1)}, u32[]{:S(2)}, u32[]{:S(2)}) collective-permute-start(bf16[1,2,64,1536]{3,2,1,0:T(8,128)(2,1)} %bitcast.4), channel_id=1, source_target_pairs={{0,4},{4,8},{8,12},{1,5},{5,9},{9,13},{2,6},{6,10},{10,14},{3,7},{... | collective-permute-start | bytes 1179656 | tf_op jit(solution)/shard_map/ppermute | solution.py:43
  24.7 12.8 %collective-permute-start.1 = (bf16[1,2,64,1536]{3,2,1,0:T(8,128)(2,1)}, bf16[1,2,64,1536]{3,2,1,0:T(8,128)(2,1)}, u32[]{:S(2)}, u32[]{:S(2)}) collective-permute-start(bf16[1,2,64,1536]{3,2,1,0:T(8,128)(2,1)} %bitcast.4), channel_id=1, source_target_pairs={{4,0},{8,4},{12,8},{5,1},{9,5},{13,9},{6,2},{10,6},{14,10},{7,3},{... | collective-permute-start | bytes 1179656 | tf_op jit(solution)/shard_map/ppermute | solution.py:44
  39.9 23.5 %collective-permute-start.2 = (bf16[3,1,64,1536]{3,2,1,0:T(8,128)(2,1)}, bf16[3,1,64,1536]{3,2,1,0:T(8,128)(2,1)}, u32[]{:S(2)}, u32[]{:S(2)}) collective-permute-start(bf16[3,1,64,1536]{3,2,1,0:T(8,128)(2,1)} %get-tuple-element.23), channel_id=1, source_target_pairs={{0,1},{1,2},{2,3},{4,5},{5,6},{6,7},{8,9},{9,10},{10,11},{12,13},{... | collective-permute-start | bytes 1769480 | tf_op jit(solution)/shard_map/ppermute | solution.py:46
  44.2 19.2 %collective-permute-start.3 = (bf16[3,1,64,1536]{3,2,1,0:T(8,128)(2,1)}, bf16[3,1,64,1536]{3,2,1,0:T(8,128)(2,1)}, u32[]{:S(2)}, u32[]{:S(2)}) collective-permute-start(bf16[3,1,64,1536]{3,2,1,0:T(8,128)(2,1)} %get-tuple-element.24), channel_id=1, source_target_pairs={{1,0},{2,1},{3,2},{5,4},{6,5},{7,6},{9,8},{10,9},{11,10},{13,12},{... | collective-permute-start | bytes 1769480 | tf_op jit(solution)/shard_map/ppermute | solution.py:47
  61.5 3.9 %copy-start.13 = (bf16[128,768]{1,0:T(8,128)(2,1)}, bf16[128,768]{1,0:T(8,128)(2,1)S(1)}, u32[]{:S(2)}) copy-start(bf16[128,768]{1,0:T(8,128)(2,1)S(1)} %fusion.7) | copy-start | bytes 589828
  63.4 2.0 copy-start.3
  63.4 2.0 copy-start.5
  63.4 2.0 copy-start.6
  77.4 2.8 %copy-start.1 = (bf16[128,768]{1,0:T(8,128)(2,1)}, bf16[128,768]{1,0:T(8,128)(2,1)S(1)}, u32[]{:S(2)}) copy-start(bf16[128,768]{1,0:T(8,128)(2,1)S(1)} %get-tuple-element.10) | copy-start | bytes 589828
  77.4 2.8 %copy-start.4 = (bf16[128,768]{1,0:T(8,128)(2,1)}, bf16[128,768]{1,0:T(8,128)(2,1)S(1)}, u32[]{:S(2)}) copy-start(bf16[128,768]{1,0:T(8,128)(2,1)S(1)} %get-tuple-element.11) | copy-start | bytes 589828
  81.4 15.7 %collective-permute-start.4 = (bf16[3,1,64,1536]{3,2,1,0:T(8,128)(2,1)}, bf16[3,1,64,1536]{3,2,1,0:T(8,128)(2,1)}, u32[]{:S(2)}, u32[]{:S(2)}) collective-permute-start(bf16[3,1,64,1536]{3,2,1,0:T(8,128)(2,1)} %get-tuple-element.19), channel_id=1, source_target_pairs={{0,1},{1,2},{2,3},{4,5},{5,6},{6,7},{8,9},{9,10},{10,11},{12,13},{... | collective-permute-start | bytes 1769480 | tf_op jit(solution)/shard_map/ppermute | solution.py:55
  86.8 15.3 %collective-permute-start.5 = (bf16[3,1,64,1536]{3,2,1,0:T(8,128)(2,1)}, bf16[3,1,64,1536]{3,2,1,0:T(8,128)(2,1)}, u32[]{:S(2)}, u32[]{:S(2)}) collective-permute-start(bf16[3,1,64,1536]{3,2,1,0:T(8,128)(2,1)} %get-tuple-element.20), channel_id=1, source_target_pairs={{1,0},{2,1},{3,2},{5,4},{6,5},{7,6},{9,8},{10,9},{11,10},{13,12},{... | collective-permute-start | bytes 1769480 | tf_op jit(solution)/shard_map/ppermute | solution.py:54
  89.8 23.2 %copy-start.11 = (bf16[1,8,16,768]{3,2,1,0:T(8,128)(2,1)S(1)}, bf16[1,8,16,768]{3,2,1,0:T(8,128)(2,1)}, u32[]{:S(2)}) copy-start(bf16[1,8,16,768]{3,2,1,0:T(8,128)(2,1)} %param.9) | copy-start | bytes 589828
  89.8 23.2 %copy-start.15 = (f32[768]{0:T(1024)S(1)}, f32[768]{0:T(1024)}, u32[]{:S(2)}) copy-start(f32[768]{0:T(1024)} %add_reduce_fusion) | copy-start | bytes 9220
  89.8 23.3 %copy-start.17 = (f32[768]{0:T(1024)S(1)}, f32[768]{0:T(1024)}, u32[]{:S(2)}) copy-start(f32[768]{0:T(1024)} %reduce.4) | copy-start | bytes 9220
  107.0 11.2 %collective-permute-start.6 = (bf16[1,2,64,1536]{3,2,1,0:T(8,128)(2,1)}, bf16[1,2,64,1536]{3,2,1,0:T(8,128)(2,1)}, u32[]{:S(2)}, u32[]{:S(2)}) collective-permute-start(bf16[1,2,64,1536]{3,2,1,0:T(8,128)(2,1)} %get-tuple-element.21), channel_id=1, source_target_pairs={{0,4},{4,8},{8,12},{1,5},{5,9},{9,13},{2,6},{6,10},{10,14},{3,7},{... | collective-permute-start | bytes 1179656 | tf_op jit(solution)/shard_map/ppermute | solution.py:61
  109.0 10.4 %collective-permute-start.7 = (bf16[1,2,64,1536]{3,2,1,0:T(8,128)(2,1)}, bf16[1,2,64,1536]{3,2,1,0:T(8,128)(2,1)}, u32[]{:S(2)}, u32[]{:S(2)}) collective-permute-start(bf16[1,2,64,1536]{3,2,1,0:T(8,128)(2,1)} %get-tuple-element.22), channel_id=1, source_target_pairs={{4,0},{8,4},{12,8},{5,1},{9,5},{13,9},{6,2},{10,6},{14,10},{7,3},{... | collective-permute-start | bytes 1179656 | tf_op jit(solution)/shard_map/ppermute | solution.py:60
  124.7 2.1 copy-start.7
  136.1 0.7 copy-start.16
  136.1 0.7 copy-start.19
  136.1 0.7 copy-start.20
  136.8 2.9 %copy-start.2 = (bf16[128,768]{1,0:T(8,128)(2,1)S(1)}, bf16[128,768]{1,0:T(8,128)(2,1)}, u32[]{:S(2)}) copy-start(bf16[128,768]{1,0:T(8,128)(2,1)} %copy-done.1) | copy-start | bytes 589828
  136.8 2.9 %copy-start.8 = (bf16[768,768]{1,0:T(8,128)(2,1)S(1)}, bf16[768,768]{1,0:T(8,128)(2,1)}, u32[]{:S(2)}) copy-start(bf16[768,768]{1,0:T(8,128)(2,1)} %param.14) | copy-start | bytes 3538948
  136.8 2.9 %copy-start.9 = (f32[1,8,2,8,768]{4,3,1,2,0:T(8,128)S(1)}, f32[1,8,2,8,768]{4,3,1,2,0:T(8,128)}, u32[]{:S(2)}) copy-start(f32[1,8,2,8,768]{4,3,1,2,0:T(8,128)} %copy.50) | copy-start | bytes 1179652
  136.8 2.9 %copy-start.10 = (f32[1,8,2,8,768]{4,3,1,2,0:T(8,128)S(1)}, f32[1,8,2,8,768]{4,3,1,2,0:T(8,128)}, u32[]{:S(2)}) copy-start(f32[1,8,2,8,768]{4,3,1,2,0:T(8,128)} %copy.51) | copy-start | bytes 1179652
  136.8 2.9 %copy-start.18 = (f32[768]{0:T(1024)S(1)}, f32[768]{0:T(1024)}, u32[]{:S(2)}) copy-start(f32[768]{0:T(1024)} %reduce.2) | copy-start | bytes 9220
  141.5 4.0 %collective-permute-start.12 = (f32[3,768]{1,0:T(4,128)}, f32[3,768]{1,0:T(4,128)}, u32[]{:S(2)}, u32[]{:S(2)}) collective-permute-start(f32[3,768]{1,0:T(4,128)} %pad_maximum_fusion.4), channel_id=1, source_target_pairs={{0,4},{4,0},{8,12},{12,8},{1,5},{5,1},{9,13},{13,9},{2,6},{6,2},{1... | collective-permute-start | bytes 27656 | tf_op jit(solution)/shard_map/ppermute | solution.py:88
  146.8 61.3 %collective-permute-start.13 = (f32[3,768]{1,0:T(4,128)}, f32[3,768]{1,0:T(4,128)}, u32[]{:S(2)}, u32[]{:S(2)}) collective-permute-start(f32[3,768]{1,0:T(4,128)} %fusion.20), channel_id=1, source_target_pairs={{0,8},{4,12},{8,0},{12,4},{1,9},{5,13},{9,1},{13,5},{2,10},{6,14},... | collective-permute-start | bytes 27656 | tf_op jit(solution)/shard_map/ppermute | solution.py:88
  206.9 12.8 %collective-permute-start.8 = (bf16[2,2,2,48,192]{4,2,1,0,3:T(2,128)(2,1)}, bf16[2,2,2,48,192]{4,2,1,0,3:T(2,128)(2,1)}, u32[]{:S(2)}, u32[]{:S(2)}) collective-permute-start(bf16[2,2,2,48,192]{4,2,1,0,3:T(2,128)(2,1)} %fusion.16), channel_id=1, source_target_pairs={{0,4},{4,0},{8,12},{12,8},{1,5},{5,1},{9,13},{13,9},{2,6},{6,2},{1... | collective-permute-start | bytes 442376 | tf_op jit(solution)/shard_map/ppermute | solution.py:88
  208.8 3.8 %collective-permute-start.14 = (f32[3,768]{1,0:T(4,128)S(1)}, f32[3,768]{1,0:T(4,128)S(1)}, u32[]{:S(2)}, u32[]{:S(2)}) collective-permute-start(f32[3,768]{1,0:T(4,128)S(1)} %fusion.38), channel_id=1, source_target_pairs={{0,1},{1,0},{2,3},{3,2},{4,5},{5,4},{6,7},{7,6},{8,9},{9,8},{10,11... | collective-permute-start | bytes 27656 | tf_op jit(solution)/shard_map/ppermute | solution.py:88
  212.6 6.3 %collective-permute-start.15 = (f32[3,768]{1,0:T(4,128)S(1)}, f32[3,768]{1,0:T(4,128)}, u32[]{:S(2)}, u32[]{:S(2)}) collective-permute-start(f32[3,768]{1,0:T(4,128)S(1)} %add.134), channel_id=1, source_target_pairs={{0,2},{1,3},{2,0},{3,1},{4,6},{5,7},{6,4},{7,5},{8,10},{9,11},{10,... | collective-permute-start | bytes 27656 | tf_op jit(solution)/shard_map/ppermute | solution.py:88
  221.3 6.2 %collective-permute-start.9 = (bf16[2,2,48,192]{3,1,0,2:T(2,128)(2,1)S(1)}, bf16[2,2,48,192]{3,1,0,2:T(2,128)(2,1)S(1)}, u32[]{:S(2)}, u32[]{:S(2)}) collective-permute-start(bf16[2,2,48,192]{3,1,0,2:T(2,128)(2,1)S(1)} %fusion.18), channel_id=1, source_target_pairs={{0,8},{4,12},{8,0},{12,4},{1,9},{5,13},{9,1},{13,5},{2,10},{6,14},... | collective-permute-start | bytes 221192 | tf_op jit(solution)/shard_map/ppermute | solution.py:88
  227.8 4.2 %collective-permute-start.10 = (bf16[2,48,192]{2,0,1:T(2,128)(2,1)S(1)}, bf16[2,48,192]{2,0,1:T(2,128)(2,1)S(1)}, u32[]{:S(2)}, u32[]{:S(2)}) collective-permute-start(bf16[2,48,192]{2,0,1:T(2,128)(2,1)S(1)} %copy.69), channel_id=1, source_target_pairs={{0,1},{1,0},{2,3},{3,2},{4,5},{5,4},{6,7},{7,6},{8,9},{9,8},{10,11... | collective-permute-start | bytes 110600 | tf_op jit(solution)/shard_map/ppermute | solution.py:88
  232.2 5.4 %collective-permute-start.11 = (bf16[48,192]{1,0:T(8,128)(2,1)S(1)}, bf16[48,192]{1,0:T(8,128)(2,1)S(1)}, u32[]{:S(2)}, u32[]{:S(2)}) collective-permute-start(bf16[48,192]{1,0:T(8,128)(2,1)S(1)} %bitcast.163), channel_id=1, source_target_pairs={{0,2},{1,3},{2,0},{3,1},{4,6},{5,7},{6,4},{7,5},{8,10},{9,11},{10,... | collective-permute-start | bytes 55304 | tf_op jit(solution)/shard_map/ppermute | solution.py:88
  237.6 0.7 copy-start.14
Sparse Core Ops, SparseCore 0:
  136.2 65.9 reduce-scatter.1

commit v3 on v2

--- a/solution.py
+++ b/solution.py
@@ -38,31 +38,62 @@
     return [(i + 1, i) for i in range(count - 1)]
 
 
+def shifts(rows, cols, step_row, step_col):
+    pairs = []
+    for r in range(rows):
+        for c in range(cols):
+            r2, c2 = r + step_row, c + step_col
+            if 0 <= r2 < rows and 0 <= c2 < cols:
+                pairs.append((r * cols + c, r2 * cols + c2))
+    return pairs
+
+
+def send(block, step_row, step_col):
+    rows, cols = lax.axis_size("row"), lax.axis_size("col")
+    return lax.ppermute(block, ("row", "col"), shifts(rows, cols, step_row, step_col))
+
+
 def halo(grid):
-    rows, cols = lax.axis_size("row"), lax.axis_size("col")
-    from_above = lax.ppermute(grid[-1:], "row", forward_pairs(rows))
-    from_below = lax.ppermute(grid[:1], "row", backward_pairs(rows))
-    grid = jnp.concatenate([from_above, grid, from_below], axis=0)
-    from_left = lax.ppermute(grid[:, -1:], "col", forward_pairs(cols))
-    from_right = lax.ppermute(grid[:, :1], "col", backward_pairs(cols))
-    return jnp.concatenate([from_left, grid, from_right], axis=1)
+    top = send(grid[-1:], 1, 0)
+    bottom = send(grid[:1], -1, 0)
+    left = send(grid[:, -1:], 0, 1)
+    right = send(grid[:, :1], 0, -1)
+    top_left = send(grid[-1:, -1:], 1, 1)
+    top_right = send(grid[-1:, :1], 1, -1)
+    bottom_left = send(grid[:1, -1:], -1, 1)
+    bottom_right = send(grid[:1, :1], -1, -1)
+    upper = jnp.concatenate([top_left, top, top_right], axis=1)
+    middle = jnp.concatenate([left, grid, right], axis=1)
+    lower = jnp.concatenate([bottom_left, bottom, bottom_right], axis=1)
+    return jnp.concatenate([upper, middle, lower], axis=0)
+
+
+def place(block, tile_rows, tile_cols, at_row, at_col):
+    def side(at, count):
+        if at is None:
+            return (0, 0)
+        return (0, count - 1) if at == 0 else (count - 1, 0)
+
+    rest = [(0, 0)] * (block.ndim - 2)
+    return jnp.pad(block.astype(F32), [side(at_row, tile_rows), side(at_col, tile_cols)] + rest)
 
 
 def return_rims(grid):
-    rows, cols = lax.axis_size("row"), lax.axis_size("col")
     tile_rows, tile_cols = grid.shape[0] - 2, grid.shape[1] - 2
-    from_right = lax.ppermute(grid[:, :1].astype(BF16), "col", backward_pairs(cols))
-    from_left = lax.ppermute(grid[:, -1:].astype(BF16), "col", forward_pairs(cols))
-    middle = grid[:, 1:-1]
-    pad_c = ((0, 0), (0, tile_cols - 1), (0, 0), (0, 0))
-    middle = middle + jnp.pad(from_left.astype(F32), pad_c)
-    middle = middle + jnp.pad(from_right.astype(F32), (pad_c[0], pad_c[1][::-1], pad_c[2], pad_c[3]))
-    from_below = lax.ppermute(middle[:1].astype(BF16), "row", backward_pairs(rows))
-    from_above = lax.ppermute(middle[-1:].astype(BF16), "row", forward_pairs(rows))
-    inner = middle[1:-1]
-    pad_r = ((0, tile_rows - 1), (0, 0), (0, 0), (0, 0))
-    inner = inner + jnp.pad(from_above.astype(F32), pad_r)
-    inner = inner + jnp.pad(from_below.astype(F32), (pad_r[0][::-1], pad_r[1], pad_r[2], pad_r[3]))
+    inner = grid[1:-1, 1:-1]
+    parts = [
+        (grid[:1, 1:-1], -1, 0, -1, None),
+        (grid[-1:, 1:-1], 1, 0, 0, None),
+        (grid[1:-1, :1], 0, -1, None, -1),
+        (grid[1:-1, -1:], 0, 1, None, 0),
+        (grid[:1, :1], -1, -1, -1, -1),
+        (grid[:1, -1:], -1, 1, -1, 0),
+        (grid[-1:, :1], 1, -1, 0, -1),
+        (grid[-1:, -1:], 1, 1, 0, 0),
+    ]
+    received = [(send(block.astype(BF16), dr, dc), at_row, at_col) for block, dr, dc, at_row, at_col in parts]
+    for block, at_row, at_col in received:
+        inner = inner + place(block, tile_rows, tile_cols, at_row, at_col)
     return inner
 
 
@@ -83,15 +114,16 @@
     low = lax.index_in_dim(value, 0, split_axis, keepdims=False)
     high = lax.index_in_dim(value, 1, split_axis, keepdims=False)
     keep = jnp.where(mine == 1, high, low)
-    send = jnp.where(mine == 1, low, high)
+    away = jnp.where(mine == 1, low, high)
     pairs = [(i, i ^ xor) for i in range(count)]
-    got, got_extra = lax.ppermute((send.astype(BF16), extra), axis, pairs)
+    if extra is None:
+        return keep + lax.ppermute(away.astype(BF16), axis, pairs).astype(F32), None
+    got, got_extra = lax.ppermute((away.astype(BF16), extra), axis, pairs)
     return keep + got.astype(F32), extra + got_extra
 
 
-def reduce_weights(combined, extra):
-    model_width = combined.shape[0]
-    part = lax.psum_scatter(combined.astype(BF16), "dp", scatter_dimension=0, tiled=True).astype(F32)
+def reduce_weights(term, extra):
+    part = lax.psum_scatter(term.astype(BF16), "dp", scatter_dimension=0, tiled=True).astype(F32)
     rows, cols = lax.axis_size("row"), lax.axis_size("col")
     rest = part.shape[0]
     value = part.reshape(rest, rows // 2, 2, cols // 2, 2, -1).transpose(1, 2, 3, 4, 0, 5)
@@ -218,19 +250,8 @@
     mixed = (values + branch_gate * projected).astype(BF16)
     latent_grad = (incoming + latent_term).astype(BF16)
 
-    blocks = lax.axis_size("row") * lax.axis_size("col")
-    width_in = input_term.shape[1] // blocks
-    width_out = output_term.shape[1] // blocks
-    combined = jnp.concatenate(
-        [
-            input_term.reshape(model_width, blocks, width_in),
-            output_term.reshape(model_width, blocks, width_out),
-        ],
-        axis=-1,
-    ).reshape(model_width, blocks * (width_in + width_out))
-    reduced, sums = reduce_weights(combined, jnp.stack([shift_term, scale_term, gate_term]))
-    input_grad = reduced[:, :width_in]
-    output_grad = reduced[:, width_in:]
+    output_grad, _ = reduce_weights(output_term, None)
+    input_grad, sums = reduce_weights(input_term, jnp.stack([shift_term, scale_term, gate_term]))
 
     return (
         from_tiles(mixed, height, across)[None],

time: 247 us -> 243 us (0.984)
  starting transfers between devices: 36.5 us -> 68.9 us
  other arithmetic: 40.2 us -> 24 us
  local copies, waits for them, and re-layouts: 44.1 us -> 29.6 us
  waiting for transfers between devices: 86.7 us -> 81.8 us
    ppermute x16 -> x28, starting transfers between devices: 36.5 us -> 68.9 us  [the longest x16 48.4 us: send(): lax.ppermute(block, ('row', 'col'), shifts(rows, cols, step_row, step_col))]
    convert_element_type x4 -> x0, local copies, waits for them, and re-layouts: 8.63 us -> none  [the longest x1 6.64 us: reduce_weights(): combined.astype(BF16)]
    reduce_scatter x1 -> x2, waiting for transfers between devices: 52.7 us -> 46.8 us  [reduce_weights(): lax.psum_scatter(term.astype(BF16), 'dp', scatter_dimension=0, tiled=True)]
    transpose x1 -> x4, local copies, waits for them, and re-layouts: 2.61 us -> 8.2 us  [reduce_weights(): part.reshape(rest, rows // 2, 2, cols // 2, 2, -1)]
    concatenate x4 -> x1, other arithmetic: 7.01 us -> 1.7 us  [halo(): return jnp.concatenate([upper, middle, lower], axis=0)]
    another operation x2 -> x1, other arithmetic: 6.74 us -> 2.63 us
    ppermute x16 -> x28, waiting for transfers between devices: 33.9 us -> 35 us  [the longest x8 16.8 us: exchange(): got, got_extra = lax.ppermute((away.astype(BF16), extra), axis, pairs)]
  transfers between devices with their start and end apart: 17 -> 30, of which waited for: 11 -> 12; matrix products, arithmetic and copies ran while one was open for 19% -> 16% of each run, Pallas kernels for 0% -> 0%
where the time goes in v3:
time: 243 us; the launch traced here: 242 us
  waiting for transfers between devices  81.8 us (34%)
  starting transfers between devices  68.9 us (28%)
  local copies, waits for them, and re-layouts  29.6 us (12%)
  other arithmetic  24 us (10%)
  between operations  14.7 us (6%)
  Pallas kernels  12.1 us (5%)
  matrix products  10.8 us (4%)
    ppermute x16, starting transfers between devices, send(): lax.ppermute(block, ('row', 'col'), shifts(rows, cols, step_row, step_col))  48.4 us
    reduce_scatter x2, waiting for transfers between devices, reduce_weights(): lax.psum_scatter(term.astype(BF16), 'dp', scatter_dimension=0, tiled=True)  46.8 us
    ppermute x8, waiting for transfers between devices, exchange(): got, got_extra = lax.ppermute((away.astype(BF16), extra), axis, pairs)  16.8 us
    ppermute x16, waiting for transfers between devices, send(): lax.ppermute(block, ('row', 'col'), shifts(rows, cols, step_row, step_col))  14.1 us
    ppermute x8, starting transfers between devices, exchange(): got, got_extra = lax.ppermute((away.astype(BF16), extra), axis, pairs)  13.7 us
    pallas_call x1, Pallas kernels, attention(): pl.pallas_call(attention_kernel, out_shape=(jax.ShapeDtypeStruct((tokens,...  12.1 us
    transpose x4, local copies, waits for them, and re-layouts, reduce_weights(): part.reshape(rest, rows // 2, 2, cols // 2, 2, -1)  8.2 us
    ppermute x4, starting transfers between devices, exchange(): lax.ppermute(away.astype(BF16), axis, pairs).astype(F32)  6.79 us
  transfers between devices with their start and end apart: 30, of which 12 were waited for; matrix products, arithmetic and copies ran while one was open for 16% of the time, Pallas kernels for 0%

profile of v3, /device:TPU:4, one launch (start us, length us, event | category | flops | bytes accessed | tf_op | source)
XLA Modules:
  0.0 241.9 jit_solution(6346679347468295014)
XLA Ops:
  9.6 1.7 bitcast_convert_fusion.1
  12.7 1.8 copy.23
  17.9 1.8 fusion.30
  19.7 4.1 %collective-permute-start.5 = (bf16[1,1,64,1536]{3,2,1,0:T(8,128)(2,1)}, bf16[1,1,64,1536]{3,2,1,0:T(8,128)(2,1)}, u32[]{:S(2)}, u32[]{:S(2)}) collective-permute-start(bf16[1,1,64,1536]{3,2,1,0:T(8,128)(2,1)} %get-tuple-element.28), channel_id=1, source_target_pairs={{4,1},{5,2},{6,3},{8,5},{9,6},{10,7},{12,9},{13,10},{14,11},{20,17... | collective-permute-start | bytes 589832 | tf_op jit(solution)/shard_map/ppermute | solution.py:53
  23.9 3.5 %collective-permute-start.3 = (bf16[1,1,64,1536]{3,2,1,0:T(8,128)(2,1)}, bf16[1,1,64,1536]{3,2,1,0:T(8,128)(2,1)}, u32[]{:S(2)}, u32[]{:S(2)}) collective-permute-start(bf16[1,1,64,1536]{3,2,1,0:T(8,128)(2,1)} %get-tuple-element.28), channel_id=1, source_target_pairs={{0,1},{1,2},{2,3},{4,5},{5,6},{6,7},{8,9},{9,10},{10,11},{12,13},{... | collective-permute-start | bytes 589832 | tf_op jit(solution)/shard_map/ppermute | solution.py:53
  27.4 4.8 %collective-permute-start = (bf16[1,1,64,1536]{3,2,1,0:T(8,128)(2,1)}, bf16[1,1,64,1536]{3,2,1,0:T(8,128)(2,1)}, u32[]{:S(2)}, u32[]{:S(2)}) collective-permute-start(bf16[1,1,64,1536]{3,2,1,0:T(8,128)(2,1)} %get-tuple-element.28), channel_id=1, source_target_pairs={{0,5},{1,6},{2,7},{4,9},{5,10},{6,11},{8,13},{9,14},{10,15},{16,21... | collective-permute-start | bytes 589832 | tf_op jit(solution)/shard_map/ppermute | solution.py:53
  32.1 1.9 collective-permute-start.6
  34.1 4.6 %collective-permute-start.1 = (bf16[1,2,64,1536]{3,2,1,0:T(8,128)(2,1)}, bf16[1,2,64,1536]{3,2,1,0:T(8,128)(2,1)}, u32[]{:S(2)}, u32[]{:S(2)}) collective-permute-start(bf16[1,2,64,1536]{3,2,1,0:T(8,128)(2,1)} %bitcast.4), channel_id=1, source_target_pairs={{0,4},{1,5},{2,6},{3,7},{4,8},{5,9},{6,10},{7,11},{8,12},{9,13},{1... | collective-permute-start | bytes 1179656 | tf_op jit(solution)/shard_map/ppermute | solution.py:53
  42.2 1.6 slice.144.q_ref
  46.6 1.5 broadcast_in_dim.15
  48.1 1.9 copy.25.mask_ref
  55.0 1.8 fusion.ga_ref
  56.8 4.9 %collective-permute-done.7 = bf16[1,1,64,1536]{3,2,1,0:T(8,128)(2,1)S(1)} collective-permute-done((bf16[1,1,64,1536]{3,2,1,0:T(8,128)(2,1)}, bf16[1,1,64,1536]{3,2,1,0:T(8,128)(2,1)S(1)}, u32[]{:S(2)}, u32[]{:S(2)}) %collective-permute-start.7) | collective-permute-done | bytes 196640 | tf_op jit(solution)/shard_map/ppermute | solution.py:53
  61.7 6.0 %collective-permute-done.4 = bf16[1,1,64,1536]{3,2,1,0:T(8,128)(2,1)S(1)} collective-permute-done((bf16[1,1,64,1536]{3,2,1,0:T(8,128)(2,1)}, bf16[1,1,64,1536]{3,2,1,0:T(8,128)(2,1)S(1)}, u32[]{:S(2)}, u32[]{:S(2)}) %collective-permute-start.4) | collective-permute-done | bytes 196640 | tf_op jit(solution)/shard_map/ppermute | solution.py:53
  67.7 1.7 maximum_maximum_fusion
  69.4 12.1 %shard_map.144 = (bf16[128,768]{1,0:T(8,128)(2,1)S(1)}, bf16[128,768]{1,0:T(8,128)(2,1)S(1)}, f32[768,1536]{1,0:T(8,128)}) custom-call(bf16[128,768]{1,0:T(8,128)(2,1)S(1)} %copy-done.4, bf16[768,1536]{1,0:T(8,128)(2,1)S(1)} %bitcast.114, bf16[128,768]{1,0:T(8,128)(2,1)S(1)} %fusion.ga_ref, f32[128,768]{1,0:T(8,128)S(1)} %copy-done.3, f32[128,1]{1,0:T(8,128)S(1)} %copy-done.7), custom_call_target="tpu_custom_call" | custom-call | flops 3019898880 | bytes 12582912 | tf_op jit(solution)/shard_map/pallas_call | solution.py:182
  82.9 1.5 convolution_convert_fusion.2
  84.5 2.6 %convert.34 = bf16[3,4,64,1536]{3,2,1,0:T(8,128)(2,1)S(1)} convert(f32[3,4,64,1536]{3,2,1,0:T(8,128)} %bitcast.115) | non-fusion elementwise | flops 1179648 | bytes 7077888 | tf_op jit(solution)/shard_map/convert.31
  88.5 2.9 %collective-permute-start.15 = (bf16[1,1,64,1536]{3,2,1,0:T(8,128)(2,1)S(1)}, bf16[1,1,64,1536]{3,2,1,0:T(8,128)(2,1)S(1)}, u32[]{:S(2)}, u32[]{:S(2)}) collective-permute-start(bf16[1,1,64,1536]{3,2,1,0:T(8,128)(2,1)S(1)} %get-tuple-element.18), channel_id=1, source_target_pairs={{0,5},{1,6},{2,7},{4,9},{5,10},{6,11},{8,13},{9,14},{10,15},{16,21... | collective-permute-start | bytes 589832 | tf_op jit(solution)/shard_map/ppermute | solution.py:53
  92.8 5.4 %collective-permute-start.8 = (bf16[1,2,64,1536]{3,2,1,0:T(8,128)(2,1)S(1)}, bf16[1,2,64,1536]{3,2,1,0:T(8,128)(2,1)S(1)}, u32[]{:S(2)}, u32[]{:S(2)}) collective-permute-start(bf16[1,2,64,1536]{3,2,1,0:T(8,128)(2,1)S(1)} %get-tuple-element.23), channel_id=1, source_target_pairs={{4,0},{5,1},{6,2},{7,3},{8,4},{9,5},{10,6},{11,7},{12,8},{13,9},{1... | collective-permute-start | bytes 1179656 | tf_op jit(solution)/shard_map/ppermute | solution.py:53
  98.1 1.9 collective-permute-start.9
  100.1 5.5 %collective-permute-start.13 = (bf16[1,1,64,1536]{3,2,1,0:T(8,128)(2,1)S(1)}, bf16[1,1,64,1536]{3,2,1,0:T(8,128)(2,1)S(1)}, u32[]{:S(2)}, u32[]{:S(2)}) collective-permute-start(bf16[1,1,64,1536]{3,2,1,0:T(8,128)(2,1)S(1)} %get-tuple-element.20), channel_id=1, source_target_pairs={{4,1},{5,2},{6,3},{8,5},{9,6},{10,7},{12,9},{13,10},{14,11},{20,17... | collective-permute-start | bytes 589832 | tf_op jit(solution)/shard_map/ppermute | solution.py:53
  106.9 6.0 %collective-permute-start.11 = (bf16[1,1,64,1536]{3,2,1,0:T(8,128)(2,1)S(1)}, bf16[1,1,64,1536]{3,2,1,0:T(8,128)(2,1)S(1)}, u32[]{:S(2)}, u32[]{:S(2)}) collective-permute-start(bf16[1,1,64,1536]{3,2,1,0:T(8,128)(2,1)S(1)} %get-tuple-element.22), channel_id=1, source_target_pairs={{0,1},{1,2},{2,3},{4,5},{5,6},{6,7},{8,9},{9,10},{10,11},{12,13},{... | collective-permute-start | bytes 589832 | tf_op jit(solution)/shard_map/ppermute | solution.py:53
  112.9 2.5 %collective-permute-done.12 = bf16[1,1,64,1536]{3,2,1,0:T(8,128)(2,1)S(1)} collective-permute-done((bf16[1,1,64,1536]{3,2,1,0:T(8,128)(2,1)S(1)}, bf16[1,1,64,1536]{3,2,1,0:T(8,128)(2,1)S(1)}, u32[]{:S(2)}, u32[]{:S(2)}) %collective-permute-start.12) | collective-permute-done | bytes 196640 | tf_op jit(solution)/shard_map/ppermute | solution.py:53
  116.1 1.5 fusion.8
  118.3 2.9 %convolution_convert_fusion = bf16[768,2304]{1,0:T(8,128)(2,1)} fusion(bf16[128,768]{1,0:T(8,128)(2,1)S(1)} %copy-done.13, bf16[128,1536]{1,0:T(8,128)(2,1)S(1)} %bitcast.122, bf16[128,768]{1,0:T(8,128)(2,1)S(1)} %copy-done.6), kind=kOutput, calls=%fused_computation | convolution fusion | flops 455933952 | bytes 4325376 | tf_op jit(solution)/shard_map/nd,nf->df/dot_general | solution.py:239
  121.8 2.8 %multiply_reduce_fusion = (f32[768]{0:T(1024)S(1)}, f32[128]{0:T(128)S(1)}, f32[128]{0:T(128)S(1)}, f32[768]{0:T(1024)S(1)}, f32[128,768]{1,0:T(8,128)S(1)}) fusion(f32[1,8,2,8,768]{4,3,1,2,0:T(8,128)} %copy.23, f32[128]{0:T(128)S(1)} %copy-done.23, f32[128]{0:T(128)S(1)} %copy-done.21, f32[768]{0:T(1024)S(1)} %add_reduce_fusion, ...), kind=kOutput, calls=%fused_computation.33 | convolution fusion | flops 455047424 | bytes 4926464 | tf_op jit(solution)/shard_map/nf,df->nd/dot_general | solution.py:240
  126.5 4.0 %collective-permute-done.24 = f32[3,768]{1,0:T(4,128)} collective-permute-done((f32[3,768]{1,0:T(4,128)}, f32[3,768]{1,0:T(4,128)}, u32[]{:S(2)}, u32[]{:S(2)}) %collective-permute-start.24) | collective-permute-done | bytes 9248 | tf_op jit(solution)/shard_map/ppermute | solution.py:121
  131.8 3.2 %collective-permute-start.25 = (f32[3,768]{1,0:T(4,128)}, f32[3,768]{1,0:T(4,128)}, u32[]{:S(2)}, u32[]{:S(2)}) collective-permute-start(f32[3,768]{1,0:T(4,128)} %fusion.27), channel_id=1, source_target_pairs={{0,8},{4,12},{8,0},{12,4},{1,9},{5,13},{9,1},{13,5},{2,10},{6,14},... | collective-permute-start | bytes 27656 | tf_op jit(solution)/shard_map/ppermute | solution.py:121
  135.0 8.3 %reduce-scatter.5.cloned.1.call-done = bf16[48,768]{1,0:T(8,128)(2,1)} async-done(((bf16[768,768]{1,0:T(8,128)(2,1)}), bf16[48,768]{1,0:T(8,128)(2,1)}) %reduce-scatter.5.cloned.1.call-update) | async-done | bytes 73744 | tf_op jit(solution)/shard_map/reduce_scatter | solution.py:126
  143.3 2.3 reshape.159
  150.2 1.6 collective-permute-start.26
  151.8 2.2 collective-permute-done.26
  154.0 2.8 %collective-permute-start.27 = (f32[3,768]{1,0:T(4,128)S(1)}, f32[3,768]{1,0:T(4,128)}, u32[]{:S(2)}, u32[]{:S(2)}) collective-permute-start(f32[3,768]{1,0:T(4,128)S(1)} %add.172), channel_id=1, source_target_pairs={{0,2},{1,3},{2,0},{3,1},{4,6},{5,7},{6,4},{7,5},{8,10},{9,11},{10,... | collective-permute-start | bytes 27656 | tf_op jit(solution)/shard_map/ppermute | solution.py:121
  156.8 1.6 copy.39
  158.4 1.6 copy.40
  163.4 4.1 %collective-permute-done.21 = bf16[2,2,48,48]{3,2,0,1:T(8,128)(2,1)S(1)} collective-permute-done((bf16[2,2,48,48]{3,2,0,1:T(8,128)(2,1)S(1)}, bf16[2,2,48,48]{3,2,0,1:T(8,128)(2,1)S(1)}, u32[]{:S(2)}, u32[]{:S(2)}) %collective-permute-start.21) | collective-permute-done | bytes 18464 | tf_op jit(solution)/shard_map/ppermute | solution.py:120
  168.2 38.5 %reduce-scatter.3.cloned.1.call-done = bf16[48,2304]{1,0:T(8,128)(2,1)} async-done(((bf16[768,2304]{1,0:T(8,128)(2,1)}), bf16[48,2304]{1,0:T(8,128)(2,1)}) %reduce-scatter.3.cloned.1.call-update) | async-done | bytes 221200 | tf_op jit(solution)/shard_map/reduce_scatter | solution.py:126
  206.7 3.2 %reshape.158 = f32[48,2,2,2,2,144]{5,4,3,2,1,0:T(2,128)} reshape(bf16[48,2304]{1,0:T(8,128)(2,1)} %reduce-scatter.3.cloned.1.call-done) | data formatting | bytes 663552 | tf_op jit(solution)/shard_map/transpose | solution.py:129
  209.8 1.6 copy.37
  211.5 1.5 collective-permute-start.16
  213.8 1.7 collective-permute-start.22
  215.5 2.7 %collective-permute-done.16 = bf16[2,2,2,48,144]{4,3,1,2,0:T(8,128)(2,1)S(1)} collective-permute-done((bf16[2,2,2,48,144]{4,3,1,2,0:T(8,128)(2,1)S(1)}, bf16[2,2,2,48,144]{4,3,1,2,0:T(8,128)(2,1)S(1)}, u32[]{:S(2)}, u32[]{:S(2)}) %collective-permute-start.16) | collective-permute-done | bytes 110624 | tf_op jit(solution)/shard_map/ppermute | solution.py:121
  218.5 6.1 %collective-permute-done.17 = bf16[2,2,48,144]{3,2,0,1:T(8,128)(2,1)S(1)} collective-permute-done((bf16[2,2,48,144]{3,2,0,1:T(8,128)(2,1)S(1)}, bf16[2,2,48,144]{3,2,0,1:T(8,128)(2,1)S(1)}, u32[]{:S(2)}, u32[]{:S(2)}) %collective-permute-start.17) | collective-permute-done | bytes 55328 | tf_op jit(solution)/shard_map/ppermute | solution.py:121
  224.6 1.6 collective-permute-start.18
  226.2 2.7 %collective-permute-start.23 = (bf16[48,48]{1,0:T(8,128)(2,1)S(1)}, bf16[48,48]{1,0:T(8,128)(2,1)S(1)}, u32[]{:S(2)}, u32[]{:S(2)}) collective-permute-start(bf16[48,48]{1,0:T(8,128)(2,1)S(1)} %fusion.24), channel_id=1, source_target_pairs={{0,2},{1,3},{2,0},{3,1},{4,6},{5,7},{6,4},{7,5},{8,10},{9,11},{10,... | collective-permute-start | bytes 13832 | tf_op jit(solution)/shard_map/ppermute | solution.py:120
  229.0 3.0 %collective-permute-start.19 = (bf16[48,144]{1,0:T(8,128)(2,1)S(1)}, bf16[48,144]{1,0:T(8,128)(2,1)S(1)}, u32[]{:S(2)}, u32[]{:S(2)}) collective-permute-start(bf16[48,144]{1,0:T(8,128)(2,1)S(1)} %fusion.22), channel_id=1, source_target_pairs={{0,2},{1,3},{2,0},{3,1},{4,6},{5,7},{6,4},{7,5},{8,10},{9,11},{10,... | collective-permute-start | bytes 41480 | tf_op jit(solution)/shard_map/ppermute | solution.py:121
  232.6 1.8 collective-permute-done.19
  (142 shorter events, 40.1 us)
Async XLA Ops:
  7.2 9.1 %copy-start = (bf16[768,2304]{1,0:T(8,128)(2,1)S(1)}, bf16[768,2304]{1,0:T(8,128)(2,1)}, u32[]{:S(2)}) copy-start(bf16[768,2304]{1,0:T(8,128)(2,1)} %param.13) | copy-start | bytes 10616836
  7.2 136.1 %reduce-scatter.5.cloned.1.call-start = ((), (), s32[]{:S(2)}) async-start(), calls=%async_computation.3 | async-start | bytes 1253376 | tf_op jit(solution)/shard_map/reduce_scatter | solution.py:126
  8.5 6.6 %copy-start.20 = (f32[128]{0:T(128)}, f32[128]{0:T(128)S(1)}, u32[]{:S(2)}) copy-start(f32[128]{0:T(128)S(1)} %div.36) | copy-start | bytes 1540
  16.3 22.4 %copy-start.25 = (s32[1,4,8]{2,1,0:T(4,128)S(1)}, s32[1,4,8]{2,1,0:T(4,128)}, u32[]{:S(2)}) copy-start(s32[1,4,8]{2,1,0:T(4,128)} %param.15) | copy-start | bytes 388
  16.3 28.8 %copy-start.19 = (f32[2,12]{0,1:T(8,128)S(1)}, f32[2,12]{0,1:T(8,128)}, u32[]{:S(2)}) copy-start(f32[2,12]{0,1:T(8,128)} %constant.104.clone) | copy-start | bytes 292
  19.7 31.3 %collective-permute-start.5 = (bf16[1,1,64,1536]{3,2,1,0:T(8,128)(2,1)}, bf16[1,1,64,1536]{3,2,1,0:T(8,128)(2,1)}, u32[]{:S(2)}, u32[]{:S(2)}) collective-permute-start(bf16[1,1,64,1536]{3,2,1,0:T(8,128)(2,1)} %get-tuple-element.28), channel_id=1, source_target_pairs={{4,1},{5,2},{6,3},{8,5},{9,6},{10,7},{12,9},{13,10},{14,11},{20,17... | collective-permute-start | bytes 589832 | tf_op jit(solution)/shard_map/ppermute | solution.py:53
  23.9 28.5 %collective-permute-start.3 = (bf16[1,1,64,1536]{3,2,1,0:T(8,128)(2,1)}, bf16[1,1,64,1536]{3,2,1,0:T(8,128)(2,1)}, u32[]{:S(2)}, u32[]{:S(2)}) collective-permute-start(bf16[1,1,64,1536]{3,2,1,0:T(8,128)(2,1)} %get-tuple-element.28), channel_id=1, source_target_pairs={{0,1},{1,2},{2,3},{4,5},{5,6},{6,7},{8,9},{9,10},{10,11},{12,13},{... | collective-permute-start | bytes 589832 | tf_op jit(solution)/shard_map/ppermute | solution.py:53
  27.4 26.3 %collective-permute-start = (bf16[1,1,64,1536]{3,2,1,0:T(8,128)(2,1)}, bf16[1,1,64,1536]{3,2,1,0:T(8,128)(2,1)}, u32[]{:S(2)}, u32[]{:S(2)}) collective-permute-start(bf16[1,1,64,1536]{3,2,1,0:T(8,128)(2,1)} %get-tuple-element.28), channel_id=1, source_target_pairs={{0,5},{1,6},{2,7},{4,9},{5,10},{6,11},{8,13},{9,14},{10,15},{16,21... | collective-permute-start | bytes 589832 | tf_op jit(solution)/shard_map/ppermute | solution.py:53
  32.1 35.6 %collective-permute-start.6 = (bf16[1,2,64,1536]{3,2,1,0:T(8,128)(2,1)}, bf16[1,2,64,1536]{3,2,1,0:T(8,128)(2,1)}, u32[]{:S(2)}, u32[]{:S(2)}) collective-permute-start(bf16[1,2,64,1536]{3,2,1,0:T(8,128)(2,1)} %bitcast.4), channel_id=1, source_target_pairs={{4,0},{5,1},{6,2},{7,3},{8,4},{9,5},{10,6},{11,7},{12,8},{13,9},{1... | collective-permute-start | bytes 1179656 | tf_op jit(solution)/shard_map/ppermute | solution.py:53
  34.1 33.6 %collective-permute-start.1 = (bf16[1,2,64,1536]{3,2,1,0:T(8,128)(2,1)}, bf16[1,2,64,1536]{3,2,1,0:T(8,128)(2,1)}, u32[]{:S(2)}, u32[]{:S(2)}) collective-permute-start(bf16[1,2,64,1536]{3,2,1,0:T(8,128)(2,1)} %bitcast.4), channel_id=1, source_target_pairs={{0,4},{1,5},{2,6},{3,7},{4,8},{5,9},{6,10},{7,11},{8,12},{9,13},{1... | collective-permute-start | bytes 1179656 | tf_op jit(solution)/shard_map/ppermute | solution.py:53
  46.6 4.4 %copy-start.18 = (f32[768]{0:T(1024)S(1)}, f32[768]{0:T(1024)}, u32[]{:S(2)}) copy-start(f32[768]{0:T(1024)} %reduce.2) | copy-start | bytes 9220
  46.6 8.4 %copy-start.26 = (f32[128]{0:T(128)S(1)}, f32[128]{0:T(128)}, u32[]{:S(2)}) copy-start(f32[128]{0:T(128)} %mul.100) | copy-start | bytes 1540
  51.0 10.7 %collective-permute-start.7 = (bf16[1,1,64,1536]{3,2,1,0:T(8,128)(2,1)}, bf16[1,1,64,1536]{3,2,1,0:T(8,128)(2,1)S(1)}, u32[]{:S(2)}, u32[]{:S(2)}) collective-permute-start(bf16[1,1,64,1536]{3,2,1,0:T(8,128)(2,1)} %get-tuple-element.29), channel_id=1, source_target_pairs={{5,0},{6,1},{7,2},{9,4},{10,5},{11,6},{13,8},{14,9},{15,10},{21,16... | collective-permute-start | bytes 589832 | tf_op jit(solution)/shard_map/ppermute | solution.py:53
  52.3 15.4 %collective-permute-start.4 = (bf16[1,1,64,1536]{3,2,1,0:T(8,128)(2,1)}, bf16[1,1,64,1536]{3,2,1,0:T(8,128)(2,1)S(1)}, u32[]{:S(2)}, u32[]{:S(2)}) collective-permute-start(bf16[1,1,64,1536]{3,2,1,0:T(8,128)(2,1)} %get-tuple-element.29), channel_id=1, source_target_pairs={{1,0},{2,1},{3,2},{5,4},{6,5},{7,6},{9,8},{10,9},{11,10},{13,12},{... | collective-permute-start | bytes 589832 | tf_op jit(solution)/shard_map/ppermute | solution.py:53
  53.6 14.0 %collective-permute-start.2 = (bf16[1,1,64,1536]{3,2,1,0:T(8,128)(2,1)}, bf16[1,1,64,1536]{3,2,1,0:T(8,128)(2,1)S(1)}, u32[]{:S(2)}, u32[]{:S(2)}) collective-permute-start(bf16[1,1,64,1536]{3,2,1,0:T(8,128)(2,1)} %get-tuple-element.29), channel_id=1, source_target_pairs={{1,4},{2,5},{3,6},{5,8},{6,9},{7,10},{9,12},{10,13},{11,14},{17,20... | collective-permute-start | bytes 589832 | tf_op jit(solution)/shard_map/ppermute | solution.py:53
  56.8 12.6 %copy-start.3 = (f32[128,768]{1,0:T(8,128)S(1)}, f32[128,768]{1,0:T(8,128)}, u32[]{:S(2)}) copy-start(f32[128,768]{1,0:T(8,128)} %copy.25.mask_ref) | copy-start | bytes 1179652
  56.8 12.6 %copy-start.4 = (bf16[128,768]{1,0:T(8,128)(2,1)S(1)}, bf16[128,768]{1,0:T(8,128)(2,1)}, u32[]{:S(2)}) copy-start(bf16[128,768]{1,0:T(8,128)(2,1)} %slice.144.q_ref) | copy-start | bytes 589828
  56.8 12.6 %copy-start.7 = (f32[128,1]{1,0:T(8,128)S(1)}, f32[128,1]{1,0:T(8,128)}, u32[]{:S(2)}) copy-start(f32[128,1]{1,0:T(8,128)} %broadcast_in_dim_reshape.12.valid_ref) | copy-start | bytes 1540
  84.4 122.2 %reduce-scatter.3.cloned.1.call-start = ((), (), s32[]{:S(2)}) async-start(), calls=%async_computation.2 | async-start | bytes 3760128 | tf_op jit(solution)/shard_map/reduce_scatter | solution.py:126
  87.2 12.9 %collective-permute-start.10 = (bf16[1,1,64,1536]{3,2,1,0:T(8,128)(2,1)S(1)}, bf16[1,1,64,1536]{3,2,1,0:T(8,128)(2,1)S(1)}, u32[]{:S(2)}, u32[]{:S(2)}) collective-permute-start(bf16[1,1,64,1536]{3,2,1,0:T(8,128)(2,1)S(1)} %get-tuple-element.17), channel_id=1, source_target_pairs={{1,0},{2,1},{3,2},{5,4},{6,5},{7,6},{9,8},{10,9},{11,10},{13,12},{... | collective-permute-start | bytes 589832 | tf_op jit(solution)/shard_map/ppermute | solution.py:53
  88.5 29.8 %copy-start.6 = (bf16[128,768]{1,0:T(8,128)(2,1)S(1)}, bf16[128,768]{1,0:T(8,128)(2,1)}, u32[]{:S(2)}) copy-start(bf16[128,768]{1,0:T(8,128)(2,1)} %copy-done.5) | copy-start | bytes 589828
  88.5 29.8 %copy-start.13 = (bf16[128,768]{1,0:T(8,128)(2,1)S(1)}, bf16[128,768]{1,0:T(8,128)(2,1)}, u32[]{:S(2)}) copy-start(bf16[128,768]{1,0:T(8,128)(2,1)} %copy-done.12) | copy-start | bytes 589828
  88.5 17.0 %collective-permute-start.15 = (bf16[1,1,64,1536]{3,2,1,0:T(8,128)(2,1)S(1)}, bf16[1,1,64,1536]{3,2,1,0:T(8,128)(2,1)S(1)}, u32[]{:S(2)}, u32[]{:S(2)}) collective-permute-start(bf16[1,1,64,1536]{3,2,1,0:T(8,128)(2,1)S(1)} %get-tuple-element.18), channel_id=1, source_target_pairs={{0,5},{1,6},{2,7},{4,9},{5,10},{6,11},{8,13},{9,14},{10,15},{16,21... | collective-permute-start | bytes 589832 | tf_op jit(solution)/shard_map/ppermute | solution.py:53
  91.5 15.4 %collective-permute-start.14 = (bf16[1,1,64,1536]{3,2,1,0:T(8,128)(2,1)S(1)}, bf16[1,1,64,1536]{3,2,1,0:T(8,128)(2,1)S(1)}, u32[]{:S(2)}, u32[]{:S(2)}) collective-permute-start(bf16[1,1,64,1536]{3,2,1,0:T(8,128)(2,1)S(1)} %get-tuple-element.19), channel_id=1, source_target_pairs={{1,4},{2,5},{3,6},{5,8},{6,9},{7,10},{9,12},{10,13},{11,14},{17,20... | collective-permute-start | bytes 589832 | tf_op jit(solution)/shard_map/ppermute | solution.py:53
  92.8 23.3 %collective-permute-start.8 = (bf16[1,2,64,1536]{3,2,1,0:T(8,128)(2,1)S(1)}, bf16[1,2,64,1536]{3,2,1,0:T(8,128)(2,1)S(1)}, u32[]{:S(2)}, u32[]{:S(2)}) collective-permute-start(bf16[1,2,64,1536]{3,2,1,0:T(8,128)(2,1)S(1)} %get-tuple-element.23), channel_id=1, source_target_pairs={{4,0},{5,1},{6,2},{7,3},{8,4},{9,5},{10,6},{11,7},{12,8},{13,9},{1... | collective-permute-start | bytes 1179656 | tf_op jit(solution)/shard_map/ppermute | solution.py:53
  98.1 17.9 %collective-permute-start.9 = (bf16[1,2,64,1536]{3,2,1,0:T(8,128)(2,1)S(1)}, bf16[1,2,64,1536]{3,2,1,0:T(8,128)(2,1)S(1)}, u32[]{:S(2)}, u32[]{:S(2)}) collective-permute-start(bf16[1,2,64,1536]{3,2,1,0:T(8,128)(2,1)S(1)} %get-tuple-element.24), channel_id=1, source_target_pairs={{0,4},{1,5},{2,6},{3,7},{4,8},{5,9},{6,10},{7,11},{8,12},{9,13},{1... | collective-permute-start | bytes 1179656 | tf_op jit(solution)/shard_map/ppermute | solution.py:53
  100.1 12.8 %collective-permute-start.13 = (bf16[1,1,64,1536]{3,2,1,0:T(8,128)(2,1)S(1)}, bf16[1,1,64,1536]{3,2,1,0:T(8,128)(2,1)S(1)}, u32[]{:S(2)}, u32[]{:S(2)}) collective-permute-start(bf16[1,1,64,1536]{3,2,1,0:T(8,128)(2,1)S(1)} %get-tuple-element.20), channel_id=1, source_target_pairs={{4,1},{5,2},{6,3},{8,5},{9,6},{10,7},{12,9},{13,10},{14,11},{20,17... | collective-permute-start | bytes 589832 | tf_op jit(solution)/shard_map/ppermute | solution.py:53
  105.6 9.8 %collective-permute-start.12 = (bf16[1,1,64,1536]{3,2,1,0:T(8,128)(2,1)S(1)}, bf16[1,1,64,1536]{3,2,1,0:T(8,128)(2,1)S(1)}, u32[]{:S(2)}, u32[]{:S(2)}) collective-permute-start(bf16[1,1,64,1536]{3,2,1,0:T(8,128)(2,1)S(1)} %get-tuple-element.21), channel_id=1, source_target_pairs={{5,0},{6,1},{7,2},{9,4},{10,5},{11,6},{13,8},{14,9},{15,10},{21,16... | collective-permute-start | bytes 589832 | tf_op jit(solution)/shard_map/ppermute | solution.py:53
  106.9 9.2 %collective-permute-start.11 = (bf16[1,1,64,1536]{3,2,1,0:T(8,128)(2,1)S(1)}, bf16[1,1,64,1536]{3,2,1,0:T(8,128)(2,1)S(1)}, u32[]{:S(2)}, u32[]{:S(2)}) collective-permute-start(bf16[1,1,64,1536]{3,2,1,0:T(8,128)(2,1)S(1)} %get-tuple-element.22), channel_id=1, source_target_pairs={{0,1},{1,2},{2,3},{4,5},{5,6},{6,7},{8,9},{9,10},{10,11},{12,13},{... | collective-permute-start | bytes 589832 | tf_op jit(solution)/shard_map/ppermute | solution.py:53
  121.8 2.8 %copy-start.2 = (bf16[128,768]{1,0:T(8,128)(2,1)S(1)}, bf16[128,768]{1,0:T(8,128)(2,1)}, u32[]{:S(2)}) copy-start(bf16[128,768]{1,0:T(8,128)(2,1)} %copy-done.1) | copy-start | bytes 589828
  121.8 2.8 %copy-start.8 = (bf16[768,768]{1,0:T(8,128)(2,1)S(1)}, bf16[768,768]{1,0:T(8,128)(2,1)}, u32[]{:S(2)}) copy-start(bf16[768,768]{1,0:T(8,128)(2,1)} %param.14) | copy-start | bytes 3538948
  121.8 2.8 %copy-start.9 = (f32[1,8,2,8,768]{4,3,1,2,0:T(8,128)S(1)}, f32[1,8,2,8,768]{4,3,1,2,0:T(8,128)}, u32[]{:S(2)}) copy-start(f32[1,8,2,8,768]{4,3,1,2,0:T(8,128)} %copy.23) | copy-start | bytes 1179652
  121.8 2.8 %copy-start.11 = (f32[1,8,2,8,768]{4,3,1,2,0:T(8,128)S(1)}, f32[1,8,2,8,768]{4,3,1,2,0:T(8,128)}, u32[]{:S(2)}) copy-start(f32[1,8,2,8,768]{4,3,1,2,0:T(8,128)} %copy-done.10) | copy-start | bytes 1179652
  121.8 2.8 %copy-start.22 = (f32[128]{0:T(128)S(1)}, f32[128]{0:T(128)}, u32[]{:S(2)}) copy-start(f32[128]{0:T(128)} %copy-done.20) | copy-start | bytes 1540
  121.8 2.8 %copy-start.24 = (f32[128]{0:T(128)S(1)}, f32[128]{0:T(128)}, u32[]{:S(2)}) copy-start(f32[128]{0:T(128)} %rsqrt.12) | copy-start | bytes 1540
  126.5 4.0 %collective-permute-start.24 = (f32[3,768]{1,0:T(4,128)}, f32[3,768]{1,0:T(4,128)}, u32[]{:S(2)}, u32[]{:S(2)}) collective-permute-start(f32[3,768]{1,0:T(4,128)} %pad_maximum_fusion.3), channel_id=1, source_target_pairs={{0,4},{4,0},{8,12},{12,8},{1,5},{5,1},{9,13},{13,9},{2,6},{6,2},{1... | collective-permute-start | bytes 27656 | tf_op jit(solution)/shard_map/ppermute | solution.py:121
  131.8 17.6 %collective-permute-start.25 = (f32[3,768]{1,0:T(4,128)}, f32[3,768]{1,0:T(4,128)}, u32[]{:S(2)}, u32[]{:S(2)}) collective-permute-start(f32[3,768]{1,0:T(4,128)} %fusion.27), channel_id=1, source_target_pairs={{0,8},{4,12},{8,0},{12,4},{1,9},{5,13},{9,1},{13,5},{2,10},{6,14},... | collective-permute-start | bytes 27656 | tf_op jit(solution)/shard_map/ppermute | solution.py:121
  148.1 12.6 %collective-permute-start.20 = (bf16[2,2,2,48,48]{4,3,1,2,0:T(8,128)(2,1)}, bf16[2,2,2,48,48]{4,3,1,2,0:T(8,128)(2,1)}, u32[]{:S(2)}, u32[]{:S(2)}) collective-permute-start(bf16[2,2,2,48,48]{4,3,1,2,0:T(8,128)(2,1)} %fusion.19), channel_id=1, source_target_pairs={{0,4},{4,0},{8,12},{12,8},{1,5},{5,1},{9,13},{13,9},{2,6},{6,2},{1... | collective-permute-start | bytes 110600 | tf_op jit(solution)/shard_map/ppermute | solution.py:120
  150.2 3.8 %collective-permute-start.26 = (f32[3,768]{1,0:T(4,128)S(1)}, f32[3,768]{1,0:T(4,128)S(1)}, u32[]{:S(2)}, u32[]{:S(2)}) collective-permute-start(f32[3,768]{1,0:T(4,128)S(1)} %fusion.42), channel_id=1, source_target_pairs={{0,1},{1,0},{2,3},{3,2},{4,5},{5,4},{6,7},{7,6},{8,9},{9,8},{10,11... | collective-permute-start | bytes 27656 | tf_op jit(solution)/shard_map/ppermute | solution.py:121
  154.0 6.0 %collective-permute-start.27 = (f32[3,768]{1,0:T(4,128)S(1)}, f32[3,768]{1,0:T(4,128)}, u32[]{:S(2)}, u32[]{:S(2)}) collective-permute-start(f32[3,768]{1,0:T(4,128)S(1)} %add.172), channel_id=1, source_target_pairs={{0,2},{1,3},{2,0},{3,1},{4,6},{5,7},{6,4},{7,5},{8,10},{9,11},{10,... | collective-permute-start | bytes 27656 | tf_op jit(solution)/shard_map/ppermute | solution.py:121
  161.9 5.7 %collective-permute-start.21 = (bf16[2,2,48,48]{3,2,0,1:T(8,128)(2,1)S(1)}, bf16[2,2,48,48]{3,2,0,1:T(8,128)(2,1)S(1)}, u32[]{:S(2)}, u32[]{:S(2)}) collective-permute-start(bf16[2,2,48,48]{3,2,0,1:T(8,128)(2,1)S(1)} %fusion.21), channel_id=1, source_target_pairs={{0,8},{4,12},{8,0},{12,4},{1,9},{5,13},{9,1},{13,5},{2,10},{6,14},... | collective-permute-start | bytes 55304 | tf_op jit(solution)/shard_map/ppermute | solution.py:120
  209.8 8.6 %copy-start.17 = (f32[2,2,48,48]{3,2,0,1:T(8,128)S(1)}, f32[2,2,48,48]{3,2,0,1:T(8,128)}, u32[]{:S(2)}) copy-start(f32[2,2,48,48]{3,2,0,1:T(8,128)} %bitcast_add_fusion.5) | copy-start | bytes 110596
  211.5 6.7 %collective-permute-start.16 = (bf16[2,2,2,48,144]{4,3,1,2,0:T(8,128)(2,1)S(1)}, bf16[2,2,2,48,144]{4,3,1,2,0:T(8,128)(2,1)S(1)}, u32[]{:S(2)}, u32[]{:S(2)}) collective-permute-start(bf16[2,2,2,48,144]{4,3,1,2,0:T(8,128)(2,1)S(1)} %fusion.17), channel_id=1, source_target_pairs={{0,4},{4,0},{8,12},{12,8},{1,5},{5,1},{9,13},{13,9},{2,6},{6,2},{1... | collective-permute-start | bytes 331784 | tf_op jit(solution)/shard_map/ppermute | solution.py:121
  213.8 4.6 %collective-permute-start.22 = (bf16[2,48,48]{2,1,0:T(8,128)(2,1)S(1)}, bf16[2,48,48]{2,1,0:T(8,128)(2,1)S(1)}, u32[]{:S(2)}, u32[]{:S(2)}) collective-permute-start(bf16[2,48,48]{2,1,0:T(8,128)(2,1)S(1)} %fusion.23), channel_id=1, source_target_pairs={{0,1},{1,0},{2,3},{3,2},{4,5},{5,4},{6,7},{7,6},{8,9},{9,8},{10,11... | collective-permute-start | bytes 27656 | tf_op jit(solution)/shard_map/ppermute | solution.py:120
  218.3 6.2 %collective-permute-start.17 = (bf16[2,2,48,144]{3,2,0,1:T(8,128)(2,1)S(1)}, bf16[2,2,48,144]{3,2,0,1:T(8,128)(2,1)S(1)}, u32[]{:S(2)}, u32[]{:S(2)}) collective-permute-start(bf16[2,2,48,144]{3,2,0,1:T(8,128)(2,1)S(1)} %fusion.18), channel_id=1, source_target_pairs={{0,8},{4,12},{8,0},{12,4},{1,9},{5,13},{9,1},{13,5},{2,10},{6,14},... | collective-permute-start | bytes 165896 | tf_op jit(solution)/shard_map/ppermute | solution.py:121
  224.6 4.4 %collective-permute-start.18 = (bf16[2,48,144]{2,1,0:T(8,128)(2,1)S(1)}, bf16[2,48,144]{2,1,0:T(8,128)(2,1)S(1)}, u32[]{:S(2)}, u32[]{:S(2)}) collective-permute-start(bf16[2,48,144]{2,1,0:T(8,128)(2,1)S(1)} %fusion.20), channel_id=1, source_target_pairs={{0,1},{1,0},{2,3},{3,2},{4,5},{5,4},{6,7},{7,6},{8,9},{9,8},{10,11... | collective-permute-start | bytes 82952 | tf_op jit(solution)/shard_map/ppermute | solution.py:121
  226.2 5.7 %collective-permute-start.23 = (bf16[48,48]{1,0:T(8,128)(2,1)S(1)}, bf16[48,48]{1,0:T(8,128)(2,1)S(1)}, u32[]{:S(2)}, u32[]{:S(2)}) collective-permute-start(bf16[48,48]{1,0:T(8,128)(2,1)S(1)} %fusion.24), channel_id=1, source_target_pairs={{0,2},{1,3},{2,0},{3,1},{4,6},{5,7},{6,4},{7,5},{8,10},{9,11},{10,... | collective-permute-start | bytes 13832 | tf_op jit(solution)/shard_map/ppermute | solution.py:120
  229.0 5.4 %collective-permute-start.19 = (bf16[48,144]{1,0:T(8,128)(2,1)S(1)}, bf16[48,144]{1,0:T(8,128)(2,1)S(1)}, u32[]{:S(2)}, u32[]{:S(2)}) collective-permute-start(bf16[48,144]{1,0:T(8,128)(2,1)S(1)} %fusion.22), channel_id=1, source_target_pairs={{0,2},{1,3},{2,0},{3,1},{4,6},{5,7},{6,4},{7,5},{8,10},{9,11},{10,... | collective-permute-start | bytes 41480 | tf_op jit(solution)/shard_map/ppermute | solution.py:121
  (9 other events, 9.4 us)
Sparse Core Ops, SparseCore 0:
  84.5 58.7 reduce-scatter.4
  145.9 60.7 reduce-scatter.2

commit v4 on v3

--- a/solution.py
+++ b/solution.py
@@ -250,8 +250,19 @@
     mixed = (values + branch_gate * projected).astype(BF16)
     latent_grad = (incoming + latent_term).astype(BF16)
 
-    output_grad, _ = reduce_weights(output_term, None)
-    input_grad, sums = reduce_weights(input_term, jnp.stack([shift_term, scale_term, gate_term]))
+    blocks = lax.axis_size("row") * lax.axis_size("col")
+    width_in = input_term.shape[1] // blocks
+    width_out = output_term.shape[1] // blocks
+    combined = jnp.concatenate(
+        [
+            input_term.reshape(model_width, blocks, width_in),
+            output_term.reshape(model_width, blocks, width_out),
+        ],
+        axis=-1,
+    ).reshape(model_width, blocks * (width_in + width_out))
+    reduced, sums = reduce_weights(combined, jnp.stack([shift_term, scale_term, gate_term]))
+    input_grad = reduced[:, :width_in]
+    output_grad = reduced[:, width_in:]
 
     return (
         from_tiles(mixed, height, across)[None],

time: 243 us -> 260 us (1.070)
  local copies, waits for them, and re-layouts: 29.6 us -> 42.2 us
  other arithmetic: 24 us -> 34.3 us
  starting transfers between devices: 68.9 us -> 61.6 us
    reduce_scatter x2 -> x1, waiting for transfers between devices: 46.8 us -> 56.5 us  [reduce_weights(): lax.psum_scatter(term.astype(BF16), 'dp', scatter_dimension=0, tiled=True)]
    convert_element_type x0 -> x4, local copies, waits for them, and re-layouts: none -> 8.61 us  [the longest x1 6.63 us: reduce_weights(): term.astype(BF16)]
    ppermute x4 -> x0, starting transfers between devices: 6.79 us -> none  [exchange(): lax.ppermute(away.astype(BF16), axis, pairs).astype(F32)]
    transpose x4 -> x1, local copies, waits for them, and re-layouts: 8.2 us -> 2.59 us  [reduce_weights(): part.reshape(rest, rows // 2, 2, cols // 2, 2, -1)]
    ppermute x16, waiting for transfers between devices: 14.1 us -> 8.98 us  [send(): lax.ppermute(block, ('row', 'col'), shifts(rows, cols, step_row, step_col))]
    ppermute x4 -> x0, waiting for transfers between devices: 4.1 us -> none  [exchange(): lax.ppermute(away.astype(BF16), axis, pairs).astype(F32)]
    concatenate x0 -> x2, other arithmetic: none -> 3.76 us  [the longest x1 2.67 us: local(): jnp.concatenate([input_term.reshape(model_width, blocks, width_in), outpu...]
  transfers between devices with their start and end apart: 30 -> 25, of which waited for: 12 -> 9; matrix products, arithmetic and copies ran while one was open for 16% -> 17% of each run, Pallas kernels for 0% -> 0%
where the time goes in v4:
time: 260 us; the launch traced here: 258 us
  waiting for transfers between devices  82.2 us (32%)
  starting transfers between devices  61.6 us (24%)
  local copies, waits for them, and re-layouts  42.2 us (16%)
  other arithmetic  34.3 us (13%)
  between operations  14.6 us (6%)
  Pallas kernels  12.1 us (5%)
  matrix products  11 us (4%)
    reduce_scatter x1, waiting for transfers between devices, reduce_weights(): lax.psum_scatter(term.astype(BF16), 'dp', scatter_dimension=0, tiled=True)  56.5 us
    ppermute x16, starting transfers between devices, send(): lax.ppermute(block, ('row', 'col'), shifts(rows, cols, step_row, step_col))  48.9 us
    ppermute x8, waiting for transfers between devices, exchange(): got, got_extra = lax.ppermute((away.astype(BF16), extra), axis, pairs)  16.8 us
    ppermute x8, starting transfers between devices, exchange(): got, got_extra = lax.ppermute((away.astype(BF16), extra), axis, pairs)  12.7 us
    pallas_call x1, Pallas kernels, attention(): pl.pallas_call(attention_kernel, out_shape=(jax.ShapeDtypeStruct((tokens,...  12.1 us
    ppermute x16, waiting for transfers between devices, send(): lax.ppermute(block, ('row', 'col'), shifts(rows, cols, step_row, step_col))  8.98 us
    convert_element_type x1, local copies, waits for them, and re-layouts, reduce_weights(): term.astype(BF16)  6.63 us
  transfers between devices with their start and end apart: 25, of which 9 were waited for; matrix products, arithmetic and copies ran while one was open for 17% of the time, Pallas kernels for 0%

profile of v4, /device:TPU:4, one launch (start us, length us, event | category | flops | bytes accessed | tf_op | source)
XLA Modules:
  0.0 258.0 jit_solution(13353418236941956113)
XLA Ops:
  8.4 1.7 multiply_reduce_fusion.2
  10.8 1.7 bitcast_convert_fusion.1
  15.1 1.8 copy.50
  21.6 1.8 fusion.29
  23.4 4.8 %collective-permute-start = (bf16[1,1,64,1536]{3,2,1,0:T(8,128)(2,1)}, bf16[1,1,64,1536]{3,2,1,0:T(8,128)(2,1)}, u32[]{:S(2)}, u32[]{:S(2)}) collective-permute-start(bf16[1,1,64,1536]{3,2,1,0:T(8,128)(2,1)} %get-tuple-element.28), channel_id=1, source_target_pairs={{0,5},{1,6},{2,7},{4,9},{5,10},{6,11},{8,13},{9,14},{10,15},{16,21... | collective-permute-start | bytes 589832 | tf_op jit(solution)/shard_map/ppermute | solution.py:53
  28.2 3.5 %collective-permute-start.3 = (bf16[1,1,64,1536]{3,2,1,0:T(8,128)(2,1)}, bf16[1,1,64,1536]{3,2,1,0:T(8,128)(2,1)}, u32[]{:S(2)}, u32[]{:S(2)}) collective-permute-start(bf16[1,1,64,1536]{3,2,1,0:T(8,128)(2,1)} %get-tuple-element.28), channel_id=1, source_target_pairs={{0,1},{1,2},{2,3},{4,5},{5,6},{6,7},{8,9},{9,10},{10,11},{12,13},{... | collective-permute-start | bytes 589832 | tf_op jit(solution)/shard_map/ppermute | solution.py:53
  31.7 1.9 collective-permute-start.1
  33.6 3.9 %collective-permute-start.6 = (bf16[1,2,64,1536]{3,2,1,0:T(8,128)(2,1)}, bf16[1,2,64,1536]{3,2,1,0:T(8,128)(2,1)}, u32[]{:S(2)}, u32[]{:S(2)}) collective-permute-start(bf16[1,2,64,1536]{3,2,1,0:T(8,128)(2,1)} %bitcast.4), channel_id=1, source_target_pairs={{4,0},{5,1},{6,2},{7,3},{8,4},{9,5},{10,6},{11,7},{12,8},{13,9},{1... | collective-permute-start | bytes 1179656 | tf_op jit(solution)/shard_map/ppermute | solution.py:53
  46.1 1.6 slice.120.q_ref
  53.6 1.5 broadcast_in_dim.15
  55.0 1.9 copy.52.mask_ref
  57.0 1.7 fusion.12
  58.7 1.8 copy.58
  61.7 6.1 %collective-permute-start.5 = (bf16[1,1,64,1536]{3,2,1,0:T(8,128)(2,1)}, bf16[1,1,64,1536]{3,2,1,0:T(8,128)(2,1)S(1)}, u32[]{:S(2)}, u32[]{:S(2)}) collective-permute-start(bf16[1,1,64,1536]{3,2,1,0:T(8,128)(2,1)} %get-tuple-element.28), channel_id=1, source_target_pairs={{4,1},{5,2},{6,3},{8,5},{9,6},{10,7},{12,9},{13,10},{14,11},{20,17... | collective-permute-start | bytes 589832 | tf_op jit(solution)/shard_map/ppermute | solution.py:53
  69.1 1.8 fusion.ga_ref
  71.3 6.6 %collective-permute-done.7 = bf16[1,1,64,1536]{3,2,1,0:T(8,128)(2,1)S(1)} collective-permute-done((bf16[1,1,64,1536]{3,2,1,0:T(8,128)(2,1)}, bf16[1,1,64,1536]{3,2,1,0:T(8,128)(2,1)S(1)}, u32[]{:S(2)}, u32[]{:S(2)}) %collective-permute-start.7) | collective-permute-done | bytes 196640 | tf_op jit(solution)/shard_map/ppermute | solution.py:53
  77.9 1.7 maximum_maximum_fusion
  79.6 12.1 %shard_map.144 = (bf16[128,768]{1,0:T(8,128)(2,1)S(1)}, bf16[128,768]{1,0:T(8,128)(2,1)S(1)}, f32[768,1536]{1,0:T(8,128)}) custom-call(bf16[128,768]{1,0:T(8,128)(2,1)S(1)} %copy-done.4, bf16[768,1536]{1,0:T(8,128)(2,1)S(1)} %bitcast.145, bf16[128,768]{1,0:T(8,128)(2,1)S(1)} %fusion.ga_ref, f32[128,768]{1,0:T(8,128)S(1)} %copy-done.3, f32[128,1]{1,0:T(8,128)S(1)} %copy-done.6), custom_call_target="tpu_custom_call" | custom-call | flops 3019898880 | bytes 12582912 | tf_op jit(solution)/shard_map/pallas_call | solution.py:182
  91.7 2.8 %convert.38 = bf16[3,4,64,1536]{3,2,1,0:T(8,128)(2,1)S(1)} convert(f32[3,4,64,1536]{3,2,1,0:T(8,128)} %bitcast.147) | non-fusion elementwise | flops 1179648 | bytes 7077888 | tf_op jit(solution)/shard_map/convert.31
  97.7 5.2 %collective-permute-start.11 = (bf16[1,1,64,1536]{3,2,1,0:T(8,128)(2,1)}, bf16[1,1,64,1536]{3,2,1,0:T(8,128)(2,1)}, u32[]{:S(2)}, u32[]{:S(2)}) collective-permute-start(bf16[1,1,64,1536]{3,2,1,0:T(8,128)(2,1)} %get-tuple-element.22), channel_id=1, source_target_pairs={{0,1},{1,2},{2,3},{4,5},{5,6},{6,7},{8,9},{9,10},{10,11},{12,13},{... | collective-permute-start | bytes 589832 | tf_op jit(solution)/shard_map/ppermute | solution.py:53
  104.3 3.3 %collective-permute-start.8 = (bf16[1,2,64,1536]{3,2,1,0:T(8,128)(2,1)}, bf16[1,2,64,1536]{3,2,1,0:T(8,128)(2,1)}, u32[]{:S(2)}, u32[]{:S(2)}) collective-permute-start(bf16[1,2,64,1536]{3,2,1,0:T(8,128)(2,1)} %get-tuple-element.23), channel_id=1, source_target_pairs={{4,0},{5,1},{6,2},{7,3},{8,4},{9,5},{10,6},{11,7},{12,8},{13,9},{1... | collective-permute-start | bytes 1179656 | tf_op jit(solution)/shard_map/ppermute | solution.py:53
  107.6 3.4 %collective-permute-start.9 = (bf16[1,2,64,1536]{3,2,1,0:T(8,128)(2,1)}, bf16[1,2,64,1536]{3,2,1,0:T(8,128)(2,1)}, u32[]{:S(2)}, u32[]{:S(2)}) collective-permute-start(bf16[1,2,64,1536]{3,2,1,0:T(8,128)(2,1)} %get-tuple-element.24), channel_id=1, source_target_pairs={{0,4},{1,5},{2,6},{3,7},{4,8},{5,9},{6,10},{7,11},{8,12},{9,13},{1... | collective-permute-start | bytes 1179656 | tf_op jit(solution)/shard_map/ppermute | solution.py:53
  111.9 1.7 copy.55
  113.7 5.6 %collective-permute-start.13 = (bf16[1,1,64,1536]{3,2,1,0:T(8,128)(2,1)}, bf16[1,1,64,1536]{3,2,1,0:T(8,128)(2,1)S(1)}, u32[]{:S(2)}, u32[]{:S(2)}) collective-permute-start(bf16[1,1,64,1536]{3,2,1,0:T(8,128)(2,1)} %get-tuple-element.20), channel_id=1, source_target_pairs={{4,1},{5,2},{6,3},{8,5},{9,6},{10,7},{12,9},{13,10},{14,11},{20,17... | collective-permute-start | bytes 589832 | tf_op jit(solution)/shard_map/ppermute | solution.py:53
  120.6 3.4 %collective-permute-start.15 = (bf16[1,1,64,1536]{3,2,1,0:T(8,128)(2,1)}, bf16[1,1,64,1536]{3,2,1,0:T(8,128)(2,1)S(1)}, u32[]{:S(2)}, u32[]{:S(2)}) collective-permute-start(bf16[1,1,64,1536]{3,2,1,0:T(8,128)(2,1)} %get-tuple-element.18), channel_id=1, source_target_pairs={{0,5},{1,6},{2,7},{4,9},{5,10},{6,11},{8,13},{9,14},{10,15},{16,21... | collective-permute-start | bytes 589832 | tf_op jit(solution)/shard_map/ppermute | solution.py:53
  124.0 2.5 convolution_convert_fusion.2
  126.5 2.0 collective-permute-done.14
  128.6 2.6 %fusion.8 = bf16[1,2,64,1536]{3,2,1,0:T(8,128)(2,1)} fusion(f32[3,4,64,1536]{3,2,1,0:T(8,128)} %bitcast.148, bf16[1,2,64,1536]{3,2,1,0:T(8,128)(2,1)} %collective-permute-done.9, bf16[1,2,64,1536]{3,2,1,0:T(8,128)(2,1)} %collective-permute-done.8, bf16[1,1,64,1536]{3,2,1,0:T(8,128)(2,1)S(1)} %collective-permute-done.15, ...), kind=kLoop, calls=%fused_computation.15 | loop fusion | flops 3342336 | bytes 3145728 | tf_op jit(solution)/shard_map/convert_element_type | solution.py:238
  131.2 1.9 copy.56
  134.2 2.1 convolution_convert_fusion.1
  136.3 2.7 %pad_maximum_fusion = bf16[768,16,192]{0,2,1:T(8,128)(2,1)} fusion(bf16[768,16,48]{0,2,1:T(8,128)(2,1)S(1)} %copy-done.7, bf16[768,16,144]{0,2,1:T(8,128)(2,1)S(1)} %convolution_convert_fusion.1), kind=kLoop, calls=%fused_computation | loop fusion | flops 9437184 | bytes 9437184 | tf_op jit(solution)/shard_map/concatenate | solution.py:256
  139.0 6.6 %copy.59 = bf16[768,3072]{1,0:T(8,128)(2,1)} copy(bf16[768,3072]{0,1:T(8,128)(2,1)} %bitcast.146) | data formatting | bytes 9437184 | tf_op jit(solution)/shard_map/convert_element_type | solution.py:126
  146.3 2.8 %multiply_reduce_fusion = (f32[768]{0:T(1024)S(1)}, f32[128]{0:T(128)S(1)}, f32[128]{0:T(128)S(1)}, f32[768]{0:T(1024)S(1)}, f32[128,768]{1,0:T(8,128)S(1)}) fusion(f32[1,8,2,8,768]{4,3,1,2,0:T(8,128)} %copy.50, f32[128]{0:T(128)S(1)} %copy-done.20, f32[128]{0:T(128)S(1)} %copy-done.19, f32[768]{0:T(1024)S(1)} %copy-done.15, ...), kind=kOutput, calls=%fused_computation.34 | convolution fusion | flops 455047424 | bytes 4926464 | tf_op jit(solution)/shard_map/nf,df->nd/dot_general | solution.py:240
  151.9 3.1 %collective-permute-done.20 = f32[3,768]{1,0:T(4,128)} collective-permute-done((f32[3,768]{1,0:T(4,128)}, f32[3,768]{1,0:T(4,128)}, u32[]{:S(2)}, u32[]{:S(2)}) %collective-permute-start.20) | collective-permute-done | bytes 9248 | tf_op jit(solution)/shard_map/ppermute | solution.py:121
  156.3 2.5 collective-permute-start.21
  158.8 56.5 %reduce-scatter.2.cloned.1.call-done = bf16[48,3072]{1,0:T(8,128)(2,1)} async-done(((bf16[768,3072]{1,0:T(8,128)(2,1)}), bf16[48,3072]{1,0:T(8,128)(2,1)}) %reduce-scatter.2.cloned.1.call-update) | async-done | bytes 294928 | tf_op jit(solution)/shard_map/reduce_scatter | solution.py:126
  215.2 2.6 %reshape.164 = f32[48,2,2,2,2,192]{5,4,3,2,1,0:T(2,128)} reshape(bf16[48,3072]{1,0:T(8,128)(2,1)} %reduce-scatter.2.cloned.1.call-done) | data formatting | bytes 884736 | tf_op jit(solution)/shard_map/transpose | solution.py:129
  217.8 2.0 fusion.21
  221.8 1.6 collective-permute-start.22
  223.3 2.2 collective-permute-done.22
  225.6 3.0 %collective-permute-start.23 = (f32[3,768]{1,0:T(4,128)S(1)}, f32[3,768]{1,0:T(4,128)}, u32[]{:S(2)}, u32[]{:S(2)}) collective-permute-start(f32[3,768]{1,0:T(4,128)S(1)} %add.158), channel_id=1, source_target_pairs={{0,2},{1,3},{2,0},{3,1},{4,6},{5,7},{6,4},{7,5},{8,10},{9,11},{10,... | collective-permute-start | bytes 27656 | tf_op jit(solution)/shard_map/ppermute | solution.py:121
  228.6 1.6 copy.84
  230.2 1.6 copy.85
  232.5 1.5 fusion.11
  235.6 4.8 %collective-permute-done.17 = bf16[2,2,48,192]{3,1,0,2:T(2,128)(2,1)S(1)} collective-permute-done((bf16[2,2,48,192]{3,1,0,2:T(2,128)(2,1)S(1)}, bf16[2,2,48,192]{3,1,0,2:T(2,128)(2,1)S(1)}, u32[]{:S(2)}, u32[]{:S(2)}) %collective-permute-start.17) | collective-permute-done | bytes 73760 | tf_op jit(solution)/shard_map/ppermute | solution.py:121
  241.4 3.4 %collective-permute-done.18 = bf16[2,48,192]{2,0,1:T(2,128)(2,1)S(1)} collective-permute-done((bf16[2,48,192]{2,0,1:T(2,128)(2,1)S(1)}, bf16[2,48,192]{2,0,1:T(2,128)(2,1)S(1)}, u32[]{:S(2)}, u32[]{:S(2)}) %collective-permute-start.18) | collective-permute-done | bytes 36896 | tf_op jit(solution)/shard_map/ppermute | solution.py:121
  245.1 2.2 collective-permute-start.19
  247.3 3.2 %collective-permute-done.19 = bf16[48,192]{1,0:T(8,128)(2,1)S(1)} collective-permute-done((bf16[48,192]{1,0:T(8,128)(2,1)S(1)}, bf16[48,192]{1,0:T(8,128)(2,1)S(1)}, u32[]{:S(2)}, u32[]{:S(2)}) %collective-permute-start.19) | collective-permute-done | bytes 18464 | tf_op jit(solution)/shard_map/ppermute | solution.py:121
  (121 shorter events, 45.1 us)
Async XLA Ops:
  7.2 12.2 %copy-start = (bf16[768,2304]{1,0:T(8,128)(2,1)S(1)}, bf16[768,2304]{1,0:T(8,128)(2,1)}, u32[]{:S(2)}) copy-start(bf16[768,2304]{1,0:T(8,128)(2,1)} %param.13) | copy-start | bytes 10616836
  7.2 208.1 %reduce-scatter.2.cloned.1.call-start = ((), (), s32[]{:S(2)}) async-start(), calls=%async_computation.1 | async-start | bytes 5013504 | tf_op jit(solution)/shard_map/reduce_scatter | solution.py:126
  20.0 0.8 copy-start.12
  23.4 37.0 %collective-permute-start = (bf16[1,1,64,1536]{3,2,1,0:T(8,128)(2,1)}, bf16[1,1,64,1536]{3,2,1,0:T(8,128)(2,1)}, u32[]{:S(2)}, u32[]{:S(2)}) collective-permute-start(bf16[1,1,64,1536]{3,2,1,0:T(8,128)(2,1)} %get-tuple-element.28), channel_id=1, source_target_pairs={{0,5},{1,6},{2,7},{4,9},{5,10},{6,11},{8,13},{9,14},{10,15},{16,21... | collective-permute-start | bytes 589832 | tf_op jit(solution)/shard_map/ppermute | solution.py:53
  28.2 39.6 %collective-permute-start.3 = (bf16[1,1,64,1536]{3,2,1,0:T(8,128)(2,1)}, bf16[1,1,64,1536]{3,2,1,0:T(8,128)(2,1)}, u32[]{:S(2)}, u32[]{:S(2)}) collective-permute-start(bf16[1,1,64,1536]{3,2,1,0:T(8,128)(2,1)} %get-tuple-element.28), channel_id=1, source_target_pairs={{0,1},{1,2},{2,3},{4,5},{5,6},{6,7},{8,9},{9,10},{10,11},{12,13},{... | collective-permute-start | bytes 589832 | tf_op jit(solution)/shard_map/ppermute | solution.py:53
  31.7 46.2 %collective-permute-start.1 = (bf16[1,2,64,1536]{3,2,1,0:T(8,128)(2,1)}, bf16[1,2,64,1536]{3,2,1,0:T(8,128)(2,1)}, u32[]{:S(2)}, u32[]{:S(2)}) collective-permute-start(bf16[1,2,64,1536]{3,2,1,0:T(8,128)(2,1)} %bitcast.4), channel_id=1, source_target_pairs={{0,4},{1,5},{2,6},{3,7},{4,8},{5,9},{6,10},{7,11},{8,12},{9,13},{1... | collective-permute-start | bytes 1179656 | tf_op jit(solution)/shard_map/ppermute | solution.py:53
  33.6 44.3 %collective-permute-start.6 = (bf16[1,2,64,1536]{3,2,1,0:T(8,128)(2,1)}, bf16[1,2,64,1536]{3,2,1,0:T(8,128)(2,1)}, u32[]{:S(2)}, u32[]{:S(2)}) collective-permute-start(bf16[1,2,64,1536]{3,2,1,0:T(8,128)(2,1)} %bitcast.4), channel_id=1, source_target_pairs={{4,0},{5,1},{6,2},{7,3},{8,4},{9,5},{10,6},{11,7},{12,8},{13,9},{1... | collective-permute-start | bytes 1179656 | tf_op jit(solution)/shard_map/ppermute | solution.py:53
  37.5 24.2 %collective-permute-start.2 = (bf16[1,1,64,1536]{3,2,1,0:T(8,128)(2,1)}, bf16[1,1,64,1536]{3,2,1,0:T(8,128)(2,1)}, u32[]{:S(2)}, u32[]{:S(2)}) collective-permute-start(bf16[1,1,64,1536]{3,2,1,0:T(8,128)(2,1)} %get-tuple-element.29), channel_id=1, source_target_pairs={{1,4},{2,5},{3,6},{5,8},{6,9},{7,10},{9,12},{10,13},{11,14},{17,20... | collective-permute-start | bytes 589832 | tf_op jit(solution)/shard_map/ppermute | solution.py:53
  40.9 0.6 copy-start.18
  60.4 10.6 %collective-permute-start.4 = (bf16[1,1,64,1536]{3,2,1,0:T(8,128)(2,1)}, bf16[1,1,64,1536]{3,2,1,0:T(8,128)(2,1)S(1)}, u32[]{:S(2)}, u32[]{:S(2)}) collective-permute-start(bf16[1,1,64,1536]{3,2,1,0:T(8,128)(2,1)} %get-tuple-element.29), channel_id=1, source_target_pairs={{1,0},{2,1},{3,2},{5,4},{6,5},{7,6},{9,8},{10,9},{11,10},{13,12},{... | collective-permute-start | bytes 589832 | tf_op jit(solution)/shard_map/ppermute | solution.py:53
  61.7 9.6 %collective-permute-start.5 = (bf16[1,1,64,1536]{3,2,1,0:T(8,128)(2,1)}, bf16[1,1,64,1536]{3,2,1,0:T(8,128)(2,1)S(1)}, u32[]{:S(2)}, u32[]{:S(2)}) collective-permute-start(bf16[1,1,64,1536]{3,2,1,0:T(8,128)(2,1)} %get-tuple-element.28), channel_id=1, source_target_pairs={{4,1},{5,2},{6,3},{8,5},{9,6},{10,7},{12,9},{13,10},{14,11},{20,17... | collective-permute-start | bytes 589832 | tf_op jit(solution)/shard_map/ppermute | solution.py:53
  67.8 10.1 %collective-permute-start.7 = (bf16[1,1,64,1536]{3,2,1,0:T(8,128)(2,1)}, bf16[1,1,64,1536]{3,2,1,0:T(8,128)(2,1)S(1)}, u32[]{:S(2)}, u32[]{:S(2)}) collective-permute-start(bf16[1,1,64,1536]{3,2,1,0:T(8,128)(2,1)} %get-tuple-element.29), channel_id=1, source_target_pairs={{5,0},{6,1},{7,2},{9,4},{10,5},{11,6},{13,8},{14,9},{15,10},{21,16... | collective-permute-start | bytes 589832 | tf_op jit(solution)/shard_map/ppermute | solution.py:53
  70.9 8.7 %copy-start.3 = (f32[128,768]{1,0:T(8,128)S(1)}, f32[128,768]{1,0:T(8,128)}, u32[]{:S(2)}) copy-start(f32[128,768]{1,0:T(8,128)} %copy.52.mask_ref) | copy-start | bytes 1179652
  70.9 8.7 %copy-start.4 = (bf16[128,768]{1,0:T(8,128)(2,1)S(1)}, bf16[128,768]{1,0:T(8,128)(2,1)}, u32[]{:S(2)}) copy-start(bf16[128,768]{1,0:T(8,128)(2,1)} %slice.120.q_ref) | copy-start | bytes 589828
  71.0 8.7 %copy-start.6 = (f32[128,1]{1,0:T(8,128)S(1)}, f32[128,1]{1,0:T(8,128)}, u32[]{:S(2)}) copy-start(f32[128,1]{1,0:T(8,128)} %broadcast_in_dim_reshape.12.valid_ref) | copy-start | bytes 1540
  91.7 2.8 %copy-start.1 = (bf16[128,768]{1,0:T(8,128)(2,1)}, bf16[128,768]{1,0:T(8,128)(2,1)S(1)}, u32[]{:S(2)}) copy-start(bf16[128,768]{1,0:T(8,128)(2,1)S(1)} %get-tuple-element.10) | copy-start | bytes 589828
  91.7 2.8 %copy-start.5 = (bf16[128,768]{1,0:T(8,128)(2,1)}, bf16[128,768]{1,0:T(8,128)(2,1)S(1)}, u32[]{:S(2)}) copy-start(bf16[128,768]{1,0:T(8,128)(2,1)S(1)} %get-tuple-element.11) | copy-start | bytes 589828
  94.5 16.6 %copy-start.11 = (bf16[1,8,16,768]{3,2,1,0:T(8,128)(2,1)S(1)}, bf16[1,8,16,768]{3,2,1,0:T(8,128)(2,1)}, u32[]{:S(2)}) copy-start(bf16[1,8,16,768]{3,2,1,0:T(8,128)(2,1)} %param.9) | copy-start | bytes 589828
  94.5 16.6 %copy-start.14 = (f32[768]{0:T(1024)S(1)}, f32[768]{0:T(1024)}, u32[]{:S(2)}) copy-start(f32[768]{0:T(1024)} %add_reduce_fusion) | copy-start | bytes 9220
  94.5 16.6 %copy-start.17 = (f32[768]{0:T(1024)S(1)}, f32[768]{0:T(1024)}, u32[]{:S(2)}) copy-start(f32[768]{0:T(1024)} %reduce.4) | copy-start | bytes 9220
  96.5 17.2 %collective-permute-start.10 = (bf16[1,1,64,1536]{3,2,1,0:T(8,128)(2,1)}, bf16[1,1,64,1536]{3,2,1,0:T(8,128)(2,1)}, u32[]{:S(2)}, u32[]{:S(2)}) collective-permute-start(bf16[1,1,64,1536]{3,2,1,0:T(8,128)(2,1)} %get-tuple-element.17), channel_id=1, source_target_pairs={{1,0},{2,1},{3,2},{5,4},{6,5},{7,6},{9,8},{10,9},{11,10},{13,12},{... | collective-permute-start | bytes 589832 | tf_op jit(solution)/shard_map/ppermute | solution.py:53
  97.7 21.5 %collective-permute-start.11 = (bf16[1,1,64,1536]{3,2,1,0:T(8,128)(2,1)}, bf16[1,1,64,1536]{3,2,1,0:T(8,128)(2,1)}, u32[]{:S(2)}, u32[]{:S(2)}) collective-permute-start(bf16[1,1,64,1536]{3,2,1,0:T(8,128)(2,1)} %get-tuple-element.22), channel_id=1, source_target_pairs={{0,1},{1,2},{2,3},{4,5},{5,6},{6,7},{8,9},{9,10},{10,11},{12,13},{... | collective-permute-start | bytes 589832 | tf_op jit(solution)/shard_map/ppermute | solution.py:53
  103.0 17.6 %collective-permute-start.12 = (bf16[1,1,64,1536]{3,2,1,0:T(8,128)(2,1)}, bf16[1,1,64,1536]{3,2,1,0:T(8,128)(2,1)}, u32[]{:S(2)}, u32[]{:S(2)}) collective-permute-start(bf16[1,1,64,1536]{3,2,1,0:T(8,128)(2,1)} %get-tuple-element.21), channel_id=1, source_target_pairs={{5,0},{6,1},{7,2},{9,4},{10,5},{11,6},{13,8},{14,9},{15,10},{21,16... | collective-permute-start | bytes 589832 | tf_op jit(solution)/shard_map/ppermute | solution.py:53
  104.3 24.3 %collective-permute-start.8 = (bf16[1,2,64,1536]{3,2,1,0:T(8,128)(2,1)}, bf16[1,2,64,1536]{3,2,1,0:T(8,128)(2,1)}, u32[]{:S(2)}, u32[]{:S(2)}) collective-permute-start(bf16[1,2,64,1536]{3,2,1,0:T(8,128)(2,1)} %get-tuple-element.23), channel_id=1, source_target_pairs={{4,0},{5,1},{6,2},{7,3},{8,4},{9,5},{10,6},{11,7},{12,8},{13,9},{1... | collective-permute-start | bytes 1179656 | tf_op jit(solution)/shard_map/ppermute | solution.py:53
  107.6 20.9 %collective-permute-start.9 = (bf16[1,2,64,1536]{3,2,1,0:T(8,128)(2,1)}, bf16[1,2,64,1536]{3,2,1,0:T(8,128)(2,1)}, u32[]{:S(2)}, u32[]{:S(2)}) collective-permute-start(bf16[1,2,64,1536]{3,2,1,0:T(8,128)(2,1)} %get-tuple-element.24), channel_id=1, source_target_pairs={{0,4},{1,5},{2,6},{3,7},{4,8},{5,9},{6,10},{7,11},{8,12},{9,13},{1... | collective-permute-start | bytes 1179656 | tf_op jit(solution)/shard_map/ppermute | solution.py:53
  113.7 12.8 %collective-permute-start.13 = (bf16[1,1,64,1536]{3,2,1,0:T(8,128)(2,1)}, bf16[1,1,64,1536]{3,2,1,0:T(8,128)(2,1)S(1)}, u32[]{:S(2)}, u32[]{:S(2)}) collective-permute-start(bf16[1,1,64,1536]{3,2,1,0:T(8,128)(2,1)} %get-tuple-element.20), channel_id=1, source_target_pairs={{4,1},{5,2},{6,3},{8,5},{9,6},{10,7},{12,9},{13,10},{14,11},{20,17... | collective-permute-start | bytes 589832 | tf_op jit(solution)/shard_map/ppermute | solution.py:53
  119.3 9.2 %collective-permute-start.14 = (bf16[1,1,64,1536]{3,2,1,0:T(8,128)(2,1)}, bf16[1,1,64,1536]{3,2,1,0:T(8,128)(2,1)S(1)}, u32[]{:S(2)}, u32[]{:S(2)}) collective-permute-start(bf16[1,1,64,1536]{3,2,1,0:T(8,128)(2,1)} %get-tuple-element.19), channel_id=1, source_target_pairs={{1,4},{2,5},{3,6},{5,8},{6,9},{7,10},{9,12},{10,13},{11,14},{17,20... | collective-permute-start | bytes 589832 | tf_op jit(solution)/shard_map/ppermute | solution.py:53
  120.6 7.9 %collective-permute-start.15 = (bf16[1,1,64,1536]{3,2,1,0:T(8,128)(2,1)}, bf16[1,1,64,1536]{3,2,1,0:T(8,128)(2,1)S(1)}, u32[]{:S(2)}, u32[]{:S(2)}) collective-permute-start(bf16[1,1,64,1536]{3,2,1,0:T(8,128)(2,1)} %get-tuple-element.18), channel_id=1, source_target_pairs={{0,5},{1,6},{2,7},{4,9},{5,10},{6,11},{8,13},{9,14},{10,15},{16,21... | collective-permute-start | bytes 589832 | tf_op jit(solution)/shard_map/ppermute | solution.py:53
  134.2 2.1 copy-start.7
  145.6 0.7 copy-start.15
  145.6 0.7 copy-start.19
  145.6 0.7 copy-start.20
  146.3 2.8 %copy-start.2 = (bf16[128,768]{1,0:T(8,128)(2,1)S(1)}, bf16[128,768]{1,0:T(8,128)(2,1)}, u32[]{:S(2)}) copy-start(bf16[128,768]{1,0:T(8,128)(2,1)} %copy-done.1) | copy-start | bytes 589828
  146.3 2.9 %copy-start.8 = (bf16[768,768]{1,0:T(8,128)(2,1)S(1)}, bf16[768,768]{1,0:T(8,128)(2,1)}, u32[]{:S(2)}) copy-start(bf16[768,768]{1,0:T(8,128)(2,1)} %param.14) | copy-start | bytes 3538948
  146.3 2.9 %copy-start.9 = (f32[1,8,2,8,768]{4,3,1,2,0:T(8,128)S(1)}, f32[1,8,2,8,768]{4,3,1,2,0:T(8,128)}, u32[]{:S(2)}) copy-start(f32[1,8,2,8,768]{4,3,1,2,0:T(8,128)} %copy.50) | copy-start | bytes 1179652
  146.3 2.9 %copy-start.10 = (f32[1,8,2,8,768]{4,3,1,2,0:T(8,128)S(1)}, f32[1,8,2,8,768]{4,3,1,2,0:T(8,128)}, u32[]{:S(2)}) copy-start(f32[1,8,2,8,768]{4,3,1,2,0:T(8,128)} %copy.51) | copy-start | bytes 1179652
  146.3 2.9 %copy-start.16 = (f32[768]{0:T(1024)S(1)}, f32[768]{0:T(1024)}, u32[]{:S(2)}) copy-start(f32[768]{0:T(1024)} %reduce.2) | copy-start | bytes 9220
  151.0 4.0 %collective-permute-start.20 = (f32[3,768]{1,0:T(4,128)}, f32[3,768]{1,0:T(4,128)}, u32[]{:S(2)}, u32[]{:S(2)}) collective-permute-start(f32[3,768]{1,0:T(4,128)} %pad_maximum_fusion.2), channel_id=1, source_target_pairs={{0,4},{4,0},{8,12},{12,8},{1,5},{5,1},{9,13},{13,9},{2,6},{6,2},{1... | collective-permute-start | bytes 27656 | tf_op jit(solution)/shard_map/ppermute | solution.py:121
  156.3 64.7 %collective-permute-start.21 = (f32[3,768]{1,0:T(4,128)}, f32[3,768]{1,0:T(4,128)}, u32[]{:S(2)}, u32[]{:S(2)}) collective-permute-start(f32[3,768]{1,0:T(4,128)} %fusion.25), channel_id=1, source_target_pairs={{0,8},{4,12},{8,0},{12,4},{1,9},{5,13},{9,1},{13,5},{2,10},{6,14},... | collective-permute-start | bytes 27656 | tf_op jit(solution)/shard_map/ppermute | solution.py:121
  219.8 12.7 %collective-permute-start.16 = (bf16[2,2,2,48,192]{4,2,1,0,3:T(2,128)(2,1)}, bf16[2,2,2,48,192]{4,2,1,0,3:T(2,128)(2,1)}, u32[]{:S(2)}, u32[]{:S(2)}) collective-permute-start(bf16[2,2,2,48,192]{4,2,1,0,3:T(2,128)(2,1)} %fusion.21), channel_id=1, source_target_pairs={{0,4},{4,0},{8,12},{12,8},{1,5},{5,1},{9,13},{13,9},{2,6},{6,2},{1... | collective-permute-start | bytes 442376 | tf_op jit(solution)/shard_map/ppermute | solution.py:121
  221.8 3.8 %collective-permute-start.22 = (f32[3,768]{1,0:T(4,128)S(1)}, f32[3,768]{1,0:T(4,128)S(1)}, u32[]{:S(2)}, u32[]{:S(2)}) collective-permute-start(f32[3,768]{1,0:T(4,128)S(1)} %fusion.41), channel_id=1, source_target_pairs={{0,1},{1,0},{2,3},{3,2},{4,5},{5,4},{6,7},{7,6},{8,9},{9,8},{10,11... | collective-permute-start | bytes 27656 | tf_op jit(solution)/shard_map/ppermute | solution.py:121
  225.6 6.3 %collective-permute-start.23 = (f32[3,768]{1,0:T(4,128)S(1)}, f32[3,768]{1,0:T(4,128)}, u32[]{:S(2)}, u32[]{:S(2)}) collective-permute-start(f32[3,768]{1,0:T(4,128)S(1)} %add.158), channel_id=1, source_target_pairs={{0,2},{1,3},{2,0},{3,1},{4,6},{5,7},{6,4},{7,5},{8,10},{9,11},{10,... | collective-permute-start | bytes 27656 | tf_op jit(solution)/shard_map/ppermute | solution.py:121
  234.1 6.2 %collective-permute-start.17 = (bf16[2,2,48,192]{3,1,0,2:T(2,128)(2,1)S(1)}, bf16[2,2,48,192]{3,1,0,2:T(2,128)(2,1)S(1)}, u32[]{:S(2)}, u32[]{:S(2)}) collective-permute-start(bf16[2,2,48,192]{3,1,0,2:T(2,128)(2,1)S(1)} %fusion.23), channel_id=1, source_target_pairs={{0,8},{4,12},{8,0},{12,4},{1,9},{5,13},{9,1},{13,5},{2,10},{6,14},... | collective-permute-start | bytes 221192 | tf_op jit(solution)/shard_map/ppermute | solution.py:121
  240.7 4.2 %collective-permute-start.18 = (bf16[2,48,192]{2,0,1:T(2,128)(2,1)S(1)}, bf16[2,48,192]{2,0,1:T(2,128)(2,1)S(1)}, u32[]{:S(2)}, u32[]{:S(2)}) collective-permute-start(bf16[2,48,192]{2,0,1:T(2,128)(2,1)S(1)} %copy.69), channel_id=1, source_target_pairs={{0,1},{1,0},{2,3},{3,2},{4,5},{5,4},{6,7},{7,6},{8,9},{9,8},{10,11... | collective-permute-start | bytes 110600 | tf_op jit(solution)/shard_map/ppermute | solution.py:121
  245.1 5.4 %collective-permute-start.19 = (bf16[48,192]{1,0:T(8,128)(2,1)S(1)}, bf16[48,192]{1,0:T(8,128)(2,1)S(1)}, u32[]{:S(2)}, u32[]{:S(2)}) collective-permute-start(bf16[48,192]{1,0:T(8,128)(2,1)S(1)} %bitcast.163), channel_id=1, source_target_pairs={{0,2},{1,3},{2,0},{3,1},{4,6},{5,7},{6,4},{7,5},{8,10},{9,11},{10,... | collective-permute-start | bytes 55304 | tf_op jit(solution)/shard_map/ppermute | solution.py:121
  250.5 0.7 copy-start.13
Sparse Core Ops, SparseCore 0:
  145.8 69.4 reduce-scatter.1
